TPU v7x, 256 devices: a whole 4x4x8 slice. The times are simulated.
256 devices in a mesh: dp: 32 (over z, y), section: 4 (over x_lo, core), mp: 2 (over x_hi).
Axes of the slice: x: 4 (x_hi: 2, x_lo: 2; x = x_hi * 2 + x_lo), y: 4, z: 8, core: 2. Of those that a mesh axis runs over, the one named last changes fastest.
Arguments:
- arriving: bfloat16 [4, 4608, 8192], P('section', 'dp', 'mp'), may hold values from -6 to 6
- keep_mask: int32 [4608], P('dp'), may hold values 0 or 1
- mask_vector: bfloat16 [8192], P('mp'), may hold values from -5 to 5
- stashed: bfloat16 [4, 4608, 8192], P('section', 'dp', 'mp'), may hold values from -6 to 6
- cotangent: bfloat16 [4, 4608, 8192], P('section', 'dp', 'mp'), may hold values from -6 to 6
- gain: bfloat16 [4, 8192], P('section', 'mp'), may hold values from 0.3984375 to 1.59375
- down_adapter: bfloat16 [4, 8192, 256], P('section', None, 'mp'), may hold values from -0.0625 to 0.0625
- up_adapter: bfloat16 [4, 256, 8192], P('section', 'mp'), may hold values from -0.375 to 0.375
Outputs:
- next_input: bfloat16 [4, 4608, 8192], P('section', 'dp', 'mp')
- prev_grad: bfloat16 [4, 4608, 8192], P('section', 'dp', 'mp')
- down_grad: float32 [4, 8192, 256], P('section', 'dp', 'mp')
- up_grad: float32 [4, 256, 8192], P('section', 'mp', 'dp')
All inputs are finite; a program needn't handle non-finite values. No bound on the sum of `keep_mask` on one device may be relied on, other than what follows from the above.
Results may differ from a plain program's by a relative error of at most 0.0015.
The roundings to bfloat16 on the way count: a program that leaves them out, or rounds other values in their place, can miss the bound.
Values may be sent and summed in bfloat16 or wider, within the bound.
No kernel may reach another device: no remote copies, remote signals or barrier semaphores. Data moves between devices by JAX's collectives and lax.ppermute only.
A program may use at most 128 MiB of HBM per device.

v0:
```python
import jax
import jax.numpy as jnp
from jax import lax
from jax.sharding import PartitionSpec as P


def shifted(shard, axis, by):
    peers = lax.axis_size(axis)
    pairs = [(i, i + by) for i in range(peers) if 0 <= i + by < peers]
    return lax.ppermute(shard, axis, pairs)


def row_scale(rows):
    values = rows.astype(jnp.float32)
    return lax.rsqrt(jnp.mean(values * values, axis=1, keepdims=True) + 1e-05)


def contract_rows(left, right):
    return lax.dot_general(
        left, right, (((0,), (0,)), ((), ())), preferred_element_type=jnp.float32
    )


def contract_cols(left, right):
    return lax.dot_general(
        left, right, (((1,), (1,)), ((), ())), preferred_element_type=jnp.float32
    )


def on_device(arriving, keep_mask, mask_vector, stashed, cotangent, gain, down_adapter, up_adapter):
    is_first = lax.axis_index("section") == 0
    kept_rows = jnp.logical_or(keep_mask == 1, jnp.logical_not(is_first))
    inputs = jnp.where(kept_rows[:, None], arriving[0], mask_vector[None, :])
    saved = stashed[0]
    upstream = cotangent[0]
    gain_part = gain[0]
    down_local = down_adapter[0]
    up_local = up_adapter[0]
    replicas = lax.axis_size("dp")
    inputs_full, saved_full, upstream_full, gain_full = (
        lax.all_gather(inputs, "mp", axis=1, tiled=True),
        lax.all_gather(saved, "mp", axis=1, tiled=True),
        lax.all_gather(upstream, "mp", axis=1, tiled=True),
        lax.all_gather(gain_part, "mp", axis=0, tiled=True),
    )
    gain_row = gain_full.astype(jnp.float32)[None, :]
    full_width = inputs_full.shape[1]
    normed = (inputs_full.astype(jnp.float32) * row_scale(inputs_full) * gain_row).astype(
        jnp.bfloat16
    )
    hidden_pre = jnp.dot(normed, down_local, preferred_element_type=jnp.float32)
    hidden = jax.nn.silu(hidden_pre).astype(jnp.bfloat16)
    branch_part = jnp.dot(hidden, up_local, preferred_element_type=jnp.float32)
    saved_scale = row_scale(saved_full)
    saved_normed = (saved_full.astype(jnp.float32) * saved_scale * gain_row).astype(jnp.bfloat16)
    saved_pre = jnp.dot(saved_normed, down_local, preferred_element_type=jnp.float32)
    sigmoid_pre = jax.nn.sigmoid(saved_pre)
    saved_hidden = (saved_pre * sigmoid_pre).astype(jnp.bfloat16)
    hidden_grad = contract_cols(upstream_full, up_local)
    pre_grad = (hidden_grad * sigmoid_pre * (1.0 + saved_pre * (1.0 - sigmoid_pre))).astype(
        jnp.bfloat16
    )
    normed_part = contract_cols(pre_grad, down_local)
    down_part = contract_rows(saved_normed, pre_grad)
    up_part = contract_rows(saved_hidden, upstream_full)
    down_sum, up_sum = (
        lax.psum_scatter(down_part, "dp", scatter_dimension=0, tiled=True),
        lax.psum_scatter(up_part, "dp", scatter_dimension=1, tiled=True),
    )
    branch, normed_grad = (
        lax.psum_scatter(branch_part, "mp", scatter_dimension=1, tiled=True),
        lax.psum_scatter(normed_part, "mp", scatter_dimension=1, tiled=True),
    )
    output = (inputs.astype(jnp.float32) + branch).astype(jnp.bfloat16)
    saved_values = saved.astype(jnp.float32)
    scaled_grad = normed_grad * gain_part.astype(jnp.float32)[None, :]
    row_dot = lax.psum(jnp.sum(saved_values * scaled_grad, axis=1), "mp")
    cubed = saved_scale * saved_scale * saved_scale
    input_grad = (
        upstream.astype(jnp.float32)
        + saved_scale * scaled_grad
        - saved_values * cubed * (row_dot[:, None] / full_width)
    ).astype(jnp.bfloat16)
    next_input = shifted(output, "section", 1)
    prev_grad = shifted(input_grad, "section", -1)
    down_grad = down_sum / replicas
    up_grad = up_sum / replicas
    return (next_input[None], prev_grad[None], down_grad[None], up_grad[None])


def solution(mesh):
    placed = (
        P("section", "dp", "mp"),
        P("dp"),
        P("mp"),
        P("section", "dp", "mp"),
        P("section", "dp", "mp"),
        P("section", "mp"),
        P("section", None, "mp"),
        P("section", "mp", None),
    )
    return jax.shard_map(
        on_device,
        mesh=mesh,
        in_specs=placed,
        out_specs=(
            P("section", "dp", "mp"),
            P("section", "dp", "mp"),
            P("section", "dp", "mp"),
            P("section", "mp", "dp"),
        ),
        check_vma=False,
    )
```

profile of v0, /device:TPU:38, one launch (start us, length us, event | category | flops | bytes accessed | tf_op | source)
XLA Modules:
  0.0 749.9 jit_solution(12541325084801085045)
XLA Ops:
  7.2 0.0 copy-start
  7.2 0.0 all-gather.7.cloned.1.call-start
  7.2 0.8 compare_or_fusion
  8.1 2.4 bitcast_select_fusion
  10.5 0.0 copy-start.3
  10.5 0.0 all-gather.7.cloned.1.call-update
  10.5 0.0 all-gather.9.cloned.1.call-start
  10.6 0.7 all-gather.9.cloned.1.call-update
  11.3 0.0 all-gather.11.cloned.1.call-start
  11.3 0.7 all-gather.11.cloned.1.call-update
  12.0 0.0 reduce-scatter.5.cloned.1.call-start
  12.1 0.0 copy-done.3
  12.1 5.9 all-gather
  18.0 36.3 %all-gather.7.cloned.1.call-done = bf16[144,8192]{1,0:T(8,128)(2,1)} async-done(((bf16[144,4096]{1,0:T(8,128)(2,1)}), bf16[144,8192]{1,0:T(8,128)(2,1)}) %all-gather.7.cloned.1.call-update) | async-done | bytes 2359312 | tf_op jit(solution)/shard_map/all_gather | solution.py:41
  54.3 2.2 fusion
  56.5 0.0 copy-done
  56.6 6.1 fusion.19
  62.6 0.0 reduce-scatter.5.cloned.1.call-update
  62.6 0.0 reduce-scatter.7.cloned.1.call-start
  62.7 35.5 %all-gather.9.cloned.1.call-done = bf16[1,144,8192]{2,1,0:T(8,128)(2,1)} async-done(((bf16[1,144,4096]{2,1,0:T(8,128)(2,1)}), bf16[1,144,8192]{2,1,0:T(8,128)(2,1)}) %all-gather.9.cloned.1.call-update) | async-done | bytes 2359312 | tf_op jit(solution)/shard_map/all_gather | solution.py:42
  98.2 0.0 copy-start.1
  98.2 2.4 fusion.3
  100.6 0.0 copy-done.1
  100.6 1.0 fusion.23
  101.6 40.6 %all-gather.11.cloned.1.call-done = bf16[1,144,8192]{2,1,0:T(8,128)(2,1)} async-done(((bf16[1,144,4096]{2,1,0:T(8,128)(2,1)}), bf16[1,144,8192]{2,1,0:T(8,128)(2,1)}) %all-gather.11.cloned.1.call-update) | async-done | bytes 2359312 | tf_op jit(solution)/shard_map/all_gather | solution.py:43
  142.2 3.1 fusion.36
  145.3 2.9 fusion.21
  148.2 0.0 reduce-scatter.7.cloned.1.call-update
  148.2 0.0 reduce-scatter.11.cloned.1.call-start
  148.3 4.5 fusion.12
  152.8 0.0 reduce-scatter.11.cloned.1.call-update
  152.8 0.0 reduce-scatter.9.cloned.1.call-start
  152.8 5.3 fusion.41
  158.1 0.0 copy-start.4
  158.1 0.0 reduce-scatter.9.cloned.1.call-update
  158.2 0.0 copy-start.2
  158.2 52.5 %reduce-scatter.5.cloned.1.call-done = f32[144,4096]{1,0:T(8,128)} async-done(((f32[144,8192]{1,0:T(8,128)}), f32[144,4096]{1,0:T(8,128)}) %reduce-scatter.5.cloned.1.call-update) | async-done | bytes 2359312 | tf_op jit(solution)/shard_map/reduce_scatter | solution.py:71
  210.7 0.0 copy-done.4
  210.7 3.4 add_convert_fusion
  214.1 1.9 collective-permute-start
  216.0 63.2 %reduce-scatter.7.cloned.1.call-done = f32[144,4096]{1,0:T(8,128)} async-done(((f32[144,8192]{1,0:T(8,128)}), f32[144,4096]{1,0:T(8,128)}) %reduce-scatter.7.cloned.1.call-update) | async-done | bytes 2359312 | tf_op jit(solution)/shard_map/reduce_scatter | solution.py:72
  279.3 0.0 copy-done.2
  279.3 2.1 fusion.9
  281.3 6.4 psum.7
  287.8 4.0 fusion.8
  291.8 6.4 collective-permute-start.1
  298.2 214.1 %reduce-scatter.11.cloned.1.call-done = f32[128,256]{1,0:T(8,128)} async-done(((f32[128,8192]{1,0:T(8,128)}), f32[128,256]{1,0:T(8,128)}) %reduce-scatter.11.cloned.1.call-update) | async-done | bytes 131088 | tf_op jit(solution)/shard_map/reduce_scatter | solution.py:68
  512.3 1.6 multiply_bitcast_fusion
  513.9 224.2 %reduce-scatter.9.cloned.1.call-done = f32[256,128]{1,0:T(8,128)} async-done(((f32[8192,128]{1,0:T(8,128)}), f32[256,128]{1,0:T(8,128)}) %reduce-scatter.9.cloned.1.call-update) | async-done | bytes 131088 | tf_op jit(solution)/shard_map/reduce_scatter | solution.py:67
  738.1 1.6 multiply_bitcast_fusion.1
  739.6 0.0 collective-permute-done
  739.6 0.0 collective-permute-done.1
  739.6 2.4 copy.14
  742.0 1.0 copy.15
  (5 shorter events, 0.1 us)
Async XLA Ops:
  7.2 49.4 %copy-start = (bf16[1,8192,128]{2,1,0:T(8,128)(2,1)S(1)}, bf16[1,8192,128]{2,1,0:T(8,128)(2,1)}, u32[]{:S(2)}) copy-start(bf16[1,8192,128]{2,1,0:T(8,128)(2,1)} %param.14) | copy-start | bytes 6291460
  7.2 47.1 %all-gather.7.cloned.1.call-start = ((), (), s32[]{:S(2)}) async-start(), calls=%async_computation.4 | async-start | bytes 3538944 | tf_op jit(solution)/shard_map/all_gather | solution.py:41
  10.5 1.6 copy-start.3
  10.5 87.7 %all-gather.9.cloned.1.call-start = ((), (), s32[]{:S(2)}) async-start(), calls=%async_computation.9 | async-start | bytes 3538944 | tf_op jit(solution)/shard_map/all_gather | solution.py:42
  11.3 130.9 %all-gather.11.cloned.1.call-start = ((), (), s32[]{:S(2)}) async-start(), calls=%async_computation.10 | async-start | bytes 3538944 | tf_op jit(solution)/shard_map/all_gather | solution.py:43
  12.0 198.7 %reduce-scatter.5.cloned.1.call-start = ((), (), s32[]{:S(2)}) async-start(), calls=%async_computation.5 | async-start | bytes 7077888 | tf_op jit(solution)/shard_map/reduce_scatter | solution.py:71
  62.6 216.6 %reduce-scatter.7.cloned.1.call-start = ((), (), s32[]{:S(2)}) async-start(), calls=%async_computation.6 | async-start | bytes 7077888 | tf_op jit(solution)/shard_map/reduce_scatter | solution.py:72
  98.2 2.4 copy-start.1
  148.2 364.1 %reduce-scatter.11.cloned.1.call-start = ((), (), s32[]{:S(2)}) async-start(), calls=%async_computation.8 | async-start | bytes 4325376 | tf_op jit(solution)/shard_map/reduce_scatter | solution.py:68
  152.8 585.3 %reduce-scatter.9.cloned.1.call-start = ((), (), s32[]{:S(2)}) async-start(), calls=%async_computation.7 | async-start | bytes 4325376 | tf_op jit(solution)/shard_map/reduce_scatter | solution.py:67
  158.1 52.6 %copy-start.4 = (bf16[4096]{0:T(1024)(128)(2,1)S(1)}, bf16[4096]{0:T(1024)(128)(2,1)}, u32[]{:S(2)}) copy-start(bf16[4096]{0:T(1024)(128)(2,1)} %param.10) | copy-start | bytes 24580
  158.2 121.1 %copy-start.2 = (bf16[1,144,4096]{2,1,0:T(8,128)(2,1)S(1)}, bf16[1,144,4096]{2,1,0:T(8,128)(2,1)}, u32[]{:S(2)}) copy-start(bf16[1,144,4096]{2,1,0:T(8,128)(2,1)} %param.11) | copy-start | bytes 3538948
  214.1 525.5 %collective-permute-start = (bf16[144,4096]{1,0:T(8,128)(2,1)}, bf16[144,4096]{1,0:T(8,128)(2,1)}, u32[]{:S(2)}, u32[]{:S(2)}) collective-permute-start(bf16[144,4096]{1,0:T(8,128)(2,1)} %add_convert_fusion), channel_id=1, source_target_pairs={{0,2},{2,4},{4,6},{1,3},{3,5},{5,7},{8,10},{10,12},{12,14},{9,11},... | collective-permute-start | bytes 3538952 | tf_op jit(solution)/shard_map/ppermute | solution.py:10
  291.8 447.9 %collective-permute-start.1 = (bf16[144,4096]{1,0:T(8,128)(2,1)}, bf16[144,4096]{1,0:T(8,128)(2,1)S(1)}, u32[]{:S(2)}, u32[]{:S(2)}) collective-permute-start(bf16[144,4096]{1,0:T(8,128)(2,1)} %fusion.8), channel_id=1, source_target_pairs={{2,0},{4,2},{6,4},{3,1},{5,3},{7,5},{10,8},{12,10},{14,12},{11,9},... | collective-permute-start | bytes 3538952 | tf_op jit(solution)/shard_map/ppermute | solution.py:10
Sparse Core Ops, SparseCore 0:
  10.6 43.6 all-gather.6
  56.1 42.0 all-gather.8
  100.0 42.0 all-gather.10
  144.6 66.1 reduce-scatter.4
  213.1 66.1 reduce-scatter.6
  283.0 229.2 reduce-scatter.10
  516.2 221.8 reduce-scatter.8
where the time goes:
time: 752 us; the launch traced here: 750 us
  waiting for transfers between devices  668 us (89%)
  matrix products  22.8 us (3%)
  other arithmetic  20.5 us (3%)
  between operations  14.2 us (2%)
  blocking collectives  12.3 us (2%)
  starting transfers between devices  8.6 us (1%)
    reduce_scatter x1, waiting for transfers between devices, on_device(): lax.psum_scatter(down_part, 'dp', scatter_dimension=0, tiled=True)  224 us
    reduce_scatter x1, waiting for transfers between devices, on_device(): lax.psum_scatter(up_part, 'dp', scatter_dimension=1, tiled=True)  214 us
    reduce_scatter x1, waiting for transfers between devices, on_device(): lax.psum_scatter(normed_part, 'mp', scatter_dimension=1, tiled=True)  63.2 us
    reduce_scatter x1, waiting for transfers between devices, on_device(): lax.psum_scatter(branch_part, 'mp', scatter_dimension=1, tiled=True)  52.5 us
    all_gather x1, waiting for transfers between devices, on_device(): lax.all_gather(upstream, 'mp', axis=1, tiled=True)  40.6 us
    all_gather x1, waiting for transfers between devices, on_device(): lax.all_gather(inputs, 'mp', axis=1, tiled=True)  36.3 us
    all_gather x1, waiting for transfers between devices, on_device(): lax.all_gather(saved, 'mp', axis=1, tiled=True)  35.5 us
  transfers between devices with their start and end apart: 9, of which 7 were waited for; matrix products, arithmetic and copies ran while one was open for 5% of the time, Pallas kernels for 0%

commit v1 on v0

v1 whole, which is shorter than its diff:
```python
import jax
import jax.numpy as jnp
from jax import lax
from jax.sharding import PartitionSpec as P


def shifted(shard, axis, by):
    peers = lax.axis_size(axis)
    pairs = [(i, i + by) for i in range(peers) if 0 <= i + by < peers]
    return lax.ppermute(shard, axis, pairs)


def swapped(shard, axis):
    return lax.ppermute(shard, axis, [(0, 1), (1, 0)])


def contract_rows(left, right):
    return lax.dot_general(
        left, right, (((0,), (0,)), ((), ())), preferred_element_type=jnp.float32
    )


def contract_cols(left, right):
    return lax.dot_general(
        left, right, (((1,), (1,)), ((), ())), preferred_element_type=jnp.float32
    )


def in_unit_order(own, received, first, axis):
    return jnp.where(
        first,
        jnp.concatenate([own, received], axis=axis),
        jnp.concatenate([received, own], axis=axis),
    )


def on_device(arriving, keep_mask, mask_vector, stashed, cotangent, gain, down_adapter, up_adapter):
    half = lax.axis_index("mp")
    first = half == 0
    is_first = lax.axis_index("section") == 0
    kept_rows = jnp.logical_or(keep_mask == 1, jnp.logical_not(is_first))
    inputs = jnp.where(kept_rows[:, None], arriving[0], mask_vector[None, :])
    saved = stashed[0]
    upstream = cotangent[0]
    gain_row = gain[0].astype(jnp.float32)[None, :]
    down_local = down_adapter[0]
    up_local = up_adapter[0]
    width = inputs.shape[1]
    full_width = width * lax.axis_size("mp")
    replicas = lax.axis_size("dp")

    down_mine = lax.dynamic_slice_in_dim(down_local, half * width, width, axis=0)
    down_theirs = lax.dynamic_slice_in_dim(down_local, (1 - half) * width, width, axis=0)
    up_mine = lax.dynamic_slice_in_dim(up_local, half * width, width, axis=1)
    up_theirs = lax.dynamic_slice_in_dim(up_local, (1 - half) * width, width, axis=1)
    down_half = in_unit_order(down_mine, swapped(down_theirs, "mp"), first, 1)
    up_half = in_unit_order(up_mine, swapped(up_theirs, "mp"), first, 0)

    input_values = inputs.astype(jnp.float32)
    saved_values = saved.astype(jnp.float32)
    squares = lax.psum(
        jnp.stack(
            [jnp.sum(input_values * input_values, axis=1), jnp.sum(saved_values * saved_values, axis=1)]
        ),
        "mp",
    )
    scale = lax.rsqrt(squares[0] / full_width + 1e-05)[:, None]
    saved_scale = lax.rsqrt(squares[1] / full_width + 1e-05)[:, None]
    normed = (input_values * scale * gain_row).astype(jnp.bfloat16)
    saved_normed = (saved_values * saved_scale * gain_row).astype(jnp.bfloat16)

    partials = lax.psum(
        jnp.stack(
            [
                jnp.dot(normed, down_half, preferred_element_type=jnp.float32),
                jnp.dot(saved_normed, down_half, preferred_element_type=jnp.float32),
                contract_cols(upstream, up_half),
            ]
        ),
        "mp",
    )
    hidden_pre, saved_pre, hidden_grad = partials[0], partials[1], partials[2]
    hidden = jax.nn.silu(hidden_pre).astype(jnp.bfloat16)
    branch = jnp.dot(hidden, up_half, preferred_element_type=jnp.float32)
    output = (input_values + branch).astype(jnp.bfloat16)

    sigmoid_pre = jax.nn.sigmoid(saved_pre)
    saved_hidden = (saved_pre * sigmoid_pre).astype(jnp.bfloat16)
    pre_grad = (hidden_grad * sigmoid_pre * (1.0 + saved_pre * (1.0 - sigmoid_pre))).astype(
        jnp.bfloat16
    )
    scaled_grad = contract_cols(pre_grad, down_half) * gain_row
    row_dot = lax.psum(jnp.sum(saved_values * scaled_grad, axis=1), "mp")
    cubed = saved_scale * saved_scale * saved_scale
    input_grad = (
        upstream.astype(jnp.float32)
        + saved_scale * scaled_grad
        - saved_values * cubed * (row_dot[:, None] / full_width)
    ).astype(jnp.bfloat16)
    next_input = shifted(output, "section", 1)
    prev_grad = shifted(input_grad, "section", -1)

    blocks = replicas // 2
    units = down_local.shape[1]
    down_part = contract_rows(saved_normed, pre_grad)
    up_part = contract_rows(saved_hidden, upstream)
    down_slots = (
        down_part.reshape(blocks, full_width // replicas, 2, units)
        .transpose(2, 0, 1, 3)
        .reshape(replicas, -1)
    )
    up_slots = (
        up_part.reshape(2, units, blocks, full_width // replicas)
        .transpose(0, 2, 1, 3)
        .reshape(replicas, -1)
    )
    lanes = 128
    slots = jnp.concatenate([down_slots, up_slots], axis=1).reshape(replicas, -1, lanes)
    summed = lax.all_to_all(slots, "dp", 0, 0, tiled=True).sum(axis=0).reshape(-1)
    slot = lax.axis_index("dp")
    keeps = (slot // blocks) == half
    pairs = []
    for j in range(replicas):
        for m in range(2):
            if j // blocks != m:
                pairs.append((j * 2 + m, (j ^ blocks) * 2 + (1 - m)))
    moved = lax.ppermute(summed, ("dp", "mp"), pairs)
    mine = jnp.where(keeps, summed, moved) * (1.0 / replicas)
    down_grad = mine[: down_slots.shape[1]].reshape(full_width // replicas, units)
    up_grad = mine[down_slots.shape[1] :].reshape(units, full_width // replicas)
    return (next_input[None], prev_grad[None], down_grad[None], up_grad[None])


def solution(mesh):
    placed = (
        P("section", "dp", "mp"),
        P("dp"),
        P("mp"),
        P("section", "dp", "mp"),
        P("section", "dp", "mp"),
        P("section", "mp"),
        P("section", None, "mp"),
        P("section", "mp", None),
    )
    return jax.shard_map(
        on_device,
        mesh=mesh,
        in_specs=placed,
        out_specs=(
            P("section", "dp", "mp"),
            P("section", "dp", "mp"),
            P("section", "dp", "mp"),
            P("section", "mp", "dp"),
        ),
        check_vma=False,
    )
```

time: 752 us -> 369 us (0.49)
  waiting for transfers between devices: 668 us -> 214 us
  blocking collectives: 12.3 us -> 49.8 us
  starting transfers between devices: 8.6 us -> 32.7 us
  local copies, waits for them, and re-layouts: 3.43 us -> 16.6 us
    reduce_scatter x4 -> x0, waiting for transfers between devices: 554 us -> none  [the longest x1 224 us: on_device(): lax.psum_scatter(down_part, 'dp', scatter_dimension=0, tiled=True)]
    all_to_all x0 -> x1, waiting for transfers between devices: none -> 162 us  [on_device(): lax.all_to_all(slots, 'dp', 0, 0, tiled=True).sum(axis=0).reshape(-1)]
    all_gather x3 -> x0, waiting for transfers between devices: 112 us -> none  [the longest x1 40.6 us: on_device(): lax.all_gather(upstream, 'mp', axis=1, tiled=True)]
    psum x0 -> x1, blocking collectives: none -> 43.4 us  [on_device(): lax.psum(jnp.stack([jnp.sum(input_values * input_values, axis=1), jnp.sum...]
    psum x0 -> x1, waiting for transfers between devices: none -> 40.9 us  [on_device(): lax.psum(jnp.stack([jnp.dot(normed, down_half, preferred_element_type=jnp...]
    ppermute x0 -> x3, starting transfers between devices: none -> 18 us  [the longest x1 14.4 us: on_device(): moved = lax.ppermute(summed, ('dp', 'mp'), pairs)]
    ppermute x0 -> x3, waiting for transfers between devices: none -> 10.6 us  [the longest x1 10.6 us: on_device(): moved = lax.ppermute(summed, ('dp', 'mp'), pairs)]
    all_to_all x0 -> x1, starting transfers between devices: none -> 10.3 us  [on_device(): lax.all_to_all(slots, 'dp', 0, 0, tiled=True).sum(axis=0).reshape(-1)]
  transfers between devices with their start and end apart: 9 -> 7, of which waited for: 7 -> 3; matrix products, arithmetic and copies ran while one was open for 5% -> 7% of each run, Pallas kernels for 0% -> 0%
where the time goes in v1:
time: 369 us; the launch traced here: 367 us
  waiting for transfers between devices  214 us (58%)
  blocking collectives  49.8 us (13%)
  starting transfers between devices  32.7 us (9%)
  other arithmetic  20.1 us (5%)
  matrix products  19.2 us (5%)
  local copies, waits for them, and re-layouts  16.6 us (4%)
  between operations  14.4 us (4%)
    all_to_all x1, waiting for transfers between devices, on_device(): lax.all_to_all(slots, 'dp', 0, 0, tiled=True).sum(axis=0).reshape(-1)  162 us
    psum x1, blocking collectives, on_device(): lax.psum(jnp.stack([jnp.sum(input_values * input_values, axis=1), jnp.sum...  43.4 us
    psum x1, waiting for transfers between devices, on_device(): lax.psum(jnp.stack([jnp.dot(normed, down_half, preferred_element_type=jnp...  40.9 us
    ppermute x1, starting transfers between devices, on_device(): moved = lax.ppermute(summed, ('dp', 'mp'), pairs)  14.4 us
    ppermute x1, waiting for transfers between devices, on_device(): moved = lax.ppermute(summed, ('dp', 'mp'), pairs)  10.6 us
    all_to_all x1, starting transfers between devices, on_device(): lax.all_to_all(slots, 'dp', 0, 0, tiled=True).sum(axis=0).reshape(-1)  10.3 us
    concatenate x1, other arithmetic, on_device(): jnp.concatenate([down_slots, up_slots], axis=1).reshape(replicas, -1, lanes)  7.61 us
  transfers between devices with their start and end apart: 7, of which 3 were waited for; matrix products, arithmetic and copies ran while one was open for 7% of the time, Pallas kernels for 0%

profile of v1, /device:TPU:38, one launch (start us, length us, event | category | flops | bytes accessed | tf_op | source)
XLA Modules:
  0.0 366.8 jit_solution(2724530384450733557)
XLA Ops:
  7.2 0.0 all-reduce.2.cloned.1.call-start
  7.2 0.0 copy-start.3
  7.2 3.2 dynamic-slice_bitcast_fusion.3
  10.4 1.5 collective-permute-start
  11.9 0.0 copy-done.3
  11.9 1.5 dynamic-slice_bitcast_fusion.1
  13.4 2.1 collective-permute-start.1
  15.5 0.0 copy-done
  15.5 0.3 fusion.4
  15.8 0.0 copy-done.22
  15.8 0.0 copy-done.4
  15.8 0.0 copy-done.16
  15.9 0.5 fusion.1
  16.3 43.4 %psum.21 = f32[2,144]{1,0:T(2,128)S(1)} all-reduce(f32[2,144]{1,0:T(2,128)S(1)} %pad_maximum_fusion.2), channel_id=1, replica_groups=mesh['dp'=32,'section'=4,'mp'=2] {'mp'}, use_global_device_ids=true, to_apply=%region_2.3 | all-reduce | flops 288 | bytes 2304 | tf_op jit(solution)/shard_map/psum | solution.py:61
  59.7 0.6 fusion.35
  60.3 0.0 copy-done.19
  60.4 0.5 copy-done.13
  60.9 0.4 fusion.6
  61.2 0.0 collective-permute-done
  61.3 0.0 copy-start.17
  61.3 0.0 copy-start.20
  61.3 0.0 copy-start.23
  61.3 2.9 convolution_bitcast_fusion.2
  64.3 0.0 copy-start.1
  64.3 0.0 copy-start.6
  64.3 2.6 fusion.19
  66.9 0.0 collective-permute-done.1
  66.9 2.5 fusion.22
  69.5 0.8 pad_maximum_fusion.1
  70.3 0.0 all-reduce.2.cloned.1.call-update
  70.3 0.3 copy.29
  70.6 40.9 %all-reduce.2.cloned.1.call-done = f32[3,144,256]{2,1,0:T(8,128)} async-done(((f32[3,144,256]{2,1,0:T(8,128)}), f32[3,144,256]{2,1,0:T(8,128)}) %all-reduce.2.cloned.1.call-update) | async-done | bytes 442384 | tf_op jit(solution)/shard_map/psum | solution.py:72
  111.5 1.0 fusion.31
  112.6 0.0 copy-start.10
  112.6 0.7 dot_general.51
  113.2 0.0 copy-done.10
  113.2 0.9 convolution_bitcast_fusion.1
  114.2 0.0 copy-start.2
  114.2 0.0 copy-start.12
  114.2 2.3 copy.18
  116.4 0.0 copy-done.2
  116.4 2.7 convolution_bitcast_fusion
  119.2 4.7 %concatenate.25 = f32[32,256,128]{2,1,0:T(8,128)} reshape(f32[2,16,128,256]{3,2,1,0:T(8,128)} %convolution_bitcast_fusion) | data formatting | bytes 8388608 | tf_op jit(solution)/shard_map/concatenate | solution.py:118
  123.9 7.6 %pad_maximum_fusion = f32[32,512,128]{2,1,0:T(8,128)} fusion(f32[32,256,128]{2,1,0:T(8,128)} %concatenate.25, f32[32,256,128]{2,1,0:T(8,128)} %bitcast.110), kind=kLoop, calls=%fused_computation | loop fusion | flops 2097152 | bytes 16777216 | tf_op jit(solution)/shard_map/concatenate | solution.py:118
  131.5 10.3 %all-to-all-start = ((f32[32,512,128]{2,1,0:T(8,128)}), f32[32,512,128]{2,1,0:T(8,128)}, u32[]{:S(2)}, u32[]{:S(2)}) async-start(f32[32,512,128]{2,1,0:T(8,128)} %pad_maximum_fusion), calls=%async_computation | async-start | bytes 16777216 | tf_op jit(solution)/shard_map/all_to_all | solution.py:119
  141.8 0.0 copy-done.14
  141.8 0.6 multiply_multiply_fusion
  142.3 3.9 %fusion.10 = (f32[144]{0:T(256)S(1)}, f32[144,4096]{1,0:T(8,128)}) fusion(bf16[1,144,4096]{2,1,0:T(8,128)(2,1)S(1)} %copy-done, f32[4096]{0:T(1024)S(1)} %bitcast.120, bf16[144,256]{1,0:T(8,128)(2,1)S(1)} %copy-done.11, bf16[4096,128]{1,0:T(8,128)(2,1)} %collective-permute-done, bf16[4096,128]{1,0:T(8,128)(2,1)S(1)} %copy-done.9, pred[]{:T(512)S(6)} %eq.18), kind=kOutput, calls=%fused_computation.19 | convolution fusion | flops 313786240 | bytes 5726785 | tf_op jit(solution)/shard_map/dot_general | solution.py:24
  146.3 6.4 %psum.23 = f32[144]{0:T(256)S(1)} all-reduce(f32[144]{0:T(256)S(1)} %get-tuple-element.14), channel_id=1, replica_groups=mesh['dp'=32,'section'=4,'mp'=2] {'mp'}, use_global_device_ids=true, to_apply=%region_5.6 | all-reduce | flops 144 | bytes 1152 | tf_op jit(solution)/shard_map/psum | solution.py:93
  152.7 2.8 fusion.9
  155.5 1.9 collective-permute-start.3
  157.5 3.6 fusion
  161.1 2.5 collective-permute-start.2
  163.6 162.4 %all-to-all-done = f32[32,512,128]{2,1,0:T(8,128)} async-done(((f32[32,512,128]{2,1,0:T(8,128)}), f32[32,512,128]{2,1,0:T(8,128)}, u32[]{:S(2)}, u32[]{:S(2)}) %all-to-all-start) | async-done | bytes 8388640 | tf_op jit(solution)/shard_map/all_to_all | solution.py:119
  326.0 4.5 %reduce_sum.39 = f32[512,128]{1,0:T(8,128)} reduce(f32[32,512,128]{2,1,0:T(8,128)} %all-to-all-done, f32[]{:T(128)} %constant.45.clone.1), dimensions={0}, to_apply=%region_6.7 | reduce | flops 2031616 | bytes 8650756 | tf_op jit(solution)/shard_map/reduce_sum | solution.py:119
  330.5 14.4 %collective-permute-start.4 = (f32[65536]{0:T(1024)}, f32[65536]{0:T(1024)}, u32[]{:S(2)}, u32[]{:S(2)}) collective-permute-start(f32[65536]{0:T(1024)} %bitcast.116), channel_id=1, source_target_pairs={{1,128},{9,136},{17,144},{25,152},{33,160},{41,168},{49,176},{57,1... | collective-permute-start | bytes 786440 | tf_op jit(solution)/shard_map/ppermute | solution.py:127
  344.9 0.0 collective-permute-done.3
  344.9 0.0 collective-permute-done.2
  344.9 10.6 %collective-permute-done.4 = f32[65536]{0:T(1024)} collective-permute-done((f32[65536]{0:T(1024)}, f32[65536]{0:T(1024)}, u32[]{:S(2)}, u32[]{:S(2)}) %collective-permute-start.4) | collective-permute-done | bytes 262176 | tf_op jit(solution)/shard_map/ppermute | solution.py:127
  355.5 1.1 select_multiply_fusion
  356.6 0.7 fusion.39
  357.2 0.7 slice.49
  357.9 1.0 copy.45
  358.9 1.0 copy.46
  (33 shorter events, 0.1 us)
Async XLA Ops:
  7.2 104.3 %all-reduce.2.cloned.1.call-start = ((), (), s32[]{:S(2)}) async-start(), calls=%async_computation.1 | async-start | bytes 884736 | tf_op jit(solution)/shard_map/psum | solution.py:72
  7.2 4.7 %copy-start.3 = (bf16[1,128,8192]{2,1,0:T(8,128)(2,1)S(1)}, bf16[1,128,8192]{2,1,0:T(8,128)(2,1)}, u32[]{:S(2)}) copy-start(bf16[1,128,8192]{2,1,0:T(8,128)(2,1)} %param.15) | copy-start | bytes 6291460
  10.4 5.1 %copy-start = (bf16[1,144,4096]{2,1,0:T(8,128)(2,1)S(1)}, bf16[1,144,4096]{2,1,0:T(8,128)(2,1)}, u32[]{:S(2)}) copy-start(bf16[1,144,4096]{2,1,0:T(8,128)(2,1)} %param.11) | copy-start | bytes 3538948
  10.4 5.4 %copy-start.22 = (s32[144]{0:T(256)S(1)}, s32[144]{0:T(256)}, u32[]{:S(2)}) copy-start(s32[144]{0:T(256)} %param.9) | copy-start | bytes 1732
  10.4 5.4 %copy-start.4 = (bf16[1,144,4096]{2,1,0:T(8,128)(2,1)S(1)}, bf16[1,144,4096]{2,1,0:T(8,128)(2,1)}, u32[]{:S(2)}) copy-start(bf16[1,144,4096]{2,1,0:T(8,128)(2,1)} %param.8) | copy-start | bytes 3538948
  10.4 5.4 %copy-start.16 = (bf16[4096]{0:T(1024)(128)(2,1)S(1)}, bf16[4096]{0:T(1024)(128)(2,1)}, u32[]{:S(2)}) copy-start(bf16[4096]{0:T(1024)(128)(2,1)} %param.10) | copy-start | bytes 24580
  10.4 50.8 %collective-permute-start = (bf16[4096,128]{1,0:T(8,128)(2,1)}, bf16[4096,128]{1,0:T(8,128)(2,1)}, u32[]{:S(2)}, u32[]{:S(2)}) collective-permute-start(bf16[4096,128]{1,0:T(8,128)(2,1)} %get-tuple-element.5), channel_id=1, source_target_pairs={{0,1},{1,0},{2,3},{3,2},{4,5},{5,4},{6,7},{7,6},{8,9},{9,8},{10,11... | collective-permute-start | bytes 3145736 | tf_op jit(solution)/shard_map/ppermute | solution.py:14
  13.4 47.0 %copy-start.15 = (bf16[1,4096]{1,0:T(2,128)(2,1)S(1)}, bf16[1,4096]{1,0:T(2,128)(2,1)}, u32[]{:S(2)}) copy-start(bf16[1,4096]{1,0:T(2,128)(2,1)} %param.13) | copy-start | bytes 24580
  13.4 53.6 %collective-permute-start.1 = (bf16[128,4096]{1,0:T(8,128)(2,1)}, bf16[128,4096]{1,0:T(8,128)(2,1)}, u32[]{:S(2)}, u32[]{:S(2)}) collective-permute-start(bf16[128,4096]{1,0:T(8,128)(2,1)} %get-tuple-element.7), channel_id=1, source_target_pairs={{0,1},{1,0},{2,3},{3,2},{4,5},{5,4},{6,7},{7,6},{8,9},{9,8},{10,11... | collective-permute-start | bytes 3145736 | tf_op jit(solution)/shard_map/ppermute | solution.py:14
  15.8 44.5 %copy-start.19 = (pred[144]{0:T(512)(128)(4,1)}, pred[144]{0:T(512)(128)(4,1)S(1)}, u32[]{:S(2)}) copy-start(pred[144]{0:T(512)(128)(4,1)S(1)} %compare_or_fusion) | copy-start | bytes 436
  60.3 0.6 copy-start.13
  61.3 3.0 copy-start.8
  61.3 3.0 copy-start.17
  61.3 3.0 copy-start.20
  61.3 3.0 copy-start.23
  64.3 2.6 copy-start.1
  64.3 2.6 copy-start.6
  112.6 0.7 copy-start.10
  114.2 2.3 copy-start.2
  114.2 2.3 copy-start.12
  131.5 10.3 %copy-start.14 = (f32[1,144]{1,0:T(1,128)S(1)}, f32[1,144]{1,0:T(1,128)}, u32[]{:S(2)}) copy-start(f32[1,144]{1,0:T(1,128)} %copy-done.13) | copy-start | bytes 1732
  131.5 10.9 %copy-start.9 = (bf16[4096,128]{1,0:T(8,128)(2,1)S(1)}, bf16[4096,128]{1,0:T(8,128)(2,1)}, u32[]{:S(2)}) copy-start(bf16[4096,128]{1,0:T(8,128)(2,1)} %get-tuple-element.4) | copy-start | bytes 3145732
  131.5 10.9 %copy-start.11 = (bf16[144,256]{1,0:T(8,128)(2,1)S(1)}, bf16[144,256]{1,0:T(8,128)(2,1)}, u32[]{:S(2)}) copy-start(bf16[144,256]{1,0:T(8,128)(2,1)} %copy-done.10) | copy-start | bytes 221188
  131.5 194.5 %all-to-all-start = ((f32[32,512,128]{2,1,0:T(8,128)}), f32[32,512,128]{2,1,0:T(8,128)}, u32[]{:S(2)}, u32[]{:S(2)}) async-start(f32[32,512,128]{2,1,0:T(8,128)} %pad_maximum_fusion), calls=%async_computation | async-start | bytes 16777216 | tf_op jit(solution)/shard_map/all_to_all | solution.py:119
  152.7 4.7 %copy-start.5 = (bf16[1,144,4096]{2,1,0:T(8,128)(2,1)S(1)}, bf16[1,144,4096]{2,1,0:T(8,128)(2,1)}, u32[]{:S(2)}) copy-start(bf16[1,144,4096]{2,1,0:T(8,128)(2,1)} %param.8) | copy-start | bytes 3538948
  152.7 4.7 %copy-start.7 = (bf16[128,4096]{1,0:T(8,128)(2,1)S(1)}, bf16[128,4096]{1,0:T(8,128)(2,1)}, u32[]{:S(2)}) copy-start(bf16[128,4096]{1,0:T(8,128)(2,1)} %get-tuple-element.6) | copy-start | bytes 3145732
  152.7 4.8 %copy-start.18 = (bf16[4096]{0:T(1024)(128)(2,1)S(1)}, bf16[4096]{0:T(1024)(128)(2,1)}, u32[]{:S(2)}) copy-start(bf16[4096]{0:T(1024)(128)(2,1)} %param.10) | copy-start | bytes 24580
  152.7 4.8 %copy-start.21 = (pred[144]{0:T(512)(128)(4,1)S(1)}, pred[144]{0:T(512)(128)(4,1)}, u32[]{:S(2)}) copy-start(pred[144]{0:T(512)(128)(4,1)} %copy-done.19) | copy-start | bytes 436
  155.5 189.4 %collective-permute-start.3 = (bf16[144,4096]{1,0:T(8,128)(2,1)S(1)}, bf16[144,4096]{1,0:T(8,128)(2,1)S(1)}, u32[]{:S(2)}, u32[]{:S(2)}) collective-permute-start(bf16[144,4096]{1,0:T(8,128)(2,1)S(1)} %fusion.9), channel_id=1, source_target_pairs={{2,0},{4,2},{6,4},{3,1},{5,3},{7,5},{10,8},{12,10},{14,12},{11,9},... | collective-permute-start | bytes 3538952 | tf_op jit(solution)/shard_map/ppermute | solution.py:10
  161.1 183.8 %collective-permute-start.2 = (bf16[144,4096]{1,0:T(8,128)(2,1)}, bf16[144,4096]{1,0:T(8,128)(2,1)S(1)}, u32[]{:S(2)}, u32[]{:S(2)}) collective-permute-start(bf16[144,4096]{1,0:T(8,128)(2,1)} %fusion), channel_id=1, source_target_pairs={{0,2},{2,4},{4,6},{1,3},{3,5},{5,7},{8,10},{10,12},{12,14},{9,11},... | collective-permute-start | bytes 3538952 | tf_op jit(solution)/shard_map/ppermute | solution.py:10
  330.5 25.0 %collective-permute-start.4 = (f32[65536]{0:T(1024)}, f32[65536]{0:T(1024)}, u32[]{:S(2)}, u32[]{:S(2)}) collective-permute-start(f32[65536]{0:T(1024)} %bitcast.116), channel_id=1, source_target_pairs={{1,128},{9,136},{17,144},{25,152},{33,160},{41,168},{49,176},{57,1... | collective-permute-start | bytes 786440 | tf_op jit(solution)/shard_map/ppermute | solution.py:127
Sparse Core Ops, SparseCore 0:
  70.4 41.0 all-reduce.1

commit v2 on v1

--- a/solution.py
+++ b/solution.py
@@ -12,6 +12,10 @@
 
 def swapped(shard, axis):
     return lax.ppermute(shard, axis, [(0, 1), (1, 0)])
+
+
+def pair_sum(shard, axis):
+    return shard + swapped(shard, axis)
 
 
 def contract_rows(left, right):
@@ -58,7 +62,7 @@
 
     input_values = inputs.astype(jnp.float32)
     saved_values = saved.astype(jnp.float32)
-    squares = lax.psum(
+    squares = pair_sum(
         jnp.stack(
             [jnp.sum(input_values * input_values, axis=1), jnp.sum(saved_values * saved_values, axis=1)]
         ),
@@ -69,7 +73,7 @@
     normed = (input_values * scale * gain_row).astype(jnp.bfloat16)
     saved_normed = (saved_values * saved_scale * gain_row).astype(jnp.bfloat16)
 
-    partials = lax.psum(
+    partials = pair_sum(
         jnp.stack(
             [
                 jnp.dot(normed, down_half, preferred_element_type=jnp.float32),
@@ -90,7 +94,7 @@
         jnp.bfloat16
     )
     scaled_grad = contract_cols(pre_grad, down_half) * gain_row
-    row_dot = lax.psum(jnp.sum(saved_values * scaled_grad, axis=1), "mp")
+    row_dot = pair_sum(jnp.sum(saved_values * scaled_grad, axis=1), "mp")
     cubed = saved_scale * saved_scale * saved_scale
     input_grad = (
         upstream.astype(jnp.float32)

time: 369 us -> 314 us (0.85)
  blocking collectives: 49.8 us -> 0 us
  between operations: 14.4 us -> 1 us
  waiting for transfers between devices: 214 us -> 224 us
    psum x2 -> x0, blocking collectives: 49.8 us -> none  [the longest x1 43.4 us: on_device(): lax.psum(jnp.stack([jnp.sum(input_values * input_values, axis=1), jnp.sum...]
    ppermute x2 -> x5, waiting for transfers between devices: 0.01 us -> 47.3 us  [swapped(): return lax.ppermute(shard, axis, [(0, 1), (1, 0)])]
    psum x1 -> x0, waiting for transfers between devices: 40.9 us -> none  [on_device(): lax.psum(jnp.stack([jnp.dot(normed, down_half, preferred_element_type=jnp...]
    ppermute x1, starting transfers between devices: 14.4 us -> 5.14 us  [on_device(): moved = lax.ppermute(summed, ('dp', 'mp'), pairs)]
    ppermute x2 -> x5, starting transfers between devices: 3.62 us -> 9.53 us  [swapped(): return lax.ppermute(shard, axis, [(0, 1), (1, 0)])]
  transfers between devices with their start and end apart: 7 -> 9, of which waited for: 3 -> 5; matrix products, arithmetic and copies ran while one was open for 7% -> 7% of each run, Pallas kernels for 0% -> 0%
where the time goes in v2:
time: 314 us; the launch traced here: 311 us
  waiting for transfers between devices  224 us (71%)
  starting transfers between devices  31.8 us (10%)
  matrix products  19 us (6%)
  other arithmetic  18.9 us (6%)
  local copies, waits for them, and re-layouts  16.6 us (5%)
    all_to_all x1, waiting for transfers between devices, on_device(): lax.all_to_all(slots, 'dp', 0, 0, tiled=True).sum(axis=0).reshape(-1)  166 us
    ppermute x5, waiting for transfers between devices, swapped(): return lax.ppermute(shard, axis, [(0, 1), (1, 0)])  47.3 us
    all_to_all x1, starting transfers between devices, on_device(): lax.all_to_all(slots, 'dp', 0, 0, tiled=True).sum(axis=0).reshape(-1)  11.5 us
    ppermute x1, waiting for transfers between devices, on_device(): moved = lax.ppermute(summed, ('dp', 'mp'), pairs)  11.3 us
    ppermute x5, starting transfers between devices, swapped(): return lax.ppermute(shard, axis, [(0, 1), (1, 0)])  9.53 us
    concatenate x1, other arithmetic, on_device(): jnp.concatenate([down_slots, up_slots], axis=1).reshape(replicas, -1, lanes)  7.65 us
  transfers between devices with their start and end apart: 9, of which 5 were waited for; matrix products, arithmetic and copies ran while one was open for 7% of the time, Pallas kernels for 0%

profile of v2, /device:TPU:38, one launch (start us, length us, event | category | flops | bytes accessed | tf_op | source)
XLA Modules:
  0.0 311.5 jit_solution(11516774003125739387)
XLA Ops:
  0.6 0.0 copy-start.2
  0.6 1.7 fusion.4
  2.4 0.7 compare_or_fusion
  3.1 1.8 fusion.1
  4.8 1.5 collective-permute-start
  6.3 0.0 copy-done.2
  6.3 1.2 dynamic-slice_bitcast_fusion.3
  7.5 0.0 copy-done.17
  7.5 2.2 collective-permute-start.1
  9.7 1.5 dynamic-slice_bitcast_fusion.1
  11.2 1.4 collective-permute-start.2
  12.6 0.0 collective-permute-done
  12.7 0.4 fusion.6
  13.0 22.3 %collective-permute-done.1 = bf16[4096,128]{1,0:T(8,128)(2,1)S(1)} collective-permute-done((bf16[4096,128]{1,0:T(8,128)(2,1)}, bf16[4096,128]{1,0:T(8,128)(2,1)S(1)}, u32[]{:S(2)}, u32[]{:S(2)}) %collective-permute-start.1) | collective-permute-done | bytes 1048608 | tf_op jit(solution)/shard_map/ppermute | solution.py:14
  35.3 1.0 copy-done.20
  36.3 0.0 copy-done.9
  36.3 0.0 copy-start.21
  36.3 2.3 convolution_bitcast_fusion.2
  38.7 0.0 copy-done.11
  38.7 0.0 copy-done.5
  38.7 0.0 copy-done.15
  38.7 0.0 copy-done.18
  38.7 0.0 copy-done.21
  38.7 0.0 copy-start.1
  38.8 0.0 copy-start.7
  38.8 2.6 fusion.19
  41.4 15.1 %collective-permute-done.2 = bf16[128,4096]{1,0:T(8,128)(2,1)} collective-permute-done((bf16[128,4096]{1,0:T(8,128)(2,1)}, bf16[128,4096]{1,0:T(8,128)(2,1)}, u32[]{:S(2)}, u32[]{:S(2)}) %collective-permute-start.2) | collective-permute-done | bytes 1048608 | tf_op jit(solution)/shard_map/ppermute | solution.py:14
  56.5 2.5 fusion.22
  59.1 2.2 collective-permute-start.3
  61.3 0.3 copy.29
  61.6 9.9 %collective-permute-done.3 = f32[3,144,256]{2,1,0:T(8,128)S(1)} collective-permute-done((f32[3,144,256]{2,1,0:T(8,128)S(1)}, f32[3,144,256]{2,1,0:T(8,128)S(1)}, u32[]{:S(2)}, u32[]{:S(2)}) %collective-permute-start.3) | collective-permute-done | bytes 442400 | tf_op jit(solution)/shard_map/ppermute | solution.py:14
  71.4 0.1 fusion.40
  71.5 0.0 copy-start.4
  71.5 0.8 copy-done.4
  72.3 0.7 fusion.31
  73.0 1.5 dot_general.51
  74.5 1.8 convolution_bitcast_fusion.1
  76.3 2.3 copy.18
  78.6 2.7 convolution_bitcast_fusion
  81.3 4.7 %concatenate.25 = f32[32,256,128]{2,1,0:T(8,128)} reshape(f32[2,16,128,256]{3,2,1,0:T(8,128)} %convolution_bitcast_fusion) | data formatting | bytes 8388608 | tf_op jit(solution)/shard_map/concatenate | solution.py:122
  86.0 7.6 %pad_maximum_fusion = f32[32,512,128]{2,1,0:T(8,128)} fusion(f32[32,256,128]{2,1,0:T(8,128)} %concatenate.25, f32[32,256,128]{2,1,0:T(8,128)} %bitcast.110), kind=kLoop, calls=%fused_computation | loop fusion | flops 2097152 | bytes 16777216 | tf_op jit(solution)/shard_map/concatenate | solution.py:122
  93.7 11.5 %all-to-all-start = ((f32[32,512,128]{2,1,0:T(8,128)}), f32[32,512,128]{2,1,0:T(8,128)}, u32[]{:S(2)}, u32[]{:S(2)}) async-start(f32[32,512,128]{2,1,0:T(8,128)} %pad_maximum_fusion), calls=%async_computation | async-start | bytes 16777216 | tf_op jit(solution)/shard_map/all_to_all | solution.py:123
  105.2 0.0 copy-start.6
  105.3 0.0 copy-start.8
  105.3 0.0 copy-start.16
  105.3 3.4 %fusion.10 = (f32[144]{0:T(256)S(1)}, f32[144,4096]{1,0:T(8,128)S(1)}) fusion(bf16[1,144,4096]{2,1,0:T(8,128)(2,1)S(1)} %copy-done, f32[4096]{0:T(1024)S(1)} %bitcast.120, bf16[144,256]{1,0:T(8,128)(2,1)} %get-tuple-element.9, bf16[4096,128]{1,0:T(8,128)(2,1)} %copy-done.20, bf16[4096,128]{1,0:T(8,128)(2,1)} %copy-done.9, pred[]{:T(512)S(6)} %eq.18), kind=kOutput, calls=%fused_computation.19 | convolution fusion | flops 313786240 | bytes 5726785 | tf_op jit(solution)/shard_map/dot_general | solution.py:28
  108.7 0.0 copy-start.13
  108.7 2.2 collective-permute-start.5
  111.0 0.0 copy-done.19
  111.0 3.6 %fusion = bf16[144,4096]{1,0:T(8,128)(2,1)} fusion(bf16[128,4096]{1,0:T(8,128)(2,1)} %collective-permute-done.2, bf16[128,4096]{1,0:T(8,128)(2,1)S(1)} %copy-done.8, pred[]{:T(512)S(6)} %eq.18, f32[3,144,256]{2,1,0:T(8,128)} %copy-done.4, bf16[4096]{0:T(1024)(128)(2,1)S(1)} %copy-done.16, bf16[1,144,4096]{2,1,0:T(8,128)(2,1)S(1)} %copy-done.6, ...), kind=kOutput, calls=%fused_computation.3 | convolution fusion | flops 313970688 | bytes 4612241 | tf_op jit(solution)/shard_map/dot_general | solution.py:88
  114.6 1.9 collective-permute-start.4
  116.5 0.0 collective-permute-done.5
  116.5 2.0 fusion.9
  118.6 3.6 %collective-permute-start.6 = (bf16[144,4096]{1,0:T(8,128)(2,1)}, bf16[144,4096]{1,0:T(8,128)(2,1)S(1)}, u32[]{:S(2)}, u32[]{:S(2)}) collective-permute-start(bf16[144,4096]{1,0:T(8,128)(2,1)} %fusion.9), channel_id=1, source_target_pairs={{2,0},{4,2},{6,4},{3,1},{5,3},{7,5},{10,8},{12,10},{14,12},{11,9},... | collective-permute-start | bytes 3538952 | tf_op jit(solution)/shard_map/ppermute | solution.py:10
  122.2 165.6 %all-to-all-done = f32[32,512,128]{2,1,0:T(8,128)} async-done(((f32[32,512,128]{2,1,0:T(8,128)}), f32[32,512,128]{2,1,0:T(8,128)}, u32[]{:S(2)}, u32[]{:S(2)}) %all-to-all-start) | async-done | bytes 8388640 | tf_op jit(solution)/shard_map/all_to_all | solution.py:123
  287.8 3.8 %reduce_sum.39 = f32[512,128]{1,0:T(8,128)S(1)} reduce(f32[32,512,128]{2,1,0:T(8,128)} %all-to-all-done, f32[]{:T(128)} %constant.45.clone.1), dimensions={0}, to_apply=%region_3.4 | reduce | flops 2031616 | bytes 8650756 | tf_op jit(solution)/shard_map/reduce_sum | solution.py:123
  291.6 5.1 %collective-permute-start.7 = (f32[65536]{0:T(1024)S(1)}, f32[65536]{0:T(1024)S(1)}, u32[]{:S(2)}, u32[]{:S(2)}) collective-permute-start(f32[65536]{0:T(1024)S(1)} %bitcast.116), channel_id=1, source_target_pairs={{1,128},{9,136},{17,144},{25,152},{33,160},{41,168},{49,176},{57,1... | collective-permute-start | bytes 786440 | tf_op jit(solution)/shard_map/ppermute | solution.py:131
  296.7 0.0 collective-permute-done.4
  296.8 0.0 collective-permute-done.6
  296.8 11.3 %collective-permute-done.7 = f32[65536]{0:T(1024)S(1)} collective-permute-done((f32[65536]{0:T(1024)S(1)}, f32[65536]{0:T(1024)S(1)}, u32[]{:S(2)}, u32[]{:S(2)}) %collective-permute-start.7) | collective-permute-done | bytes 262176 | tf_op jit(solution)/shard_map/ppermute | solution.py:131
  308.1 0.7 fusion.41
  308.7 0.7 slice.49
  309.4 1.0 copy.44
  310.4 1.0 copy.45
  (32 shorter events, 0.2 us)
Async XLA Ops:
  0.6 5.7 %copy-start.2 = (bf16[1,8192,128]{2,1,0:T(8,128)(2,1)S(1)}, bf16[1,8192,128]{2,1,0:T(8,128)(2,1)}, u32[]{:S(2)}) copy-start(bf16[1,8192,128]{2,1,0:T(8,128)(2,1)} %param.14) | copy-start | bytes 6291460
  3.1 4.4 %copy-start.17 = (pred[144]{0:T(512)(128)(4,1)}, pred[144]{0:T(512)(128)(4,1)S(1)}, u32[]{:S(2)}) copy-start(pred[144]{0:T(512)(128)(4,1)S(1)} %compare_or_fusion) | copy-start | bytes 436
  4.8 7.8 %collective-permute-start = (f32[2,144]{1,0:T(2,128)S(1)}, f32[2,144]{1,0:T(2,128)S(1)}, u32[]{:S(2)}, u32[]{:S(2)}) collective-permute-start(f32[2,144]{1,0:T(2,128)S(1)} %pad_maximum_fusion.2), channel_id=1, source_target_pairs={{0,1},{1,0},{2,3},{3,2},{4,5},{5,4},{6,7},{7,6},{8,9},{9,8},{10,11... | collective-permute-start | bytes 3464 | tf_op jit(solution)/shard_map/ppermute | solution.py:14
  6.3 3.4 %copy-start.3 = (bf16[1,128,8192]{2,1,0:T(8,128)(2,1)S(1)}, bf16[1,128,8192]{2,1,0:T(8,128)(2,1)}, u32[]{:S(2)}) copy-start(bf16[1,128,8192]{2,1,0:T(8,128)(2,1)} %param.15) | copy-start | bytes 6291460
  7.5 28.8 %copy-start.9 = (bf16[4096,128]{1,0:T(8,128)(2,1)}, bf16[4096,128]{1,0:T(8,128)(2,1)S(1)}, u32[]{:S(2)}) copy-start(bf16[4096,128]{1,0:T(8,128)(2,1)S(1)} %get-tuple-element.4) | copy-start | bytes 3145732
  7.5 5.1 %copy-start.14 = (bf16[1,4096]{1,0:T(2,128)(2,1)S(1)}, bf16[1,4096]{1,0:T(2,128)(2,1)}, u32[]{:S(2)}) copy-start(bf16[1,4096]{1,0:T(2,128)(2,1)} %param.13) | copy-start | bytes 24580
  7.5 5.2 %copy-start = (bf16[1,144,4096]{2,1,0:T(8,128)(2,1)S(1)}, bf16[1,144,4096]{2,1,0:T(8,128)(2,1)}, u32[]{:S(2)}) copy-start(bf16[1,144,4096]{2,1,0:T(8,128)(2,1)} %param.11) | copy-start | bytes 3538948
  7.5 27.8 %collective-permute-start.1 = (bf16[4096,128]{1,0:T(8,128)(2,1)}, bf16[4096,128]{1,0:T(8,128)(2,1)S(1)}, u32[]{:S(2)}, u32[]{:S(2)}) collective-permute-start(bf16[4096,128]{1,0:T(8,128)(2,1)} %get-tuple-element.5), channel_id=1, source_target_pairs={{0,1},{1,0},{2,3},{3,2},{4,5},{5,4},{6,7},{7,6},{8,9},{9,8},{10,11... | collective-permute-start | bytes 3145736 | tf_op jit(solution)/shard_map/ppermute | solution.py:14
  11.2 45.3 %collective-permute-start.2 = (bf16[128,4096]{1,0:T(8,128)(2,1)}, bf16[128,4096]{1,0:T(8,128)(2,1)}, u32[]{:S(2)}, u32[]{:S(2)}) collective-permute-start(bf16[128,4096]{1,0:T(8,128)(2,1)} %get-tuple-element.7), channel_id=1, source_target_pairs={{0,1},{1,0},{2,3},{3,2},{4,5},{5,4},{6,7},{7,6},{8,9},{9,8},{10,11... | collective-permute-start | bytes 3145736 | tf_op jit(solution)/shard_map/ppermute | solution.py:14
  12.6 26.0 %copy-start.11 = (f32[1,144]{1,0:T(1,128)}, f32[1,144]{1,0:T(1,128)S(1)}, u32[]{:S(2)}) copy-start(f32[1,144]{1,0:T(1,128)S(1)} %get-tuple-element.13) | copy-start | bytes 1732
  35.3 1.0 copy-start.20
  36.3 2.4 copy-start.5
  36.3 2.4 copy-start.15
  36.3 2.4 copy-start.18
  36.3 2.4 copy-start.21
  38.7 17.8 %copy-start.1 = (bf16[1,144,4096]{2,1,0:T(8,128)(2,1)S(1)}, bf16[1,144,4096]{2,1,0:T(8,128)(2,1)}, u32[]{:S(2)}) copy-start(bf16[1,144,4096]{2,1,0:T(8,128)(2,1)} %param.12) | copy-start | bytes 3538948
  38.8 17.7 %copy-start.7 = (bf16[128,4096]{1,0:T(8,128)(2,1)S(1)}, bf16[128,4096]{1,0:T(8,128)(2,1)}, u32[]{:S(2)}) copy-start(bf16[128,4096]{1,0:T(8,128)(2,1)} %get-tuple-element.6) | copy-start | bytes 3145732
  59.1 12.4 %collective-permute-start.3 = (f32[3,144,256]{2,1,0:T(8,128)S(1)}, f32[3,144,256]{2,1,0:T(8,128)S(1)}, u32[]{:S(2)}, u32[]{:S(2)}) collective-permute-start(f32[3,144,256]{2,1,0:T(8,128)S(1)} %pad_maximum_fusion.1), channel_id=1, source_target_pairs={{0,1},{1,0},{2,3},{3,2},{4,5},{5,4},{6,7},{7,6},{8,9},{9,8},{10,11... | collective-permute-start | bytes 1327112 | tf_op jit(solution)/shard_map/ppermute | solution.py:14
  71.5 0.8 copy-start.4
  76.3 2.3 copy-start.10
  93.7 11.6 %copy-start.12 = (f32[1,144]{1,0:T(1,128)S(1)}, f32[1,144]{1,0:T(1,128)}, u32[]{:S(2)}) copy-start(f32[1,144]{1,0:T(1,128)} %copy-done.11) | copy-start | bytes 1732
  93.7 194.1 %all-to-all-start = ((f32[32,512,128]{2,1,0:T(8,128)}), f32[32,512,128]{2,1,0:T(8,128)}, u32[]{:S(2)}, u32[]{:S(2)}) async-start(f32[32,512,128]{2,1,0:T(8,128)} %pad_maximum_fusion), calls=%async_computation | async-start | bytes 16777216 | tf_op jit(solution)/shard_map/all_to_all | solution.py:123
  105.2 5.7 %copy-start.6 = (bf16[1,144,4096]{2,1,0:T(8,128)(2,1)S(1)}, bf16[1,144,4096]{2,1,0:T(8,128)(2,1)}, u32[]{:S(2)}) copy-start(bf16[1,144,4096]{2,1,0:T(8,128)(2,1)} %param.8) | copy-start | bytes 3538948
  105.3 5.7 %copy-start.8 = (bf16[128,4096]{1,0:T(8,128)(2,1)S(1)}, bf16[128,4096]{1,0:T(8,128)(2,1)}, u32[]{:S(2)}) copy-start(bf16[128,4096]{1,0:T(8,128)(2,1)} %get-tuple-element.6) | copy-start | bytes 3145732
  105.3 5.7 %copy-start.16 = (bf16[4096]{0:T(1024)(128)(2,1)S(1)}, bf16[4096]{0:T(1024)(128)(2,1)}, u32[]{:S(2)}) copy-start(bf16[4096]{0:T(1024)(128)(2,1)} %param.10) | copy-start | bytes 24580
  105.3 5.7 %copy-start.19 = (pred[144]{0:T(512)(128)(4,1)S(1)}, pred[144]{0:T(512)(128)(4,1)}, u32[]{:S(2)}) copy-start(pred[144]{0:T(512)(128)(4,1)} %copy-done.17) | copy-start | bytes 436
  108.7 7.8 %copy-start.13 = (f32[1,144]{1,0:T(1,128)S(1)}, f32[1,144]{1,0:T(1,128)}, u32[]{:S(2)}) copy-start(f32[1,144]{1,0:T(1,128)} %copy-done.11) | copy-start | bytes 1732
  108.7 7.8 %collective-permute-start.5 = (f32[144]{0:T(256)S(1)}, f32[144]{0:T(256)S(1)}, u32[]{:S(2)}, u32[]{:S(2)}) collective-permute-start(f32[144]{0:T(256)S(1)} %get-tuple-element.14), channel_id=1, source_target_pairs={{0,1},{1,0},{2,3},{3,2},{4,5},{5,4},{6,7},{7,6},{8,9},{9,8},{10,11... | collective-permute-start | bytes 1736 | tf_op jit(solution)/shard_map/ppermute | solution.py:14
  114.6 182.2 %collective-permute-start.4 = (bf16[144,4096]{1,0:T(8,128)(2,1)}, bf16[144,4096]{1,0:T(8,128)(2,1)S(1)}, u32[]{:S(2)}, u32[]{:S(2)}) collective-permute-start(bf16[144,4096]{1,0:T(8,128)(2,1)} %fusion), channel_id=1, source_target_pairs={{0,2},{2,4},{4,6},{1,3},{3,5},{5,7},{8,10},{10,12},{12,14},{9,11},... | collective-permute-start | bytes 3538952 | tf_op jit(solution)/shard_map/ppermute | solution.py:10
  118.6 178.2 %collective-permute-start.6 = (bf16[144,4096]{1,0:T(8,128)(2,1)}, bf16[144,4096]{1,0:T(8,128)(2,1)S(1)}, u32[]{:S(2)}, u32[]{:S(2)}) collective-permute-start(bf16[144,4096]{1,0:T(8,128)(2,1)} %fusion.9), channel_id=1, source_target_pairs={{2,0},{4,2},{6,4},{3,1},{5,3},{7,5},{10,8},{12,10},{14,12},{11,9},... | collective-permute-start | bytes 3538952 | tf_op jit(solution)/shard_map/ppermute | solution.py:10
  291.6 16.4 %collective-permute-start.7 = (f32[65536]{0:T(1024)S(1)}, f32[65536]{0:T(1024)S(1)}, u32[]{:S(2)}, u32[]{:S(2)}) collective-permute-start(f32[65536]{0:T(1024)S(1)} %bitcast.116), channel_id=1, source_target_pairs={{1,128},{9,136},{17,144},{25,152},{33,160},{41,168},{49,176},{57,1... | collective-permute-start | bytes 786440 | tf_op jit(solution)/shard_map/ppermute | solution.py:131

commit v3 on v2

--- a/solution.py
+++ b/solution.py
@@ -106,21 +106,35 @@
 
     blocks = replicas // 2
     units = down_local.shape[1]
+    block = full_width // replicas
+    ny = 4
+    nz = replicas // ny
     down_part = contract_rows(saved_normed, pre_grad)
     up_part = contract_rows(saved_hidden, upstream)
     down_slots = (
-        down_part.reshape(blocks, full_width // replicas, 2, units)
-        .transpose(2, 0, 1, 3)
-        .reshape(replicas, -1)
+        down_part.reshape(nz // 2, ny, block, 2, units)
+        .transpose(1, 3, 0, 2, 4)
+        .reshape(ny, nz, block * units)
     )
     up_slots = (
-        up_part.reshape(2, units, blocks, full_width // replicas)
-        .transpose(0, 2, 1, 3)
-        .reshape(replicas, -1)
+        up_part.reshape(2, units, nz // 2, ny, block)
+        .transpose(3, 0, 2, 1, 4)
+        .reshape(ny, nz, units * block)
     )
     lanes = 128
-    slots = jnp.concatenate([down_slots, up_slots], axis=1).reshape(replicas, -1, lanes)
-    summed = lax.all_to_all(slots, "dp", 0, 0, tiled=True).sum(axis=0).reshape(-1)
+    slots = jnp.concatenate([down_slots, up_slots], axis=2)
+    y_groups = [[z * ny + y for y in range(ny)] for z in range(nz)]
+    z_groups = [[z * ny + y for z in range(nz)] for y in range(ny)]
+    over_y = lax.all_to_all(
+        slots.reshape(ny, -1, lanes), "dp", 0, 0, tiled=True, axis_index_groups=y_groups
+    ).sum(axis=0)
+    summed = (
+        lax.all_to_all(
+            over_y.reshape(nz, -1, lanes), "dp", 0, 0, tiled=True, axis_index_groups=z_groups
+        )
+        .sum(axis=0)
+        .reshape(-1)
+    )
     slot = lax.axis_index("dp")
     keeps = (slot // blocks) == half
     pairs = []
@@ -130,8 +144,8 @@
                 pairs.append((j * 2 + m, (j ^ blocks) * 2 + (1 - m)))
     moved = lax.ppermute(summed, ("dp", "mp"), pairs)
     mine = jnp.where(keeps, summed, moved) * (1.0 / replicas)
-    down_grad = mine[: down_slots.shape[1]].reshape(full_width // replicas, units)
-    up_grad = mine[down_slots.shape[1] :].reshape(units, full_width // replicas)
+    down_grad = mine[: block * units].reshape(block, units)
+    up_grad = mine[block * units :].reshape(units, block)
     return (next_input[None], prev_grad[None], down_grad[None], up_grad[None])
 
 

time: 314 us -> 306 us (0.975)
  waiting for transfers between devices: 224 us -> 92.5 us
  blocking collectives: 0 us -> 99.5 us
  local copies, waits for them, and re-layouts: 16.6 us -> 43.4 us
  starting transfers between devices: 31.8 us -> 26.9 us
    all_to_all x1, waiting for transfers between devices: 166 us -> 37.2 us  [on_device(): lax.all_to_all(over_y.reshape(nz, -1, lanes), 'dp', 0, 0, tiled=True, axi...]
    all_to_all x0 -> x1, blocking collectives: none -> 99.5 us  [on_device(): lax.all_to_all(slots.reshape(ny, -1, lanes), 'dp', 0, 0, tiled=True, axis...]
    reshape x0 -> x4, local copies, waits for them, and re-layouts: none -> 24.8 us  [the longest x2 12.5 us: on_device(): up_slots = up_part.reshape(2, units, nz // 2, ny, block).transpose(3, 0,...]
    concatenate x1 -> x0, local copies, waits for them, and re-layouts: 4.72 us -> none  [on_device(): jnp.concatenate([down_slots, up_slots], axis=1).reshape(replicas, -1, lanes)]
    ppermute x5, waiting for transfers between devices: 47.3 us -> 43.7 us  [swapped(): return lax.ppermute(shard, axis, [(0, 1), (1, 0)])]
    dot_general x1 -> x4, local copies, waits for them, and re-layouts: 1.54 us -> 4.89 us  [contract_rows(): lax.dot_general(left, right, (((0,), (0,)), ((), ())), preferred_element_...]
  transfers between devices with their start and end apart: 9 -> 9, of which waited for: 5 -> 5; matrix products, arithmetic and copies ran while one was open for 7% -> 11% of each run, Pallas kernels for 0% -> 0%
where the time goes in v3:
time: 306 us; the launch traced here: 305 us
  blocking collectives  99.5 us (33%)
  waiting for transfers between devices  92.5 us (30%)
  local copies, waits for them, and re-layouts  43.4 us (14%)
  starting transfers between devices  26.9 us (9%)
  matrix products  21.3 us (7%)
  other arithmetic  20.6 us (7%)
    all_to_all x1, blocking collectives, on_device(): lax.all_to_all(slots.reshape(ny, -1, lanes), 'dp', 0, 0, tiled=True, axis...  99.5 us
    ppermute x5, waiting for transfers between devices, swapped(): return lax.ppermute(shard, axis, [(0, 1), (1, 0)])  43.7 us
    all_to_all x1, waiting for transfers between devices, on_device(): lax.all_to_all(over_y.reshape(nz, -1, lanes), 'dp', 0, 0, tiled=True, axi...  37.2 us
    reshape x2, local copies, waits for them, and re-layouts, on_device(): up_slots = up_part.reshape(2, units, nz // 2, ny, block).transpose(3, 0,...  12.5 us
    ppermute x1, waiting for transfers between devices, on_device(): moved = lax.ppermute(summed, ('dp', 'mp'), pairs)  11.5 us
    all_to_all x1, starting transfers between devices, on_device(): lax.all_to_all(over_y.reshape(nz, -1, lanes), 'dp', 0, 0, tiled=True, axi...  8.7 us
    ppermute x5, starting transfers between devices, swapped(): return lax.ppermute(shard, axis, [(0, 1), (1, 0)])  7.83 us
    dot_general x2, matrix products, contract_cols(): lax.dot_general(left, right, (((1,), (1,)), ((), ())), preferred_element_...  7.67 us
  transfers between devices with their start and end apart: 9, of which 5 were waited for; matrix products, arithmetic and copies ran while one was open for 11% of the time, Pallas kernels for 0%

profile of v3, /device:TPU:38, one launch (start us, length us, event | category | flops | bytes accessed | tf_op | source)
XLA Modules:
  0.0 305.2 jit_solution(13511308937673122014)
XLA Ops:
  0.7 0.0 copy-start.4
  0.7 0.0 copy-start.16
  0.7 2.8 dynamic-slice_bitcast_fusion.3
  3.5 1.4 collective-permute-start.1
  4.9 0.3 fusion.4
  5.2 0.0 copy-done.23
  5.3 0.5 fusion.1
  5.7 0.0 copy-done.20
  5.8 0.0 copy-start.13
  5.8 2.2 collective-permute-start
  8.0 3.1 %dynamic-slice_bitcast_fusion.1 = (bf16[128,4096]{1,0:T(8,128)(2,1)}, bf16[128,4096]{1,0:T(8,128)(2,1)}) fusion(bf16[1,128,8192]{2,1,0:T(8,128)(2,1)} %param.15, s32[]{:T(128)S(6)} %select_n.43, s32[]{:T(128)S(6)} %select_n.44), kind=kLoop, calls=%fused_computation.37 | loop fusion | bytes 4194312 | tf_op jit(solution)/shard_map/dynamic_slice | solution.py:58
  11.1 1.4 collective-permute-start.2
  12.5 18.8 %collective-permute-done = f32[2,144]{1,0:T(2,128)S(1)} collective-permute-done((f32[2,144]{1,0:T(2,128)S(1)}, f32[2,144]{1,0:T(2,128)S(1)}, u32[]{:S(2)}, u32[]{:S(2)}) %collective-permute-start) | collective-permute-done | bytes 1184 | tf_op jit(solution)/shard_map/ppermute | solution.py:14
  31.4 0.0 copy-start.14
  31.4 0.0 collective-permute-done.1
  31.4 0.0 copy-start.17
  31.4 2.4 convolution_bitcast_fusion.2
  33.9 0.0 copy-start
  33.9 3.3 %fusion.20 = f32[1,144,256]{2,1,0:T(8,128)S(1)} fusion(f32[4096]{0:T(1024)S(1)} %bitcast.114, f32[144]{0:T(256)S(1)} %bitcast.124, bf16[1,144,4096]{2,1,0:T(8,128)(2,1)S(1)} %copy-done.4, pred[144]{0:T(512)(128)(4,1)S(1)} %copy-done.21, bf16[4096]{0:T(1024)(128)(2,1)S(1)} %copy-done.17, bf16[4096,128]{1,0:T(8,128)(2,1)} %collective-permute-done.1, ...), kind=kOutput, calls=%fused_computation.33 | convolution fusion | flops 314376192 | bytes 3449553 | tf_op jit(solution)/shard_map/dot_general | solution.py:79
  37.2 15.5 %collective-permute-done.2 = bf16[128,4096]{1,0:T(8,128)(2,1)} collective-permute-done((bf16[128,4096]{1,0:T(8,128)(2,1)}, bf16[128,4096]{1,0:T(8,128)(2,1)}, u32[]{:S(2)}, u32[]{:S(2)}) %collective-permute-start.2) | collective-permute-done | bytes 1048608 | tf_op jit(solution)/shard_map/ppermute | solution.py:14
  52.7 0.0 copy-done.6
  52.7 2.5 fusion.23
  55.2 0.0 copy-start.10
  55.2 0.8 pad_maximum_fusion.1
  56.0 1.4 collective-permute-start.3
  57.5 0.9 dot_general.53
  58.4 1.2 multiply_multiply_fusion
  59.6 9.3 %collective-permute-done.3 = f32[3,144,256]{2,1,0:T(8,128)} collective-permute-done((f32[3,144,256]{2,1,0:T(8,128)}, f32[3,144,256]{2,1,0:T(8,128)}, u32[]{:S(2)}, u32[]{:S(2)}) %collective-permute-start.3) | collective-permute-done | bytes 442400 | tf_op jit(solution)/shard_map/ppermute | solution.py:14
  68.9 1.2 fusion.43
  70.2 0.8 copy-done.3
  70.9 0.7 fusion.34
  71.6 1.5 dot_general.51
  73.2 5.2 %fusion.10 = (f32[144]{0:T(256)}, f32[144,4096]{1,0:T(8,128)}) fusion(bf16[1,144,4096]{2,1,0:T(8,128)(2,1)S(1)} %copy-done.1, f32[4096]{0:T(1024)S(1)} %bitcast.115, bf16[144,256]{1,0:T(8,128)(2,1)} %get-tuple-element.11, bf16[4096,128]{1,0:T(8,128)(2,1)} %collective-permute-done.1, bf16[4096,128]{1,0:T(8,128)(2,1)} %copy-done.7, pred[]{:T(512)S(6)} %eq.18), kind=kOutput, calls=%fused_computation.19 | convolution fusion | flops 313786240 | bytes 5726785 | tf_op jit(solution)/shard_map/dot_general | solution.py:28
  78.4 1.4 collective-permute-start.5
  79.8 2.8 convolution_bitcast_fusion
  82.6 1.5 dot_general.48
  84.1 5.8 %reshape.87 = f32[4,8,32768]{2,0,1:T(4,128)} reshape(f32[4,2,4,128,256]{4,3,0,2,1:T(8,128)} %convolution_bitcast_fusion) | data formatting | bytes 8388608 | tf_op jit(solution)/shard_map/reshape | solution.py:122
  89.9 6.7 %copy.27 = f32[4,8,32768]{2,1,0:T(8,128)} copy(f32[4,8,32768]{2,0,1:T(4,128)} %reshape.87) | data formatting | bytes 8388608 | tf_op jit(solution)/shard_map/reshape | solution.py:122
  96.6 0.0 collective-permute-done.5
  96.6 0.7 add_multiply_fusion
  97.3 0.0 copy-done.15
  97.3 2.3 fusion.26
  99.6 0.9 dot_general.46
  100.5 0.9 convolution_bitcast_fusion.1
  101.4 2.2 copy.24
  103.7 4.9 %reshape.86 = f32[4,8,32768]{2,1,0:T(8,128)} reshape(f32[4,2,4,256,128]{4,3,2,1,0:T(8,128)} %copy.24) | data formatting | bytes 8388608 | tf_op jit(solution)/shard_map/reshape | solution.py:117
  108.6 7.3 %pad_maximum_fusion = f32[4,8,65536]{2,1,0:T(8,128)} fusion(f32[4,8,32768]{2,1,0:T(8,128)} %copy.27, f32[4,8,32768]{2,1,0:T(8,128)} %reshape.86), kind=kLoop, calls=%fused_computation | loop fusion | flops 2097152 | bytes 16777216 | tf_op jit(solution)/shard_map/concatenate | solution.py:125
  115.9 7.3 %reshape.88 = f32[4,4096,128]{2,1,0:T(8,128)} reshape(f32[4,8,65536]{2,1,0:T(8,128)} %pad_maximum_fusion) | data formatting | bytes 16777216 | tf_op jit(solution)/shard_map/reshape | solution.py:129
  123.2 99.5 %all_to_all.10 = f32[4,4096,128]{2,1,0:T(8,128)} all-to-all(f32[4,4096,128]{2,1,0:T(8,128)} %reshape.88), channel_id=1, replica_groups={{0,8,16,24},{32,40,48,56},{64,72,80,88},{96,104,112,120},{128,136,144,1..., dimensions={0} | all-to-all | bytes 16777216 | tf_op jit(solution)/shard_map/all_to_all | solution.py:128
  222.7 5.5 %reduce_sum.48 = f32[4096,128]{1,0:T(8,128)} reduce(f32[4,4096,128]{2,1,0:T(8,128)} %all_to_all.10, f32[]{:T(128)} %constant.45.clone.1), dimensions={0}, to_apply=%region_3.4 | reduce | flops 1572864 | bytes 10485764 | tf_op jit(solution)/shard_map/reduce_sum | solution.py:130
  228.2 8.7 %all-to-all-start.1 = ((f32[8,512,128]{2,1,0:T(8,128)}), f32[8,512,128]{2,1,0:T(8,128)S(1)}, u32[]{:S(2)}, u32[]{:S(2)}) async-start(f32[8,512,128]{2,1,0:T(8,128)} %bitcast.105), calls=%async_computation.1 | async-start | bytes 4194304 | tf_op jit(solution)/shard_map/all_to_all | solution.py:132
  236.9 4.2 %fusion = bf16[144,4096]{1,0:T(8,128)(2,1)} fusion(bf16[128,4096]{1,0:T(8,128)(2,1)} %collective-permute-done.2, bf16[128,4096]{1,0:T(8,128)(2,1)} %get-tuple-element.6, pred[]{:T(512)S(6)} %eq.18, f32[3,144,256]{2,1,0:T(8,128)} %copy-done.3, bf16[4096]{0:T(1024)(128)(2,1)S(1)} %copy-done.18, bf16[1,144,4096]{2,1,0:T(8,128)(2,1)S(1)} %copy-done.5, ...), kind=kOutput, calls=%fused_computation.3 | convolution fusion | flops 313970688 | bytes 4612241 | tf_op jit(solution)/shard_map/dot_general | solution.py:88
  241.1 1.9 collective-permute-start.4
  243.0 3.6 %collective-permute-start.6 = (bf16[144,4096]{1,0:T(8,128)(2,1)}, bf16[144,4096]{1,0:T(8,128)(2,1)}, u32[]{:S(2)}, u32[]{:S(2)}) collective-permute-start(bf16[144,4096]{1,0:T(8,128)(2,1)} %get-tuple-element.9), channel_id=1, source_target_pairs={{2,0},{4,2},{6,4},{3,1},{5,3},{7,5},{10,8},{12,10},{14,12},{11,9},... | collective-permute-start | bytes 3538952 | tf_op jit(solution)/shard_map/ppermute | solution.py:10
  246.7 37.2 %all-to-all-done.1 = f32[8,512,128]{2,1,0:T(8,128)S(1)} async-done(((f32[8,512,128]{2,1,0:T(8,128)}), f32[8,512,128]{2,1,0:T(8,128)S(1)}, u32[]{:S(2)}, u32[]{:S(2)}) %all-to-all-start.1) | async-done | bytes 2097184 | tf_op jit(solution)/shard_map/all_to_all | solution.py:132
  283.9 0.1 reduce_sum.49
  284.0 4.8 %collective-permute-start.7 = (f32[65536]{0:T(1024)S(1)}, f32[65536]{0:T(1024)S(1)}, u32[]{:S(2)}, u32[]{:S(2)}) collective-permute-start(f32[65536]{0:T(1024)S(1)} %bitcast.109), channel_id=1, source_target_pairs={{1,128},{9,136},{17,144},{25,152},{33,160},{41,168},{49,176},{57,1... | collective-permute-start | bytes 786440 | tf_op jit(solution)/shard_map/ppermute | solution.py:145
  288.8 0.0 collective-permute-done.4
  288.9 0.0 collective-permute-done.6
  288.9 11.5 %collective-permute-done.7 = f32[65536]{0:T(1024)S(1)} collective-permute-done((f32[65536]{0:T(1024)S(1)}, f32[65536]{0:T(1024)S(1)}, u32[]{:S(2)}, u32[]{:S(2)}) %collective-permute-start.7) | collective-permute-done | bytes 262176 | tf_op jit(solution)/shard_map/ppermute | solution.py:145
  300.4 0.7 fusion.44
  301.1 0.7 slice.49
  301.8 1.0 copy.49
  302.8 2.4 copy.50
  (42 shorter events, 0.2 us)
Async XLA Ops:
  0.6 4.3 %copy-start.1 = (bf16[1,144,4096]{2,1,0:T(8,128)(2,1)S(1)}, bf16[1,144,4096]{2,1,0:T(8,128)(2,1)}, u32[]{:S(2)}) copy-start(bf16[1,144,4096]{2,1,0:T(8,128)(2,1)} %param.11) | copy-start | bytes 3538948
  0.6 4.6 %copy-start.23 = (s32[144]{0:T(256)S(1)}, s32[144]{0:T(256)}, u32[]{:S(2)}) copy-start(s32[144]{0:T(256)} %param.9) | copy-start | bytes 1732
  0.7 4.6 %copy-start.4 = (bf16[1,144,4096]{2,1,0:T(8,128)(2,1)S(1)}, bf16[1,144,4096]{2,1,0:T(8,128)(2,1)}, u32[]{:S(2)}) copy-start(bf16[1,144,4096]{2,1,0:T(8,128)(2,1)} %param.8) | copy-start | bytes 3538948
  0.7 4.6 %copy-start.16 = (bf16[4096]{0:T(1024)(128)(2,1)S(1)}, bf16[4096]{0:T(1024)(128)(2,1)}, u32[]{:S(2)}) copy-start(bf16[4096]{0:T(1024)(128)(2,1)} %param.10) | copy-start | bytes 24580
  3.5 27.9 %copy-start.7 = (bf16[4096,128]{1,0:T(8,128)(2,1)}, bf16[4096,128]{1,0:T(8,128)(2,1)S(1)}, u32[]{:S(2)}) copy-start(bf16[4096,128]{1,0:T(8,128)(2,1)S(1)} %get-tuple-element.4) | copy-start | bytes 3145732
  3.5 27.9 %collective-permute-start.1 = (bf16[4096,128]{1,0:T(8,128)(2,1)}, bf16[4096,128]{1,0:T(8,128)(2,1)}, u32[]{:S(2)}, u32[]{:S(2)}) collective-permute-start(bf16[4096,128]{1,0:T(8,128)(2,1)} %get-tuple-element.5), channel_id=1, source_target_pairs={{0,1},{1,0},{2,3},{3,2},{4,5},{5,4},{6,7},{7,6},{8,9},{9,8},{10,11... | collective-permute-start | bytes 3145736 | tf_op jit(solution)/shard_map/ppermute | solution.py:14
  5.3 0.5 copy-start.20
  5.8 6.7 %copy-start.13 = (bf16[1,4096]{1,0:T(2,128)(2,1)S(1)}, bf16[1,4096]{1,0:T(2,128)(2,1)}, u32[]{:S(2)}) copy-start(bf16[1,4096]{1,0:T(2,128)(2,1)} %param.13) | copy-start | bytes 24580
  5.8 25.5 %collective-permute-start = (f32[2,144]{1,0:T(2,128)S(1)}, f32[2,144]{1,0:T(2,128)S(1)}, u32[]{:S(2)}, u32[]{:S(2)}) collective-permute-start(f32[2,144]{1,0:T(2,128)S(1)} %pad_maximum_fusion.2), channel_id=1, source_target_pairs={{0,1},{1,0},{2,3},{3,2},{4,5},{5,4},{6,7},{7,6},{8,9},{9,8},{10,11... | collective-permute-start | bytes 3464 | tf_op jit(solution)/shard_map/ppermute | solution.py:14
  11.1 41.6 %collective-permute-start.2 = (bf16[128,4096]{1,0:T(8,128)(2,1)}, bf16[128,4096]{1,0:T(8,128)(2,1)}, u32[]{:S(2)}, u32[]{:S(2)}) collective-permute-start(bf16[128,4096]{1,0:T(8,128)(2,1)} %get-tuple-element.7), channel_id=1, source_target_pairs={{0,1},{1,0},{2,3},{3,2},{4,5},{5,4},{6,7},{7,6},{8,9},{9,8},{10,11... | collective-permute-start | bytes 3145736 | tf_op jit(solution)/shard_map/ppermute | solution.py:14
  31.4 2.4 copy-start.14
  31.4 2.4 copy-start.17
  31.4 2.4 copy-start.21
  33.8 21.4 %copy-start.8 = (f32[1,144,256]{2,1,0:T(8,128)}, f32[1,144,256]{2,1,0:T(8,128)S(1)}, u32[]{:S(2)}) copy-start(f32[1,144,256]{2,1,0:T(8,128)S(1)} %convolution_bitcast_fusion.2) | copy-start | bytes 442372
  33.9 18.9 %copy-start = (bf16[1,144,4096]{2,1,0:T(8,128)(2,1)S(1)}, bf16[1,144,4096]{2,1,0:T(8,128)(2,1)}, u32[]{:S(2)}) copy-start(bf16[1,144,4096]{2,1,0:T(8,128)(2,1)} %param.12) | copy-start | bytes 3538948
  33.9 18.9 %copy-start.6 = (bf16[128,4096]{1,0:T(8,128)(2,1)S(1)}, bf16[128,4096]{1,0:T(8,128)(2,1)}, u32[]{:S(2)}) copy-start(bf16[128,4096]{1,0:T(8,128)(2,1)} %get-tuple-element.6) | copy-start | bytes 3145732
  37.2 18.1 %copy-start.9 = (f32[1,144,256]{2,1,0:T(8,128)}, f32[1,144,256]{2,1,0:T(8,128)S(1)}, u32[]{:S(2)}) copy-start(f32[1,144,256]{2,1,0:T(8,128)S(1)} %fusion.20) | copy-start | bytes 442372
  55.2 2.2 copy-start.10
  56.0 12.9 %collective-permute-start.3 = (f32[3,144,256]{2,1,0:T(8,128)}, f32[3,144,256]{2,1,0:T(8,128)}, u32[]{:S(2)}, u32[]{:S(2)}) collective-permute-start(f32[3,144,256]{2,1,0:T(8,128)} %pad_maximum_fusion.1), channel_id=1, source_target_pairs={{0,1},{1,0},{2,3},{3,2},{4,5},{5,4},{6,7},{7,6},{8,9},{9,8},{10,11... | collective-permute-start | bytes 1327112 | tf_op jit(solution)/shard_map/ppermute | solution.py:14
  70.1 0.8 copy-start.3
  73.2 6.6 %copy-start.12 = (bf16[2,128,144]{1,0,2:T(2,128)(2,1)S(1)}, bf16[2,128,144]{1,0,2:T(2,128)(2,1)}, u32[]{:S(2)}) copy-start(bf16[2,128,144]{1,0,2:T(2,128)(2,1)} %dot_general.51) | copy-start | bytes 221188
  78.4 18.3 %collective-permute-start.5 = (f32[144]{0:T(256)}, f32[144]{0:T(256)}, u32[]{:S(2)}, u32[]{:S(2)}) collective-permute-start(f32[144]{0:T(256)} %get-tuple-element.16), channel_id=1, source_target_pairs={{0,1},{1,0},{2,3},{3,2},{4,5},{5,4},{6,7},{7,6},{8,9},{9,8},{10,11... | collective-permute-start | bytes 1736 | tf_op jit(solution)/shard_map/ppermute | solution.py:14
  89.9 7.4 %copy-start.2 = (f32[144,4096]{1,0:T(8,128)S(1)}, f32[144,4096]{1,0:T(8,128)}, u32[]{:S(2)}) copy-start(f32[144,4096]{1,0:T(8,128)} %get-tuple-element.17) | copy-start | bytes 7077892
  89.9 7.4 %copy-start.15 = (f32[1,144]{1,0:T(1,128)S(1)}, f32[1,144]{1,0:T(1,128)}, u32[]{:S(2)}) copy-start(f32[1,144]{1,0:T(1,128)} %copy-done.14) | copy-start | bytes 1732
  89.9 7.4 %copy-start.19 = (f32[144]{0:T(256)S(1)}, f32[144]{0:T(256)}, u32[]{:S(2)}) copy-start(f32[144]{0:T(256)} %multiply_multiply_fusion) | copy-start | bytes 1732
  99.6 0.9 copy-start.11
  228.2 8.7 %copy-start.5 = (bf16[1,144,4096]{2,1,0:T(8,128)(2,1)S(1)}, bf16[1,144,4096]{2,1,0:T(8,128)(2,1)}, u32[]{:S(2)}) copy-start(bf16[1,144,4096]{2,1,0:T(8,128)(2,1)} %param.8) | copy-start | bytes 3538948
  228.2 8.7 %copy-start.18 = (bf16[4096]{0:T(1024)(128)(2,1)S(1)}, bf16[4096]{0:T(1024)(128)(2,1)}, u32[]{:S(2)}) copy-start(bf16[4096]{0:T(1024)(128)(2,1)} %param.10) | copy-start | bytes 24580
  228.2 8.7 %copy-start.22 = (pred[144]{0:T(512)(128)(4,1)S(1)}, pred[144]{0:T(512)(128)(4,1)}, u32[]{:S(2)}) copy-start(pred[144]{0:T(512)(128)(4,1)} %copy-done.20) | copy-start | bytes 436
  228.2 55.7 %all-to-all-start.1 = ((f32[8,512,128]{2,1,0:T(8,128)}), f32[8,512,128]{2,1,0:T(8,128)S(1)}, u32[]{:S(2)}, u32[]{:S(2)}) async-start(f32[8,512,128]{2,1,0:T(8,128)} %bitcast.105), calls=%async_computation.1 | async-start | bytes 4194304 | tf_op jit(solution)/shard_map/all_to_all | solution.py:132
  241.1 47.8 %collective-permute-start.4 = (bf16[144,4096]{1,0:T(8,128)(2,1)}, bf16[144,4096]{1,0:T(8,128)(2,1)S(1)}, u32[]{:S(2)}, u32[]{:S(2)}) collective-permute-start(bf16[144,4096]{1,0:T(8,128)(2,1)} %fusion), channel_id=1, source_target_pairs={{0,2},{2,4},{4,6},{1,3},{3,5},{5,7},{8,10},{10,12},{12,14},{9,11},... | collective-permute-start | bytes 3538952 | tf_op jit(solution)/shard_map/ppermute | solution.py:10
  243.0 45.8 %collective-permute-start.6 = (bf16[144,4096]{1,0:T(8,128)(2,1)}, bf16[144,4096]{1,0:T(8,128)(2,1)}, u32[]{:S(2)}, u32[]{:S(2)}) collective-permute-start(bf16[144,4096]{1,0:T(8,128)(2,1)} %get-tuple-element.9), channel_id=1, source_target_pairs={{2,0},{4,2},{6,4},{3,1},{5,3},{7,5},{10,8},{12,10},{14,12},{11,9},... | collective-permute-start | bytes 3538952 | tf_op jit(solution)/shard_map/ppermute | solution.py:10
  284.0 16.4 %collective-permute-start.7 = (f32[65536]{0:T(1024)S(1)}, f32[65536]{0:T(1024)S(1)}, u32[]{:S(2)}, u32[]{:S(2)}) collective-permute-start(f32[65536]{0:T(1024)S(1)} %bitcast.109), channel_id=1, source_target_pairs={{1,128},{9,136},{17,144},{25,152},{33,160},{41,168},{49,176},{57,1... | collective-permute-start | bytes 786440 | tf_op jit(solution)/shard_map/ppermute | solution.py:145

commit v4 on v3

--- a/solution.py
+++ b/solution.py
@@ -109,32 +109,24 @@
     block = full_width // replicas
     ny = 4
     nz = replicas // ny
-    down_part = contract_rows(saved_normed, pre_grad)
-    up_part = contract_rows(saved_hidden, upstream)
-    down_slots = (
-        down_part.reshape(nz // 2, ny, block, 2, units)
-        .transpose(1, 3, 0, 2, 4)
-        .reshape(ny, nz, block * units)
+    tokens = saved.shape[0]
+    rows = jnp.stack([saved_normed, upstream])
+    rows = rows.reshape(2, tokens, nz // 2, ny, block).transpose(3, 2, 0, 1, 4)
+    rows = jnp.broadcast_to(rows[:, None], (ny, 2, nz // 2, 2, tokens, block))
+    cols = jnp.stack([pre_grad, saved_hidden])
+    cols = cols.reshape(2, tokens, 2, units).transpose(2, 0, 1, 3)
+    cols = jnp.broadcast_to(cols[None, :, None], (ny, 2, nz // 2, 2, tokens, units))
+    slots = lax.dot_general(
+        rows, cols, (((4,), (4,)), ((0, 1, 2, 3), (0, 1, 2, 3))), preferred_element_type=jnp.float32
     )
-    up_slots = (
-        up_part.reshape(2, units, nz // 2, ny, block)
-        .transpose(3, 0, 2, 1, 4)
-        .reshape(ny, nz, units * block)
-    )
-    lanes = 128
-    slots = jnp.concatenate([down_slots, up_slots], axis=2)
     y_groups = [[z * ny + y for y in range(ny)] for z in range(nz)]
     z_groups = [[z * ny + y for z in range(nz)] for y in range(ny)]
     over_y = lax.all_to_all(
-        slots.reshape(ny, -1, lanes), "dp", 0, 0, tiled=True, axis_index_groups=y_groups
+        slots, "dp", 0, 0, tiled=True, axis_index_groups=y_groups
     ).sum(axis=0)
-    summed = (
-        lax.all_to_all(
-            over_y.reshape(nz, -1, lanes), "dp", 0, 0, tiled=True, axis_index_groups=z_groups
-        )
-        .sum(axis=0)
-        .reshape(-1)
-    )
+    summed = lax.all_to_all(
+        over_y.reshape(nz, 2, block, units), "dp", 0, 0, tiled=True, axis_index_groups=z_groups
+    ).sum(axis=0)
     slot = lax.axis_index("dp")
     keeps = (slot // blocks) == half
     pairs = []
@@ -144,8 +136,8 @@
                 pairs.append((j * 2 + m, (j ^ blocks) * 2 + (1 - m)))
     moved = lax.ppermute(summed, ("dp", "mp"), pairs)
     mine = jnp.where(keeps, summed, moved) * (1.0 / replicas)
-    down_grad = mine[: block * units].reshape(block, units)
-    up_grad = mine[block * units :].reshape(units, block)
+    down_grad = mine[0]
+    up_grad = mine[1].T
     return (next_input[None], prev_grad[None], down_grad[None], up_grad[None])
 
 

time: 306 us -> 258 us (0.84)
  local copies, waits for them, and re-layouts: 43.4 us -> 19.1 us
  waiting for transfers between devices: 92.5 us -> 80 us
  other arithmetic: 20.6 us -> 17 us
  matrix products: 21.3 us -> 17.9 us
  blocking collectives: 99.5 us -> 96.4 us
    reshape x4 -> x0, local copies, waits for them, and re-layouts: 24.8 us -> none  [the longest x2 12.5 us: on_device(): up_slots = up_part.reshape(2, units, nz // 2, ny, block).transpose(3, 0,...]
    concatenate x1 -> x0, other arithmetic: 7.28 us -> none  [on_device(): slots = jnp.concatenate([down_slots, up_slots], axis=2)]
    ppermute x5, waiting for transfers between devices: 43.7 us -> 37 us  [swapped(): return lax.ppermute(shard, axis, [(0, 1), (1, 0)])]
    all_to_all x1, waiting for transfers between devices: 37.2 us -> 30.6 us  [on_device(): lax.all_to_all(over_y.reshape(nz, 2, block, units), 'dp', 0, 0, tiled=Tru...]
    another operation x0 -> x4, local copies, waits for them, and re-layouts: none -> 5.72 us  [the longest x2 3.07 us: on_device(): cols = jnp.stack([pre_grad, saved_hidden])]
    dot_general x4 -> x0, local copies, waits for them, and re-layouts: 4.89 us -> none  [contract_rows(): lax.dot_general(left, right, (((0,), (0,)), ((), ())), preferred_element_...]
    transpose x0 -> x2, other arithmetic: none -> 4.17 us  [the longest x1 3.03 us: on_device(): rows = rows.reshape(2, tokens, nz // 2, ny, block).transpose(3, 2, 0, 1, 4)]
    convert_element_type x0 -> x3, other arithmetic: none -> 3.09 us  [the longest x1 2.01 us: on_device(): input_grad = (upstream.astype(jnp.float32) + saved_scale * scaled_grad -...]
where the time goes in v4:
time: 258 us
  blocking collectives  96.4 us (37%)
  waiting for transfers between devices  80 us (31%)
  starting transfers between devices  26.2 us (10%)
  local copies, waits for them, and re-layouts  19.1 us (7%)
  matrix products  17.9 us (7%)
  other arithmetic  17 us (7%)
    all_to_all x1, blocking collectives, on_device(): lax.all_to_all(slots, 'dp', 0, 0, tiled=True, axis_index_groups=y_groups)  96.4 us
    ppermute x5, waiting for transfers between devices, swapped(): return lax.ppermute(shard, axis, [(0, 1), (1, 0)])  37 us
    all_to_all x1, waiting for transfers between devices, on_device(): lax.all_to_all(over_y.reshape(nz, 2, block, units), 'dp', 0, 0, tiled=Tru...  30.6 us
    ppermute x1, waiting for transfers between devices, on_device(): moved = lax.ppermute(summed, ('dp', 'mp'), pairs)  12.3 us
    all_to_all x1, starting transfers between devices, on_device(): lax.all_to_all(over_y.reshape(nz, 2, block, units), 'dp', 0, 0, tiled=Tru...  8.7 us
    ppermute x5, starting transfers between devices, swapped(): return lax.ppermute(shard, axis, [(0, 1), (1, 0)])  7.9 us
    dot_general x2, matrix products, contract_cols(): lax.dot_general(left, right, (((1,), (1,)), ((), ())), preferred_element_...  6.11 us
    unnamed x59, local copies, waits for them, and re-layouts  5.61 us
  transfers between devices with their start and end apart: 9, of which 5 were waited for; matrix products, arithmetic and copies ran while one was open for 11% of the time, Pallas kernels for 0%

profile of v4, /device:TPU:38, one launch (start us, length us, event | category | flops | bytes accessed | tf_op | source)
XLA Modules:
  0.0 257.7 jit_solution(18306791033045090846)
XLA Ops:
  0.7 0.0 copy-start.4
  0.7 0.0 copy-start.21
  0.7 3.2 %dynamic-slice_bitcast_fusion.3 = (bf16[4096,128]{1,0:T(8,128)(2,1)}, bf16[4096,128]{1,0:T(8,128)(2,1)}) fusion(bf16[1,8192,128]{2,1,0:T(8,128)(2,1)} %param.14, s32[]{:T(128)S(6)} %select_n.43, s32[]{:T(128)S(6)} %select_n.44), kind=kLoop, calls=%fused_computation.44 | loop fusion | bytes 4194312 | tf_op jit(solution)/shard_map/dynamic_slice | solution.py:56
  3.9 1.4 collective-permute-start.1
  5.3 0.3 fusion.5
  5.6 0.0 copy-start.20
  5.6 0.5 fusion.14
  6.1 0.6 copy-done.19
  6.7 0.6 pad_maximum_fusion.1
  7.3 0.0 copy-done.20
  7.3 2.2 collective-permute-start
  9.5 3.1 %dynamic-slice_bitcast_fusion.1 = (bf16[128,4096]{1,0:T(8,128)(2,1)}, bf16[128,4096]{1,0:T(8,128)(2,1)}) fusion(bf16[1,128,8192]{2,1,0:T(8,128)(2,1)} %param.15, s32[]{:T(128)S(6)} %select_n.43, s32[]{:T(128)S(6)} %select_n.44), kind=kLoop, calls=%fused_computation.42 | loop fusion | bytes 4194312 | tf_op jit(solution)/shard_map/dynamic_slice | solution.py:58
  12.6 1.4 collective-permute-start.2
  14.0 0.9 stack.46
  15.0 16.8 %collective-permute-done = f32[2,144]{1,0:T(2,128)} collective-permute-done((f32[2,144]{1,0:T(2,128)}, f32[2,144]{1,0:T(2,128)}, u32[]{:S(2)}, u32[]{:S(2)}) %collective-permute-start) | collective-permute-done | bytes 1184 | tf_op jit(solution)/shard_map/ppermute | solution.py:14
  31.8 0.7 fusion.56
  32.5 0.0 collective-permute-done.1
  32.5 0.0 copy-start.5
  32.5 0.0 copy-start.22
  32.5 3.2 %fusion.30 = f32[1,144,256]{2,1,0:T(8,128)S(1)} fusion(bf16[1,144,4096]{2,1,0:T(8,128)(2,1)S(1)} %copy-done, f32[144]{0:T(256)S(1)} %bitcast.114, f32[4096]{0:T(1024)S(1)} %bitcast.110, bf16[4096,128]{1,0:T(8,128)(2,1)} %collective-permute-done.1, bf16[4096,128]{1,0:T(8,128)(2,1)} %get-tuple-element.12, pred[]{:T(512)S(6)} %eq.18), kind=kOutput, calls=%fused_computation.38 | convolution fusion | flops 313786368 | bytes 3441217 | tf_op jit(solution)/shard_map/dot_general | solution.py:80
  35.7 0.0 copy-start.10
  35.8 0.0 copy-done.5
  35.8 0.0 copy-start.8
  35.8 2.5 fusion.33
  38.4 14.7 %collective-permute-done.2 = bf16[128,4096]{1,0:T(8,128)(2,1)} collective-permute-done((bf16[128,4096]{1,0:T(8,128)(2,1)}, bf16[128,4096]{1,0:T(8,128)(2,1)}, u32[]{:S(2)}, u32[]{:S(2)}) %collective-permute-start.2) | collective-permute-done | bytes 1048608 | tf_op jit(solution)/shard_map/ppermute | solution.py:14
  53.1 2.5 fusion.36
  55.7 0.8 pad_maximum_fusion
  56.5 1.4 collective-permute-start.3
  57.9 0.4 fusion.13
  58.3 1.7 stack.45
  60.0 3.0 %maximum_bitcast_fusion = bf16[4,4,2,144,256]{4,0,1,3,2:T(4,128)(2,1)S(1)} fusion(bf16[1,144,4,4,256]{4,3,2,1,0:T(4,128)(2,1)S(1)} %stack.46, bf16[1,144,4,4,256]{4,3,2,1,0:T(4,128)(2,1)} %stack.45), kind=kLoop, calls=%fused_computation.23 | loop fusion | flops 1179648 | bytes 4718592 | tf_op jit(solution)/shard_map/transpose | solution.py:114
  63.1 0.8 copy.15
  63.9 5.5 %collective-permute-done.3 = f32[3,144,256]{2,1,0:T(8,128)} collective-permute-done((f32[3,144,256]{2,1,0:T(8,128)}, f32[3,144,256]{2,1,0:T(8,128)}, u32[]{:S(2)}, u32[]{:S(2)}) %collective-permute-start.3) | collective-permute-done | bytes 442400 | tf_op jit(solution)/shard_map/ppermute | solution.py:14
  69.4 1.1 fusion.57
  70.5 0.8 copy-done.3
  71.2 0.7 multiply_convert_fusion.1
  71.9 1.5 stack.48
  73.5 1.5 stack.49
  75.0 1.1 maximum_bitcast_fusion.1
  76.2 2.4 fusion.17
  78.6 96.4 %all_to_all.10 = f32[4,2,4,2,256,128]{5,4,3,2,1,0:T(8,128)} all-to-all(f32[4,2,4,2,256,128]{5,4,3,2,1,0:T(8,128)S(1)} %fusion.17), channel_id=1, replica_groups={{0,8,16,24},{32,40,48,56},{64,72,80,88},{96,104,112,120},{128,136,144,1..., dimensions={0} | all-to-all | bytes 16777216 | tf_op jit(solution)/shard_map/all_to_all | solution.py:124
  175.0 5.5 %reduce_sum.48 = f32[2,4,2,256,128]{4,3,2,1,0:T(8,128)} reduce(f32[4,2,4,2,256,128]{5,4,3,2,1,0:T(8,128)} %all_to_all.10, f32[]{:T(128)} %constant.45.clone.1), dimensions={0}, to_apply=%region_3.4 | reduce | flops 1572864 | bytes 10485764 | tf_op jit(solution)/shard_map/reduce_sum | solution.py:126
  180.6 8.7 %all-to-all-start.1 = ((f32[8,2,256,128]{3,2,1,0:T(8,128)}), f32[8,2,256,128]{3,2,1,0:T(8,128)S(1)}, u32[]{:S(2)}, u32[]{:S(2)}) async-start(f32[8,2,256,128]{3,2,1,0:T(8,128)} %bitcast.108), calls=%async_computation.1 | async-start | bytes 4194304 | tf_op jit(solution)/shard_map/all_to_all | solution.py:127
  189.3 0.0 copy-start.6
  189.3 0.0 copy-start.9
  189.3 0.0 copy-start.23
  189.3 3.6 %fusion.11 = (f32[144]{0:T(256)S(1)}, f32[144,4096]{1,0:T(8,128)S(1)}) fusion(bf16[1,144,4096]{2,1,0:T(8,128)(2,1)S(1)} %copy-done, f32[4096]{0:T(1024)S(1)} %bitcast.113, bf16[4096,128]{1,0:T(8,128)(2,1)} %collective-permute-done.1, bf16[4096,128]{1,0:T(8,128)(2,1)} %get-tuple-element.12, pred[]{:T(512)S(6)} %eq.18, f32[3,144,256]{2,1,0:T(8,128)} %copy-done.3), kind=kOutput, calls=%fused_computation.17 | convolution fusion | flops 314118016 | bytes 5947969 | tf_op jit(solution)/shard_map/dot_general | solution.py:28
  192.9 0.0 copy-start.2
  192.9 1.5 collective-permute-start.5
  194.4 3.6 %fusion = bf16[144,4096]{1,0:T(8,128)(2,1)} fusion(bf16[128,4096]{1,0:T(8,128)(2,1)} %collective-permute-done.2, bf16[128,4096]{1,0:T(8,128)(2,1)S(1)} %copy-done.9, pred[]{:T(512)S(6)} %eq.18, f32[3,144,256]{2,1,0:T(8,128)} %copy-done.3, bf16[4096]{0:T(1024)(128)(2,1)S(1)} %copy-done.23, bf16[1,144,4096]{2,1,0:T(8,128)(2,1)S(1)} %copy-done.6, ...), kind=kOutput, calls=%fused_computation.2 | convolution fusion | flops 313970688 | bytes 4612241 | tf_op jit(solution)/shard_map/dot_general | solution.py:88
  198.0 1.9 collective-permute-start.4
  199.9 0.0 collective-permute-done.5
  200.0 2.0 fusion.10
  202.0 3.6 %collective-permute-start.6 = (bf16[144,4096]{1,0:T(8,128)(2,1)}, bf16[144,4096]{1,0:T(8,128)(2,1)S(1)}, u32[]{:S(2)}, u32[]{:S(2)}) collective-permute-start(bf16[144,4096]{1,0:T(8,128)(2,1)} %fusion.10), channel_id=1, source_target_pairs={{2,0},{4,2},{6,4},{3,1},{5,3},{7,5},{10,8},{12,10},{14,12},{11,9},... | collective-permute-start | bytes 3538952 | tf_op jit(solution)/shard_map/ppermute | solution.py:10
  205.6 30.6 %all-to-all-done.1 = f32[8,2,256,128]{3,2,1,0:T(8,128)S(1)} async-done(((f32[8,2,256,128]{3,2,1,0:T(8,128)}), f32[8,2,256,128]{3,2,1,0:T(8,128)S(1)}, u32[]{:S(2)}, u32[]{:S(2)}) %all-to-all-start.1) | async-done | bytes 2097184 | tf_op jit(solution)/shard_map/all_to_all | solution.py:127
  236.3 0.1 reduce_sum.49
  236.4 4.1 %collective-permute-start.7 = (f32[2,256,128]{2,1,0:T(8,128)S(1)}, f32[2,256,128]{2,1,0:T(8,128)S(1)}, u32[]{:S(2)}, u32[]{:S(2)}) collective-permute-start(f32[2,256,128]{2,1,0:T(8,128)S(1)} %reduce_sum.49), channel_id=1, source_target_pairs={{1,128},{9,136},{17,144},{25,152},{33,160},{41,168},{49,176},{57,1... | collective-permute-start | bytes 786440 | tf_op jit(solution)/shard_map/ppermute | solution.py:137
  240.5 0.0 collective-permute-done.4
  240.5 0.0 collective-permute-done.6
  240.5 12.3 %collective-permute-done.7 = f32[2,256,128]{2,1,0:T(8,128)S(1)} collective-permute-done((f32[2,256,128]{2,1,0:T(8,128)S(1)}, f32[2,256,128]{2,1,0:T(8,128)S(1)}, u32[]{:S(2)}, u32[]{:S(2)}) %collective-permute-start.7) | collective-permute-done | bytes 262176 | tf_op jit(solution)/shard_map/ppermute | solution.py:137
  252.8 0.7 slice_bitcast_fusion.1
  253.5 0.8 copy.17
  254.3 2.4 copy.20
  256.6 1.0 copy.21
  (48 shorter events, 0.2 us)
Async XLA Ops:
  0.6 4.6 %copy-start = (bf16[1,144,4096]{2,1,0:T(8,128)(2,1)S(1)}, bf16[1,144,4096]{2,1,0:T(8,128)(2,1)}, u32[]{:S(2)}) copy-start(bf16[1,144,4096]{2,1,0:T(8,128)(2,1)} %param.11) | copy-start | bytes 3538948
  0.6 4.9 %copy-start.27 = (s32[144]{0:T(256)S(1)}, s32[144]{0:T(256)}, u32[]{:S(2)}) copy-start(s32[144]{0:T(256)} %param.9) | copy-start | bytes 1732
  0.7 5.0 %copy-start.4 = (bf16[1,144,4096]{2,1,0:T(8,128)(2,1)S(1)}, bf16[1,144,4096]{2,1,0:T(8,128)(2,1)}, u32[]{:S(2)}) copy-start(bf16[1,144,4096]{2,1,0:T(8,128)(2,1)} %param.8) | copy-start | bytes 3538948
  0.7 5.0 %copy-start.21 = (bf16[4096]{0:T(1024)(128)(2,1)S(1)}, bf16[4096]{0:T(1024)(128)(2,1)}, u32[]{:S(2)}) copy-start(bf16[4096]{0:T(1024)(128)(2,1)} %param.10) | copy-start | bytes 24580
  3.9 28.6 %collective-permute-start.1 = (bf16[4096,128]{1,0:T(8,128)(2,1)}, bf16[4096,128]{1,0:T(8,128)(2,1)}, u32[]{:S(2)}, u32[]{:S(2)}) collective-permute-start(bf16[4096,128]{1,0:T(8,128)(2,1)} %get-tuple-element.13), channel_id=1, source_target_pairs={{0,1},{1,0},{2,3},{3,2},{4,5},{5,4},{6,7},{7,6},{8,9},{9,8},{10,11... | collective-permute-start | bytes 3145736 | tf_op jit(solution)/shard_map/ppermute | solution.py:14
  5.6 1.7 copy-start.20
  5.6 1.6 copy-start.24
  6.1 0.6 copy-start.19
  7.3 6.7 %copy-start.18 = (bf16[1,4096]{1,0:T(2,128)(2,1)S(1)}, bf16[1,4096]{1,0:T(2,128)(2,1)}, u32[]{:S(2)}) copy-start(bf16[1,4096]{1,0:T(2,128)(2,1)} %param.13) | copy-start | bytes 24580
  7.3 6.7 %copy-start.1 = (bf16[1,144,4096]{2,1,0:T(8,128)(2,1)S(1)}, bf16[1,144,4096]{2,1,0:T(8,128)(2,1)}, u32[]{:S(2)}) copy-start(bf16[1,144,4096]{2,1,0:T(8,128)(2,1)} %param.12) | copy-start | bytes 3538948
  7.3 24.5 %collective-permute-start = (f32[2,144]{1,0:T(2,128)}, f32[2,144]{1,0:T(2,128)}, u32[]{:S(2)}, u32[]{:S(2)}) collective-permute-start(f32[2,144]{1,0:T(2,128)} %pad_maximum_fusion.1), channel_id=1, source_target_pairs={{0,1},{1,0},{2,3},{3,2},{4,5},{5,4},{6,7},{7,6},{8,9},{9,8},{10,11... | collective-permute-start | bytes 3464 | tf_op jit(solution)/shard_map/ppermute | solution.py:14
  12.6 40.5 %collective-permute-start.2 = (bf16[128,4096]{1,0:T(8,128)(2,1)}, bf16[128,4096]{1,0:T(8,128)(2,1)}, u32[]{:S(2)}, u32[]{:S(2)}) collective-permute-start(bf16[128,4096]{1,0:T(8,128)(2,1)} %get-tuple-element.15), channel_id=1, source_target_pairs={{0,1},{1,0},{2,3},{3,2},{4,5},{5,4},{6,7},{7,6},{8,9},{9,8},{10,11... | collective-permute-start | bytes 3145736 | tf_op jit(solution)/shard_map/ppermute | solution.py:14
  32.5 25.4 %copy-start.16 = (f32[1,144]{1,0:T(1,128)}, f32[1,144]{1,0:T(1,128)S(1)}, u32[]{:S(2)}) copy-start(f32[1,144]{1,0:T(1,128)S(1)} %get-tuple-element.21) | copy-start | bytes 1732
  32.5 3.3 %copy-start.5 = (bf16[1,144,4096]{2,1,0:T(8,128)(2,1)S(1)}, bf16[1,144,4096]{2,1,0:T(8,128)(2,1)}, u32[]{:S(2)}) copy-start(bf16[1,144,4096]{2,1,0:T(8,128)(2,1)} %param.8) | copy-start | bytes 3538948
  32.5 3.3 %copy-start.7 = (bf16[4096,128]{1,0:T(8,128)(2,1)S(1)}, bf16[4096,128]{1,0:T(8,128)(2,1)}, u32[]{:S(2)}) copy-start(bf16[4096,128]{1,0:T(8,128)(2,1)} %get-tuple-element.12) | copy-start | bytes 3145732
  32.5 3.3 %copy-start.22 = (bf16[4096]{0:T(1024)(128)(2,1)S(1)}, bf16[4096]{0:T(1024)(128)(2,1)}, u32[]{:S(2)}) copy-start(bf16[4096]{0:T(1024)(128)(2,1)} %param.10) | copy-start | bytes 24580
  32.5 3.3 %copy-start.25 = (pred[144]{0:T(512)(128)(4,1)S(1)}, pred[144]{0:T(512)(128)(4,1)}, u32[]{:S(2)}) copy-start(pred[144]{0:T(512)(128)(4,1)} %copy-done.24) | copy-start | bytes 436
  35.7 19.9 %copy-start.10 = (f32[1,144,256]{2,1,0:T(8,128)}, f32[1,144,256]{2,1,0:T(8,128)S(1)}, u32[]{:S(2)}) copy-start(f32[1,144,256]{2,1,0:T(8,128)S(1)} %fusion.30) | copy-start | bytes 442372
  35.8 17.3 %copy-start.8 = (bf16[128,4096]{1,0:T(8,128)(2,1)S(1)}, bf16[128,4096]{1,0:T(8,128)(2,1)}, u32[]{:S(2)}) copy-start(bf16[128,4096]{1,0:T(8,128)(2,1)} %get-tuple-element.14) | copy-start | bytes 3145732
  38.4 17.3 %copy-start.12 = (f32[1,144,256]{2,1,0:T(8,128)}, f32[1,144,256]{2,1,0:T(8,128)S(1)}, u32[]{:S(2)}) copy-start(f32[1,144,256]{2,1,0:T(8,128)S(1)} %fusion.33) | copy-start | bytes 442372
  55.7 0.8 copy-start.14
  56.5 12.9 %collective-permute-start.3 = (f32[3,144,256]{2,1,0:T(8,128)}, f32[3,144,256]{2,1,0:T(8,128)}, u32[]{:S(2)}, u32[]{:S(2)}) collective-permute-start(f32[3,144,256]{2,1,0:T(8,128)} %pad_maximum_fusion), channel_id=1, source_target_pairs={{0,1},{1,0},{2,3},{3,2},{4,5},{5,4},{6,7},{7,6},{8,9},{9,8},{10,11... | collective-permute-start | bytes 1327112 | tf_op jit(solution)/shard_map/ppermute | solution.py:14
  63.0 6.3 %copy-start.11 = (f32[1,144,256]{2,1,0:T(8,128)S(1)}, f32[1,144,256]{2,1,0:T(8,128)}, u32[]{:S(2)}) copy-start(f32[1,144,256]{2,1,0:T(8,128)} %copy-done.10) | copy-start | bytes 442372
  63.0 6.3 %copy-start.13 = (f32[1,144,256]{2,1,0:T(8,128)S(1)}, f32[1,144,256]{2,1,0:T(8,128)}, u32[]{:S(2)}) copy-start(f32[1,144,256]{2,1,0:T(8,128)} %copy-done.12) | copy-start | bytes 442372
  63.1 6.3 %copy-start.15 = (f32[1,144,256]{2,1,0:T(8,128)S(1)}, f32[1,144,256]{2,1,0:T(8,128)}, u32[]{:S(2)}) copy-start(f32[1,144,256]{2,1,0:T(8,128)} %copy-done.14) | copy-start | bytes 442372
  70.5 0.8 copy-start.3
  180.6 8.7 %copy-start.17 = (f32[1,144]{1,0:T(1,128)S(1)}, f32[1,144]{1,0:T(1,128)}, u32[]{:S(2)}) copy-start(f32[1,144]{1,0:T(1,128)} %copy-done.16) | copy-start | bytes 1732
  180.6 55.7 %all-to-all-start.1 = ((f32[8,2,256,128]{3,2,1,0:T(8,128)}), f32[8,2,256,128]{3,2,1,0:T(8,128)S(1)}, u32[]{:S(2)}, u32[]{:S(2)}) async-start(f32[8,2,256,128]{3,2,1,0:T(8,128)} %bitcast.108), calls=%async_computation.1 | async-start | bytes 4194304 | tf_op jit(solution)/shard_map/all_to_all | solution.py:127
  189.3 5.1 %copy-start.6 = (bf16[1,144,4096]{2,1,0:T(8,128)(2,1)S(1)}, bf16[1,144,4096]{2,1,0:T(8,128)(2,1)}, u32[]{:S(2)}) copy-start(bf16[1,144,4096]{2,1,0:T(8,128)(2,1)} %param.8) | copy-start | bytes 3538948
  189.3 5.1 %copy-start.9 = (bf16[128,4096]{1,0:T(8,128)(2,1)S(1)}, bf16[128,4096]{1,0:T(8,128)(2,1)}, u32[]{:S(2)}) copy-start(bf16[128,4096]{1,0:T(8,128)(2,1)} %get-tuple-element.14) | copy-start | bytes 3145732
  189.3 5.1 %copy-start.23 = (bf16[4096]{0:T(1024)(128)(2,1)S(1)}, bf16[4096]{0:T(1024)(128)(2,1)}, u32[]{:S(2)}) copy-start(bf16[4096]{0:T(1024)(128)(2,1)} %param.10) | copy-start | bytes 24580
  189.3 5.1 %copy-start.26 = (pred[144]{0:T(512)(128)(4,1)S(1)}, pred[144]{0:T(512)(128)(4,1)}, u32[]{:S(2)}) copy-start(pred[144]{0:T(512)(128)(4,1)} %copy-done.24) | copy-start | bytes 436
  192.9 7.1 %copy-start.2 = (bf16[1,144,4096]{2,1,0:T(8,128)(2,1)S(1)}, bf16[1,144,4096]{2,1,0:T(8,128)(2,1)}, u32[]{:S(2)}) copy-start(bf16[1,144,4096]{2,1,0:T(8,128)(2,1)} %param.12) | copy-start | bytes 3538948
  192.9 7.0 %collective-permute-start.5 = (f32[144]{0:T(256)S(1)}, f32[144]{0:T(256)S(1)}, u32[]{:S(2)}, u32[]{:S(2)}) collective-permute-start(f32[144]{0:T(256)S(1)} %get-tuple-element.22), channel_id=1, source_target_pairs={{0,1},{1,0},{2,3},{3,2},{4,5},{5,4},{6,7},{7,6},{8,9},{9,8},{10,11... | collective-permute-start | bytes 1736 | tf_op jit(solution)/shard_map/ppermute | solution.py:14
  198.0 42.5 %collective-permute-start.4 = (bf16[144,4096]{1,0:T(8,128)(2,1)}, bf16[144,4096]{1,0:T(8,128)(2,1)}, u32[]{:S(2)}, u32[]{:S(2)}) collective-permute-start(bf16[144,4096]{1,0:T(8,128)(2,1)} %fusion), channel_id=1, source_target_pairs={{0,2},{2,4},{4,6},{1,3},{3,5},{5,7},{8,10},{10,12},{12,14},{9,11},... | collective-permute-start | bytes 3538952 | tf_op jit(solution)/shard_map/ppermute | solution.py:10
  202.0 38.5 %collective-permute-start.6 = (bf16[144,4096]{1,0:T(8,128)(2,1)}, bf16[144,4096]{1,0:T(8,128)(2,1)S(1)}, u32[]{:S(2)}, u32[]{:S(2)}) collective-permute-start(bf16[144,4096]{1,0:T(8,128)(2,1)} %fusion.10), channel_id=1, source_target_pairs={{2,0},{4,2},{6,4},{3,1},{5,3},{7,5},{10,8},{12,10},{14,12},{11,9},... | collective-permute-start | bytes 3538952 | tf_op jit(solution)/shard_map/ppermute | solution.py:10
  236.4 16.4 %collective-permute-start.7 = (f32[2,256,128]{2,1,0:T(8,128)S(1)}, f32[2,256,128]{2,1,0:T(8,128)S(1)}, u32[]{:S(2)}, u32[]{:S(2)}) collective-permute-start(f32[2,256,128]{2,1,0:T(8,128)S(1)} %reduce_sum.49), channel_id=1, source_target_pairs={{1,128},{9,136},{17,144},{25,152},{33,160},{41,168},{49,176},{57,1... | collective-permute-start | bytes 786440 | tf_op jit(solution)/shard_map/ppermute | solution.py:137

commit v5 on v4

--- a/solution.py
+++ b/solution.py
@@ -30,6 +30,16 @@
     )
 
 
+def around_x(sections, step):
+    pairs = []
+    for section in range(sections):
+        for half in range(2):
+            x = half * 2 + section // 2
+            to = (x + step) % 4
+            pairs.append((section * 2 + half, ((to % 2) * 2 + section % 2) * 2 + to // 2))
+    return pairs
+
+
 def in_unit_order(own, received, first, axis):
     return jnp.where(
         first,
@@ -57,8 +67,12 @@
     down_theirs = lax.dynamic_slice_in_dim(down_local, (1 - half) * width, width, axis=0)
     up_mine = lax.dynamic_slice_in_dim(up_local, half * width, width, axis=1)
     up_theirs = lax.dynamic_slice_in_dim(up_local, (1 - half) * width, width, axis=1)
+    relay = around_x(lax.axis_size("section"), -1)
+    up_received = lax.ppermute(
+        lax.ppermute(up_theirs, ("section", "mp"), relay), ("section", "mp"), relay
+    )
     down_half = in_unit_order(down_mine, swapped(down_theirs, "mp"), first, 1)
-    up_half = in_unit_order(up_mine, swapped(up_theirs, "mp"), first, 0)
+    up_half = in_unit_order(up_mine, up_received, first, 0)
 
     input_values = inputs.astype(jnp.float32)
     saved_values = saved.astype(jnp.float32)

time: 258 us -> 279 us (1.081)
  waiting for transfers between devices: 80 us -> 107 us
    ppermute x0 -> x2, waiting for transfers between devices: none -> 20 us  [the longest x1 19.5 us: on_device(): lax.ppermute(lax.ppermute(up_theirs, ('section', 'mp'), relay), ('section...]
    ppermute x5 -> x4, waiting for transfers between devices: 37 us -> 43.5 us  [swapped(): return lax.ppermute(shard, axis, [(0, 1), (1, 0)])]
    ppermute x5 -> x4, starting transfers between devices: 7.9 us -> 5.04 us  [swapped(): return lax.ppermute(shard, axis, [(0, 1), (1, 0)])]
    unnamed x59 -> x63, local copies, waits for them, and re-layouts: 5.61 us -> 5.62 us
  transfers between devices with their start and end apart: 9 -> 10, of which waited for: 5 -> 6; matrix products, arithmetic and copies ran while one was open for 11% -> 9% of each run, Pallas kernels for 0% -> 0%
where the time goes in v5:
time: 279 us
  waiting for transfers between devices  107 us (38%)
  blocking collectives  95.5 us (34%)
  starting transfers between devices  23.6 us (8%)
  other arithmetic  17.7 us (6%)
  local copies, waits for them, and re-layouts  17.5 us (6%)
  matrix products  15.6 us (6%)
    all_to_all x1, blocking collectives, on_device(): lax.all_to_all(slots, 'dp', 0, 0, tiled=True, axis_index_groups=y_groups)  95.5 us
    ppermute x4, waiting for transfers between devices, swapped(): return lax.ppermute(shard, axis, [(0, 1), (1, 0)])  43.5 us
    all_to_all x1, waiting for transfers between devices, on_device(): lax.all_to_all(over_y.reshape(nz, 2, block, units), 'dp', 0, 0, tiled=Tru...  30.9 us
    ppermute x1, waiting for transfers between devices, on_device(): lax.ppermute(lax.ppermute(up_theirs, ('section', 'mp'), relay), ('section...  19.5 us
    ppermute x1, waiting for transfers between devices, on_device(): moved = lax.ppermute(summed, ('dp', 'mp'), pairs)  13 us
    all_to_all x1, starting transfers between devices, on_device(): lax.all_to_all(over_y.reshape(nz, 2, block, units), 'dp', 0, 0, tiled=Tru...  8.7 us
    unnamed x63, local copies, waits for them, and re-layouts  5.62 us
  transfers between devices with their start and end apart: 10, of which 6 were waited for; matrix products, arithmetic and copies ran while one was open for 9% of the time, Pallas kernels for 0%

profile of v5, /device:TPU:38, one launch (start us, length us, event | category | flops | bytes accessed | tf_op | source)
XLA Modules:
  0.0 278.5 jit_solution(14145185833724305520)
XLA Ops:
  0.6 3.2 %dynamic-slice_bitcast_fusion.1 = (bf16[128,4096]{1,0:T(8,128)(2,1)}, bf16[128,4096]{1,0:T(8,128)(2,1)}) fusion(bf16[1,128,8192]{2,1,0:T(8,128)(2,1)} %param.15, s32[]{:T(128)S(6)} %select_n.43, s32[]{:T(128)S(6)} %select_n.44), kind=kLoop, calls=%fused_computation.42 | loop fusion | bytes 4194312 | tf_op jit(solution)/shard_map/dynamic_slice | solution.py:68
  3.9 0.9 collective-permute-start.2
  4.8 0.0 copy-done.3
  4.8 1.5 dynamic-slice_bitcast_fusion.3
  6.3 1.1 collective-permute-start.1
  7.4 0.0 copy-done
  7.4 0.3 fusion.5
  7.7 0.0 copy-done.5
  7.8 0.5 fusion.14
  8.2 0.6 copy-done.19
  8.8 0.6 pad_maximum_fusion.1
  9.4 2.4 collective-permute-start
  11.8 0.7 mul.174
  12.6 0.9 stack.46
  13.5 38.2 %collective-permute-done = f32[2,144]{1,0:T(2,128)} collective-permute-done((f32[2,144]{1,0:T(2,128)}, f32[2,144]{1,0:T(2,128)}, u32[]{:S(2)}, u32[]{:S(2)}) %collective-permute-start) | collective-permute-done | bytes 1184 | tf_op jit(solution)/shard_map/ppermute | solution.py:14
  51.7 0.7 fusion.56
  52.4 0.5 collective-permute-done.2
  52.9 0.0 collective-permute-start.3
  52.9 0.0 collective-permute-done.1
  52.9 0.0 copy-start.6
  53.0 0.0 copy-start.22
  53.0 3.2 %fusion.30 = f32[1,144,256]{2,1,0:T(8,128)S(1)} fusion(bf16[1,144,4096]{2,1,0:T(8,128)(2,1)S(1)} %copy-done, f32[144]{0:T(256)S(1)} %bitcast.114, f32[4096]{0:T(1024)S(1)} %bitcast.110, bf16[4096,128]{1,0:T(8,128)(2,1)} %collective-permute-done.1, bf16[4096,128]{1,0:T(8,128)(2,1)} %get-tuple-element.12, pred[]{:T(512)S(6)} %eq.18), kind=kOutput, calls=%fused_computation.38 | convolution fusion | flops 313786368 | bytes 3441217 | tf_op jit(solution)/shard_map/dot_general | solution.py:94
  56.2 0.0 copy-start.8
  56.3 2.6 fusion.33
  58.8 19.5 %collective-permute-done.3 = bf16[128,4096]{1,0:T(8,128)(2,1)S(1)} collective-permute-done((bf16[128,4096]{1,0:T(8,128)(2,1)}, bf16[128,4096]{1,0:T(8,128)(2,1)S(1)}, u32[]{:S(2)}, u32[]{:S(2)}) %collective-permute-start.3) | collective-permute-done | bytes 1048608 | tf_op jit(solution)/shard_map/ppermute | solution.py:71
  78.4 1.0 fusion.36
  79.4 0.8 pad_maximum_fusion
  80.2 0.7 collective-permute-start.4
  80.9 0.4 fusion.13
  81.3 1.7 stack.45
  83.0 3.0 %maximum_bitcast_fusion = bf16[4,4,2,144,256]{4,0,1,3,2:T(4,128)(2,1)S(1)} fusion(bf16[1,144,4,4,256]{4,3,2,1,0:T(4,128)(2,1)S(1)} %stack.46, bf16[1,144,4,4,256]{4,3,2,1,0:T(4,128)(2,1)} %stack.45), kind=kLoop, calls=%fused_computation.23 | loop fusion | flops 1179648 | bytes 4718592 | tf_op jit(solution)/shard_map/transpose | solution.py:128
  86.1 0.8 copy.15
  86.9 5.3 %collective-permute-done.4 = f32[3,144,256]{2,1,0:T(8,128)} collective-permute-done((f32[3,144,256]{2,1,0:T(8,128)}, f32[3,144,256]{2,1,0:T(8,128)}, u32[]{:S(2)}, u32[]{:S(2)}) %collective-permute-start.4) | collective-permute-done | bytes 442400 | tf_op jit(solution)/shard_map/ppermute | solution.py:14
  92.2 1.1 fusion.57
  93.3 0.8 copy-done.4
  94.1 0.7 multiply_convert_fusion.1
  94.8 1.5 stack.48
  96.3 1.5 stack.49
  97.9 1.1 maximum_bitcast_fusion.1
  99.0 2.4 fusion.17
  101.5 95.5 %all_to_all.10 = f32[4,2,4,2,256,128]{5,4,3,2,1,0:T(8,128)} all-to-all(f32[4,2,4,2,256,128]{5,4,3,2,1,0:T(8,128)S(1)} %fusion.17), channel_id=1, replica_groups={{0,8,16,24},{32,40,48,56},{64,72,80,88},{96,104,112,120},{128,136,144,1..., dimensions={0} | all-to-all | bytes 16777216 | tf_op jit(solution)/shard_map/all_to_all | solution.py:138
  197.0 5.5 %reduce_sum.48 = f32[2,4,2,256,128]{4,3,2,1,0:T(8,128)} reduce(f32[4,2,4,2,256,128]{5,4,3,2,1,0:T(8,128)} %all_to_all.10, f32[]{:T(128)} %constant.45.clone.1), dimensions={0}, to_apply=%region_3.4 | reduce | flops 1572864 | bytes 10485764 | tf_op jit(solution)/shard_map/reduce_sum | solution.py:140
  202.6 8.7 %all-to-all-start.1 = ((f32[8,2,256,128]{3,2,1,0:T(8,128)}), f32[8,2,256,128]{3,2,1,0:T(8,128)S(1)}, u32[]{:S(2)}, u32[]{:S(2)}) async-start(f32[8,2,256,128]{3,2,1,0:T(8,128)} %bitcast.108), calls=%async_computation.1 | async-start | bytes 4194304 | tf_op jit(solution)/shard_map/all_to_all | solution.py:141
  211.3 0.0 copy-start.7
  211.3 0.0 copy-start.9
  211.3 0.0 copy-start.23
  211.3 3.6 %fusion.11 = (f32[144]{0:T(256)S(1)}, f32[144,4096]{1,0:T(8,128)S(1)}) fusion(bf16[1,144,4096]{2,1,0:T(8,128)(2,1)S(1)} %copy-done, f32[4096]{0:T(1024)S(1)} %bitcast.113, bf16[4096,128]{1,0:T(8,128)(2,1)} %collective-permute-done.1, bf16[4096,128]{1,0:T(8,128)(2,1)} %get-tuple-element.12, pred[]{:T(512)S(6)} %eq.18, f32[3,144,256]{2,1,0:T(8,128)} %copy-done.4), kind=kOutput, calls=%fused_computation.17 | convolution fusion | flops 314118016 | bytes 5947969 | tf_op jit(solution)/shard_map/dot_general | solution.py:28
  214.9 0.0 copy-start.2
  214.9 0.8 collective-permute-start.6
  215.7 2.9 %fusion = bf16[144,4096]{1,0:T(8,128)(2,1)} fusion(bf16[128,4096]{1,0:T(8,128)(2,1)S(1)} %copy-done.29, bf16[128,4096]{1,0:T(8,128)(2,1)S(1)} %copy-done.9, pred[]{:T(512)S(6)} %eq.18, f32[3,144,256]{2,1,0:T(8,128)} %copy-done.4, bf16[4096]{0:T(1024)(128)(2,1)S(1)} %copy-done.23, bf16[1,144,4096]{2,1,0:T(8,128)(2,1)S(1)} %copy-done.7, ...), kind=kOutput, calls=%fused_computation.2 | convolution fusion | flops 313970688 | bytes 4612241 | tf_op jit(solution)/shard_map/dot_general | solution.py:102
  218.6 1.9 collective-permute-start.5
  220.5 0.0 collective-permute-done.6
  220.5 2.0 fusion.10
  222.5 3.6 %collective-permute-start.7 = (bf16[144,4096]{1,0:T(8,128)(2,1)}, bf16[144,4096]{1,0:T(8,128)(2,1)S(1)}, u32[]{:S(2)}, u32[]{:S(2)}) collective-permute-start(bf16[144,4096]{1,0:T(8,128)(2,1)} %fusion.10), channel_id=1, source_target_pairs={{2,0},{4,2},{6,4},{3,1},{5,3},{7,5},{10,8},{12,10},{14,12},{11,9},... | collective-permute-start | bytes 3538952 | tf_op jit(solution)/shard_map/ppermute | solution.py:10
  226.2 30.9 %all-to-all-done.1 = f32[8,2,256,128]{3,2,1,0:T(8,128)S(1)} async-done(((f32[8,2,256,128]{3,2,1,0:T(8,128)}), f32[8,2,256,128]{3,2,1,0:T(8,128)S(1)}, u32[]{:S(2)}, u32[]{:S(2)}) %all-to-all-start.1) | async-done | bytes 2097184 | tf_op jit(solution)/shard_map/all_to_all | solution.py:141
  257.1 0.1 reduce_sum.49
  257.2 3.4 %collective-permute-start.8 = (f32[2,256,128]{2,1,0:T(8,128)S(1)}, f32[2,256,128]{2,1,0:T(8,128)S(1)}, u32[]{:S(2)}, u32[]{:S(2)}) collective-permute-start(f32[2,256,128]{2,1,0:T(8,128)S(1)} %reduce_sum.49), channel_id=1, source_target_pairs={{1,128},{9,136},{17,144},{25,152},{33,160},{41,168},{49,176},{57,1... | collective-permute-start | bytes 786440 | tf_op jit(solution)/shard_map/ppermute | solution.py:151
  260.7 0.0 collective-permute-done.5
  260.7 0.0 collective-permute-done.7
  260.7 13.0 %collective-permute-done.8 = f32[2,256,128]{2,1,0:T(8,128)S(1)} collective-permute-done((f32[2,256,128]{2,1,0:T(8,128)S(1)}, f32[2,256,128]{2,1,0:T(8,128)S(1)}, u32[]{:S(2)}, u32[]{:S(2)}) %collective-permute-start.8) | collective-permute-done | bytes 262176 | tf_op jit(solution)/shard_map/ppermute | solution.py:151
  273.7 0.7 slice_bitcast_fusion.1
  274.4 0.8 copy.17
  275.1 2.4 copy.20
  277.5 1.0 copy.21
  (54 shorter events, 0.2 us)
Async XLA Ops:
  0.6 4.2 %copy-start.3 = (bf16[1,8192,128]{2,1,0:T(8,128)(2,1)S(1)}, bf16[1,8192,128]{2,1,0:T(8,128)(2,1)}, u32[]{:S(2)}) copy-start(bf16[1,8192,128]{2,1,0:T(8,128)(2,1)} %param.14) | copy-start | bytes 6291460
  3.9 3.5 %copy-start = (bf16[1,144,4096]{2,1,0:T(8,128)(2,1)S(1)}, bf16[1,144,4096]{2,1,0:T(8,128)(2,1)}, u32[]{:S(2)}) copy-start(bf16[1,144,4096]{2,1,0:T(8,128)(2,1)} %param.11) | copy-start | bytes 3538948
  3.9 3.8 %copy-start.27 = (s32[144]{0:T(256)S(1)}, s32[144]{0:T(256)}, u32[]{:S(2)}) copy-start(s32[144]{0:T(256)} %param.9) | copy-start | bytes 1732
  3.9 3.9 %copy-start.5 = (bf16[1,144,4096]{2,1,0:T(8,128)(2,1)S(1)}, bf16[1,144,4096]{2,1,0:T(8,128)(2,1)}, u32[]{:S(2)}) copy-start(bf16[1,144,4096]{2,1,0:T(8,128)(2,1)} %param.8) | copy-start | bytes 3538948
  3.9 3.9 %copy-start.21 = (bf16[4096]{0:T(1024)(128)(2,1)S(1)}, bf16[4096]{0:T(1024)(128)(2,1)}, u32[]{:S(2)}) copy-start(bf16[4096]{0:T(1024)(128)(2,1)} %param.10) | copy-start | bytes 24580
  3.9 49.0 %collective-permute-start.2 = (bf16[128,4096]{1,0:T(8,128)(2,1)}, bf16[128,4096]{1,0:T(8,128)(2,1)}, u32[]{:S(2)}, u32[]{:S(2)}) collective-permute-start(bf16[128,4096]{1,0:T(8,128)(2,1)} %get-tuple-element.15), channel_id=1, source_target_pairs={{0,5},{1,4},{2,7},{3,6},{4,0},{5,1},{6,2},{7,3},{8,13},{9,12},{10,... | collective-permute-start | bytes 3145736 | tf_op jit(solution)/shard_map/ppermute | solution.py:72
  6.3 6.3 %copy-start.1 = (bf16[1,144,4096]{2,1,0:T(8,128)(2,1)S(1)}, bf16[1,144,4096]{2,1,0:T(8,128)(2,1)}, u32[]{:S(2)}) copy-start(bf16[1,144,4096]{2,1,0:T(8,128)(2,1)} %param.12) | copy-start | bytes 3538948
  6.3 46.7 %collective-permute-start.1 = (bf16[4096,128]{1,0:T(8,128)(2,1)}, bf16[4096,128]{1,0:T(8,128)(2,1)}, u32[]{:S(2)}, u32[]{:S(2)}) collective-permute-start(bf16[4096,128]{1,0:T(8,128)(2,1)} %get-tuple-element.13), channel_id=1, source_target_pairs={{0,1},{1,0},{2,3},{3,2},{4,5},{5,4},{6,7},{7,6},{8,9},{9,8},{10,11... | collective-permute-start | bytes 3145736 | tf_op jit(solution)/shard_map/ppermute | solution.py:14
  7.7 4.1 %copy-start.20 = (f32[144]{0:T(256)}, f32[144]{0:T(256)S(1)}, u32[]{:S(2)}) copy-start(f32[144]{0:T(256)S(1)} %fusion.5) | copy-start | bytes 1732
  7.8 1.7 copy-start.24
  8.2 0.6 copy-start.19
  9.4 42.3 %collective-permute-start = (f32[2,144]{1,0:T(2,128)}, f32[2,144]{1,0:T(2,128)}, u32[]{:S(2)}, u32[]{:S(2)}) collective-permute-start(f32[2,144]{1,0:T(2,128)} %pad_maximum_fusion.1), channel_id=1, source_target_pairs={{0,1},{1,0},{2,3},{3,2},{4,5},{5,4},{6,7},{7,6},{8,9},{9,8},{10,11... | collective-permute-start | bytes 3464 | tf_op jit(solution)/shard_map/ppermute | solution.py:14
  52.9 25.5 %collective-permute-start.3 = (bf16[128,4096]{1,0:T(8,128)(2,1)}, bf16[128,4096]{1,0:T(8,128)(2,1)S(1)}, u32[]{:S(2)}, u32[]{:S(2)}) collective-permute-start(bf16[128,4096]{1,0:T(8,128)(2,1)} %collective-permute-done.2), channel_id=1, source_target_pairs={{0,5},{1,4},{2,7},{3,6},{4,0},{5,1},{6,2},{7,3},{8,13},{9,12},{10,... | collective-permute-start | bytes 3145736 | tf_op jit(solution)/shard_map/ppermute | solution.py:71
  52.9 28.0 %copy-start.17 = (f32[1,144]{1,0:T(1,128)}, f32[1,144]{1,0:T(1,128)S(1)}, u32[]{:S(2)}) copy-start(f32[1,144]{1,0:T(1,128)S(1)} %get-tuple-element.21) | copy-start | bytes 1732
  52.9 3.3 %copy-start.6 = (bf16[1,144,4096]{2,1,0:T(8,128)(2,1)S(1)}, bf16[1,144,4096]{2,1,0:T(8,128)(2,1)}, u32[]{:S(2)}) copy-start(bf16[1,144,4096]{2,1,0:T(8,128)(2,1)} %param.8) | copy-start | bytes 3538948
  53.0 3.3 %copy-start.10 = (bf16[4096,128]{1,0:T(8,128)(2,1)S(1)}, bf16[4096,128]{1,0:T(8,128)(2,1)}, u32[]{:S(2)}) copy-start(bf16[4096,128]{1,0:T(8,128)(2,1)} %get-tuple-element.12) | copy-start | bytes 3145732
  53.0 3.3 %copy-start.22 = (bf16[4096]{0:T(1024)(128)(2,1)S(1)}, bf16[4096]{0:T(1024)(128)(2,1)}, u32[]{:S(2)}) copy-start(bf16[4096]{0:T(1024)(128)(2,1)} %param.10) | copy-start | bytes 24580
  53.0 3.3 %copy-start.25 = (pred[144]{0:T(512)(128)(4,1)S(1)}, pred[144]{0:T(512)(128)(4,1)}, u32[]{:S(2)}) copy-start(pred[144]{0:T(512)(128)(4,1)} %copy-done.24) | copy-start | bytes 436
  56.2 23.2 %copy-start.11 = (f32[1,144,256]{2,1,0:T(8,128)}, f32[1,144,256]{2,1,0:T(8,128)S(1)}, u32[]{:S(2)}) copy-start(f32[1,144,256]{2,1,0:T(8,128)S(1)} %fusion.30) | copy-start | bytes 442372
  56.2 22.1 %copy-start.8 = (bf16[128,4096]{1,0:T(8,128)(2,1)S(1)}, bf16[128,4096]{1,0:T(8,128)(2,1)}, u32[]{:S(2)}) copy-start(bf16[128,4096]{1,0:T(8,128)(2,1)} %get-tuple-element.14) | copy-start | bytes 3145732
  58.8 20.6 %copy-start.13 = (f32[1,144,256]{2,1,0:T(8,128)}, f32[1,144,256]{2,1,0:T(8,128)S(1)}, u32[]{:S(2)}) copy-start(f32[1,144,256]{2,1,0:T(8,128)S(1)} %fusion.33) | copy-start | bytes 442372
  78.4 1.0 copy-start.28
  79.4 0.8 copy-start.15
  80.2 12.0 %collective-permute-start.4 = (f32[3,144,256]{2,1,0:T(8,128)}, f32[3,144,256]{2,1,0:T(8,128)}, u32[]{:S(2)}, u32[]{:S(2)}) collective-permute-start(f32[3,144,256]{2,1,0:T(8,128)} %pad_maximum_fusion), channel_id=1, source_target_pairs={{0,1},{1,0},{2,3},{3,2},{4,5},{5,4},{6,7},{7,6},{8,9},{9,8},{10,11... | collective-permute-start | bytes 1327112 | tf_op jit(solution)/shard_map/ppermute | solution.py:14
  86.1 6.2 %copy-start.12 = (f32[1,144,256]{2,1,0:T(8,128)S(1)}, f32[1,144,256]{2,1,0:T(8,128)}, u32[]{:S(2)}) copy-start(f32[1,144,256]{2,1,0:T(8,128)} %copy-done.11) | copy-start | bytes 442372
  86.1 6.2 %copy-start.14 = (f32[1,144,256]{2,1,0:T(8,128)S(1)}, f32[1,144,256]{2,1,0:T(8,128)}, u32[]{:S(2)}) copy-start(f32[1,144,256]{2,1,0:T(8,128)} %copy-done.13) | copy-start | bytes 442372
  86.1 6.2 %copy-start.16 = (f32[1,144,256]{2,1,0:T(8,128)S(1)}, f32[1,144,256]{2,1,0:T(8,128)}, u32[]{:S(2)}) copy-start(f32[1,144,256]{2,1,0:T(8,128)} %copy-done.15) | copy-start | bytes 442372
  93.3 0.8 copy-start.4
  202.6 8.7 %copy-start.18 = (f32[1,144]{1,0:T(1,128)S(1)}, f32[1,144]{1,0:T(1,128)}, u32[]{:S(2)}) copy-start(f32[1,144]{1,0:T(1,128)} %copy-done.17) | copy-start | bytes 1732
  202.6 54.6 %all-to-all-start.1 = ((f32[8,2,256,128]{3,2,1,0:T(8,128)}), f32[8,2,256,128]{3,2,1,0:T(8,128)S(1)}, u32[]{:S(2)}, u32[]{:S(2)}) async-start(f32[8,2,256,128]{3,2,1,0:T(8,128)} %bitcast.108), calls=%async_computation.1 | async-start | bytes 4194304 | tf_op jit(solution)/shard_map/all_to_all | solution.py:141
  211.3 4.4 %copy-start.7 = (bf16[1,144,4096]{2,1,0:T(8,128)(2,1)S(1)}, bf16[1,144,4096]{2,1,0:T(8,128)(2,1)}, u32[]{:S(2)}) copy-start(bf16[1,144,4096]{2,1,0:T(8,128)(2,1)} %param.8) | copy-start | bytes 3538948
  211.3 4.4 %copy-start.9 = (bf16[128,4096]{1,0:T(8,128)(2,1)S(1)}, bf16[128,4096]{1,0:T(8,128)(2,1)}, u32[]{:S(2)}) copy-start(bf16[128,4096]{1,0:T(8,128)(2,1)} %get-tuple-element.14) | copy-start | bytes 3145732
  211.3 4.4 %copy-start.23 = (bf16[4096]{0:T(1024)(128)(2,1)S(1)}, bf16[4096]{0:T(1024)(128)(2,1)}, u32[]{:S(2)}) copy-start(bf16[4096]{0:T(1024)(128)(2,1)} %param.10) | copy-start | bytes 24580
  211.3 4.4 %copy-start.26 = (pred[144]{0:T(512)(128)(4,1)S(1)}, pred[144]{0:T(512)(128)(4,1)}, u32[]{:S(2)}) copy-start(pred[144]{0:T(512)(128)(4,1)} %copy-done.24) | copy-start | bytes 436
  211.3 4.4 %copy-start.29 = (bf16[128,4096]{1,0:T(8,128)(2,1)S(1)}, bf16[128,4096]{1,0:T(8,128)(2,1)}, u32[]{:S(2)}) copy-start(bf16[128,4096]{1,0:T(8,128)(2,1)} %copy-done.28) | copy-start | bytes 3145732
  214.9 5.6 %copy-start.2 = (bf16[1,144,4096]{2,1,0:T(8,128)(2,1)S(1)}, bf16[1,144,4096]{2,1,0:T(8,128)(2,1)}, u32[]{:S(2)}) copy-start(bf16[1,144,4096]{2,1,0:T(8,128)(2,1)} %param.12) | copy-start | bytes 3538948
  214.9 5.6 %collective-permute-start.6 = (f32[144]{0:T(256)S(1)}, f32[144]{0:T(256)S(1)}, u32[]{:S(2)}, u32[]{:S(2)}) collective-permute-start(f32[144]{0:T(256)S(1)} %get-tuple-element.22), channel_id=1, source_target_pairs={{0,1},{1,0},{2,3},{3,2},{4,5},{5,4},{6,7},{7,6},{8,9},{9,8},{10,11... | collective-permute-start | bytes 1736 | tf_op jit(solution)/shard_map/ppermute | solution.py:14
  218.6 42.1 %collective-permute-start.5 = (bf16[144,4096]{1,0:T(8,128)(2,1)}, bf16[144,4096]{1,0:T(8,128)(2,1)}, u32[]{:S(2)}, u32[]{:S(2)}) collective-permute-start(bf16[144,4096]{1,0:T(8,128)(2,1)} %fusion), channel_id=1, source_target_pairs={{0,2},{2,4},{4,6},{1,3},{3,5},{5,7},{8,10},{10,12},{12,14},{9,11},... | collective-permute-start | bytes 3538952 | tf_op jit(solution)/shard_map/ppermute | solution.py:10
  222.5 38.1 %collective-permute-start.7 = (bf16[144,4096]{1,0:T(8,128)(2,1)}, bf16[144,4096]{1,0:T(8,128)(2,1)S(1)}, u32[]{:S(2)}, u32[]{:S(2)}) collective-permute-start(bf16[144,4096]{1,0:T(8,128)(2,1)} %fusion.10), channel_id=1, source_target_pairs={{2,0},{4,2},{6,4},{3,1},{5,3},{7,5},{10,8},{12,10},{14,12},{11,9},... | collective-permute-start | bytes 3538952 | tf_op jit(solution)/shard_map/ppermute | solution.py:10
  257.2 16.4 %collective-permute-start.8 = (f32[2,256,128]{2,1,0:T(8,128)S(1)}, f32[2,256,128]{2,1,0:T(8,128)S(1)}, u32[]{:S(2)}, u32[]{:S(2)}) collective-permute-start(f32[2,256,128]{2,1,0:T(8,128)S(1)} %reduce_sum.49), channel_id=1, source_target_pairs={{1,128},{9,136},{17,144},{25,152},{33,160},{41,168},{49,176},{57,1... | collective-permute-start | bytes 786440 | tf_op jit(solution)/shard_map/ppermute | solution.py:151

commit v6 on v4

--- a/solution.py
+++ b/solution.py
@@ -73,17 +73,17 @@
     normed = (input_values * scale * gain_row).astype(jnp.bfloat16)
     saved_normed = (saved_values * saved_scale * gain_row).astype(jnp.bfloat16)
 
-    partials = pair_sum(
+    down_partials = pair_sum(
         jnp.stack(
             [
                 jnp.dot(normed, down_half, preferred_element_type=jnp.float32),
                 jnp.dot(saved_normed, down_half, preferred_element_type=jnp.float32),
-                contract_cols(upstream, up_half),
             ]
         ),
         "mp",
     )
-    hidden_pre, saved_pre, hidden_grad = partials[0], partials[1], partials[2]
+    hidden_pre, saved_pre = down_partials[0], down_partials[1]
+    hidden_grad = pair_sum(contract_cols(upstream, up_half), "mp")
     hidden = jax.nn.silu(hidden_pre).astype(jnp.bfloat16)
     branch = jnp.dot(hidden, up_half, preferred_element_type=jnp.float32)
     output = (input_values + branch).astype(jnp.bfloat16)

time: 258 us -> 252 us (0.977)
  waiting for transfers between devices: 80 us -> 68.8 us
  starting transfers between devices: 26.2 us -> 32.4 us
  other arithmetic: 17 us -> 20.8 us
  local copies, waits for them, and re-layouts: 19.1 us -> 16.3 us
    ppermute x5 -> x6, waiting for transfers between devices: 37 us -> 31 us  [swapped(): return lax.ppermute(shard, axis, [(0, 1), (1, 0)])]
    ppermute x5 -> x6, starting transfers between devices: 7.9 us -> 11.5 us  [swapped(): return lax.ppermute(shard, axis, [(0, 1), (1, 0)])]
    all_to_all x1, waiting for transfers between devices: 30.6 us -> 28 us  [on_device(): lax.all_to_all(over_y.reshape(nz, 2, block, units), 'dp', 0, 0, tiled=Tru...]
    unnamed x59 -> x55, local copies, waits for them, and re-layouts: 5.61 us -> 6.09 us
  transfers between devices with their start and end apart: 9 -> 10, of which waited for: 5 -> 5; matrix products, arithmetic and copies ran while one was open for 11% -> 12% of each run, Pallas kernels for 0% -> 0%
where the time goes in v6:
time: 252 us
  blocking collectives  94.6 us (38%)
  waiting for transfers between devices  68.8 us (27%)
  starting transfers between devices  32.4 us (13%)
  other arithmetic  20.8 us (8%)
  matrix products  17.8 us (7%)
  local copies, waits for them, and re-layouts  16.3 us (6%)
    all_to_all x1, blocking collectives, on_device(): lax.all_to_all(slots, 'dp', 0, 0, tiled=True, axis_index_groups=y_groups)  94.6 us
    ppermute x6, waiting for transfers between devices, swapped(): return lax.ppermute(shard, axis, [(0, 1), (1, 0)])  31 us
    all_to_all x1, waiting for transfers between devices, on_device(): lax.all_to_all(over_y.reshape(nz, 2, block, units), 'dp', 0, 0, tiled=Tru...  28 us
    ppermute x6, starting transfers between devices, swapped(): return lax.ppermute(shard, axis, [(0, 1), (1, 0)])  11.5 us
    ppermute x1, waiting for transfers between devices, on_device(): moved = lax.ppermute(summed, ('dp', 'mp'), pairs)  9.8 us
    all_to_all x1, starting transfers between devices, on_device(): lax.all_to_all(over_y.reshape(nz, 2, block, units), 'dp', 0, 0, tiled=Tru...  8.7 us
    dot_general x2, matrix products, contract_cols(): lax.dot_general(left, right, (((1,), (1,)), ((), ())), preferred_element_...  6.75 us
    ppermute x1, starting transfers between devices, on_device(): moved = lax.ppermute(summed, ('dp', 'mp'), pairs)  6.67 us
  transfers between devices with their start and end apart: 10, of which 5 were waited for; matrix products, arithmetic and copies ran while one was open for 12% of the time, Pallas kernels for 0%

profile of v6, /device:TPU:38, one launch (start us, length us, event | category | flops | bytes accessed | tf_op | source)
XLA Modules:
  0.0 251.7 jit_solution(4959537084474058335)
XLA Ops:
  0.6 1.7 fusion.5
  2.4 0.7 compare_or_fusion
  3.1 1.8 fusion.14
  4.8 0.6 copy-done.18
  5.4 0.6 pad_maximum_fusion.1
  6.0 1.4 collective-permute-start
  7.4 1.6 dynamic-slice_bitcast_fusion.3
  9.0 2.1 collective-permute-start.1
  11.1 1.4 dynamic-slice_bitcast_fusion.1
  12.5 1.4 collective-permute-start.3
  14.0 0.9 stack.42
  14.9 0.0 collective-permute-done
  14.9 0.7 fusion.53
  15.6 0.6 fusion.49
  16.2 0.6 copy-done.14
  16.8 0.4 fusion.13
  17.1 1.7 stack.41
  18.9 3.0 %maximum_bitcast_fusion = bf16[4,4,2,144,256]{4,0,1,3,2:T(4,128)(2,1)S(1)} fusion(bf16[1,144,4,4,256]{4,3,2,1,0:T(4,128)(2,1)S(1)} %stack.42, bf16[1,144,4,4,256]{4,3,2,1,0:T(4,128)(2,1)} %stack.41), kind=kLoop, calls=%fused_computation.23 | loop fusion | flops 1179648 | bytes 4718592 | tf_op jit(solution)/shard_map/transpose | solution.py:114
  21.9 0.8 copy.15
  22.7 14.1 %collective-permute-done.1 = bf16[4096,128]{1,0:T(8,128)(2,1)} collective-permute-done((bf16[4096,128]{1,0:T(8,128)(2,1)}, bf16[4096,128]{1,0:T(8,128)(2,1)}, u32[]{:S(2)}, u32[]{:S(2)}) %collective-permute-start.1) | collective-permute-done | bytes 1048608 | tf_op jit(solution)/shard_map/ppermute | solution.py:14
  36.8 0.0 copy-start.25
  36.9 2.5 fusion.30
  39.4 0.0 copy-start.2
  39.4 0.0 copy-start.10
  39.4 2.6 %fusion.33 = f32[1,144,256]{2,1,0:T(8,128)S(1)} fusion(f32[4096]{0:T(1024)S(1)} %bitcast.101, f32[144]{0:T(256)S(1)} %bitcast.111, bf16[1,144,4096]{2,1,0:T(8,128)(2,1)S(1)} %copy-done.8, pred[144]{0:T(512)(128)(4,1)S(1)} %copy-done.23, bf16[4096]{0:T(1024)(128)(2,1)S(1)} %copy-done.20, bf16[4096,128]{1,0:T(8,128)(2,1)} %collective-permute-done.1, ...), kind=kOutput, calls=%fused_computation.39 | convolution fusion | flops 314376192 | bytes 3449553 | tf_op jit(solution)/shard_map/dot_general | solution.py:79
  42.0 2.2 collective-permute-start.2
  44.3 15.0 %collective-permute-done.3 = bf16[128,4096]{1,0:T(8,128)(2,1)} collective-permute-done((bf16[128,4096]{1,0:T(8,128)(2,1)}, bf16[128,4096]{1,0:T(8,128)(2,1)}, u32[]{:S(2)}, u32[]{:S(2)}) %collective-permute-start.3) | collective-permute-done | bytes 1048608 | tf_op jit(solution)/shard_map/ppermute | solution.py:14
  59.3 3.1 %fusion.36 = f32[144,256]{1,0:T(8,128)} fusion(bf16[1,144,4096]{2,1,0:T(8,128)(2,1)S(1)} %copy-done.2, bf16[128,4096]{1,0:T(8,128)(2,1)} %collective-permute-done.3, bf16[128,4096]{1,0:T(8,128)(2,1)S(1)} %copy-done.10, pred[]{:T(512)S(6)} %eq.18), kind=kOutput, calls=%fused_computation.40 | convolution fusion | flops 311427072 | bytes 3424257 | tf_op jit(solution)/shard_map/dot_general | solution.py:28
  62.4 2.1 collective-permute-start.5
  64.6 0.0 collective-permute-done.2
  64.6 0.0 copy-start.6
  64.6 0.7 copy-done.6
  65.3 0.7 multiply_convert_fusion
  66.0 1.5 stack.45
  67.5 1.9 collective-permute-done.5
  69.4 1.7 fusion.44
  71.2 1.5 stack.44
  72.7 1.1 maximum_bitcast_fusion.1
  73.9 2.4 fusion.17
  76.3 94.6 %all_to_all.10 = f32[4,2,4,2,256,128]{5,4,3,2,1,0:T(8,128)} all-to-all(f32[4,2,4,2,256,128]{5,4,3,2,1,0:T(8,128)S(1)} %fusion.17), channel_id=1, replica_groups={{0,8,16,24},{32,40,48,56},{64,72,80,88},{96,104,112,120},{128,136,144,1..., dimensions={0} | all-to-all | bytes 16777216 | tf_op jit(solution)/shard_map/all_to_all | solution.py:124
  170.9 5.6 %reduce_sum.48 = f32[2,4,2,256,128]{4,3,2,1,0:T(8,128)} reduce(f32[4,2,4,2,256,128]{5,4,3,2,1,0:T(8,128)} %all_to_all.10, f32[]{:T(128)} %constant.45.clone.1), dimensions={0}, to_apply=%region_3.4 | reduce | flops 1572864 | bytes 10485764 | tf_op jit(solution)/shard_map/reduce_sum | solution.py:126
  176.5 8.7 %all-to-all-start.1 = ((f32[8,2,256,128]{3,2,1,0:T(8,128)}), f32[8,2,256,128]{3,2,1,0:T(8,128)S(1)}, u32[]{:S(2)}, u32[]{:S(2)}) async-start(f32[8,2,256,128]{3,2,1,0:T(8,128)} %bitcast.97), calls=%async_computation.1 | async-start | bytes 4194304 | tf_op jit(solution)/shard_map/all_to_all | solution.py:127
  185.2 0.0 copy-start.7
  185.2 0.0 copy-start.9
  185.2 0.0 copy-start.11
  185.2 0.0 copy-start.21
  185.3 3.6 %fusion.11 = (f32[144]{0:T(256)S(1)}, f32[144,4096]{1,0:T(8,128)S(1)}) fusion(bf16[1,144,4096]{2,1,0:T(8,128)(2,1)S(1)} %copy-done, f32[4096]{0:T(1024)S(1)} %bitcast.102, bf16[144,256]{1,0:T(8,128)(2,1)S(1)} %copy-done.13, bf16[4096,128]{1,0:T(8,128)(2,1)} %collective-permute-done.1, bf16[4096,128]{1,0:T(8,128)(2,1)} %get-tuple-element.12, pred[]{:T(512)S(6)} %eq.18), kind=kOutput, calls=%fused_computation.17 | convolution fusion | flops 313786240 | bytes 5726785 | tf_op jit(solution)/shard_map/dot_general | solution.py:28
  188.9 0.0 copy-start.3
  188.9 2.2 collective-permute-start.6
  191.1 3.5 %fusion = bf16[144,4096]{1,0:T(8,128)(2,1)} fusion(bf16[128,4096]{1,0:T(8,128)(2,1)} %collective-permute-done.3, bf16[128,4096]{1,0:T(8,128)(2,1)S(1)} %copy-done.11, pred[]{:T(512)S(6)} %eq.18, f32[2,144,256]{2,1,0:T(8,128)S(1)} %copy-done.7, bf16[4096]{0:T(1024)(128)(2,1)S(1)} %copy-done.21, bf16[1,144,4096]{2,1,0:T(8,128)(2,1)S(1)} %copy-done.9, ...), kind=kOutput, calls=%fused_computation.2 | convolution fusion | flops 313970688 | bytes 4612609 | tf_op jit(solution)/shard_map/dot_general | solution.py:88
  194.6 1.9 collective-permute-start.4
  196.6 0.0 collective-permute-done.6
  196.6 2.0 fusion.10
  198.6 3.6 %collective-permute-start.7 = (bf16[144,4096]{1,0:T(8,128)(2,1)}, bf16[144,4096]{1,0:T(8,128)(2,1)S(1)}, u32[]{:S(2)}, u32[]{:S(2)}) collective-permute-start(bf16[144,4096]{1,0:T(8,128)(2,1)} %fusion.10), channel_id=1, source_target_pairs={{2,0},{4,2},{6,4},{3,1},{5,3},{7,5},{10,8},{12,10},{14,12},{11,9},... | collective-permute-start | bytes 3538952 | tf_op jit(solution)/shard_map/ppermute | solution.py:10
  202.2 28.0 %all-to-all-done.1 = f32[8,2,256,128]{3,2,1,0:T(8,128)S(1)} async-done(((f32[8,2,256,128]{3,2,1,0:T(8,128)}), f32[8,2,256,128]{3,2,1,0:T(8,128)S(1)}, u32[]{:S(2)}, u32[]{:S(2)}) %all-to-all-start.1) | async-done | bytes 2097184 | tf_op jit(solution)/shard_map/all_to_all | solution.py:127
  230.3 0.1 reduce_sum.49
  230.4 6.7 %collective-permute-start.8 = (f32[2,256,128]{2,1,0:T(8,128)S(1)}, f32[2,256,128]{2,1,0:T(8,128)S(1)}, u32[]{:S(2)}, u32[]{:S(2)}) collective-permute-start(f32[2,256,128]{2,1,0:T(8,128)S(1)} %reduce_sum.49), channel_id=1, source_target_pairs={{1,128},{9,136},{17,144},{25,152},{33,160},{41,168},{49,176},{57,1... | collective-permute-start | bytes 786440 | tf_op jit(solution)/shard_map/ppermute | solution.py:137
  237.1 0.0 collective-permute-done.4
  237.1 0.0 collective-permute-done.7
  237.1 9.8 %collective-permute-done.8 = f32[2,256,128]{2,1,0:T(8,128)S(1)} collective-permute-done((f32[2,256,128]{2,1,0:T(8,128)S(1)}, f32[2,256,128]{2,1,0:T(8,128)S(1)}, u32[]{:S(2)}, u32[]{:S(2)}) %collective-permute-start.8) | collective-permute-done | bytes 262176 | tf_op jit(solution)/shard_map/ppermute | solution.py:137
  246.9 0.7 slice_bitcast_fusion.1
  247.6 0.8 copy.17
  248.4 2.4 copy.20
  250.7 1.0 copy.21
  (47 shorter events, 0.2 us)
Async XLA Ops:
  0.6 6.8 %copy-start.4 = (bf16[1,8192,128]{2,1,0:T(8,128)(2,1)S(1)}, bf16[1,8192,128]{2,1,0:T(8,128)(2,1)}, u32[]{:S(2)}) copy-start(bf16[1,8192,128]{2,1,0:T(8,128)(2,1)} %param.14) | copy-start | bytes 6291460
  2.4 3.6 %copy-start.19 = (f32[144]{0:T(256)}, f32[144]{0:T(256)S(1)}, u32[]{:S(2)}) copy-start(f32[144]{0:T(256)S(1)} %fusion.5) | copy-start | bytes 1732
  3.1 2.9 %copy-start.22 = (pred[144]{0:T(512)(128)(4,1)}, pred[144]{0:T(512)(128)(4,1)S(1)}, u32[]{:S(2)}) copy-start(pred[144]{0:T(512)(128)(4,1)S(1)} %compare_or_fusion) | copy-start | bytes 436
  4.8 0.6 copy-start.18
  6.0 8.9 %collective-permute-start = (f32[2,144]{1,0:T(2,128)}, f32[2,144]{1,0:T(2,128)}, u32[]{:S(2)}, u32[]{:S(2)}) collective-permute-start(f32[2,144]{1,0:T(2,128)} %pad_maximum_fusion.1), channel_id=1, source_target_pairs={{0,1},{1,0},{2,3},{3,2},{4,5},{5,4},{6,7},{7,6},{8,9},{9,8},{10,11... | collective-permute-start | bytes 3464 | tf_op jit(solution)/shard_map/ppermute | solution.py:14
  7.4 3.7 %copy-start.5 = (bf16[1,128,8192]{2,1,0:T(8,128)(2,1)S(1)}, bf16[1,128,8192]{2,1,0:T(8,128)(2,1)}, u32[]{:S(2)}) copy-start(bf16[1,128,8192]{2,1,0:T(8,128)(2,1)} %param.15) | copy-start | bytes 6291460
  9.0 5.0 %copy-start.17 = (bf16[1,4096]{1,0:T(2,128)(2,1)S(1)}, bf16[1,4096]{1,0:T(2,128)(2,1)}, u32[]{:S(2)}) copy-start(bf16[1,4096]{1,0:T(2,128)(2,1)} %param.13) | copy-start | bytes 24580
  9.0 5.0 %copy-start.1 = (bf16[1,144,4096]{2,1,0:T(8,128)(2,1)S(1)}, bf16[1,144,4096]{2,1,0:T(8,128)(2,1)}, u32[]{:S(2)}) copy-start(bf16[1,144,4096]{2,1,0:T(8,128)(2,1)} %param.12) | copy-start | bytes 3538948
  9.0 27.8 %collective-permute-start.1 = (bf16[4096,128]{1,0:T(8,128)(2,1)}, bf16[4096,128]{1,0:T(8,128)(2,1)}, u32[]{:S(2)}, u32[]{:S(2)}) collective-permute-start(bf16[4096,128]{1,0:T(8,128)(2,1)} %get-tuple-element.13), channel_id=1, source_target_pairs={{0,1},{1,0},{2,3},{3,2},{4,5},{5,4},{6,7},{7,6},{8,9},{9,8},{10,11... | collective-permute-start | bytes 3145736 | tf_op jit(solution)/shard_map/ppermute | solution.py:14
  12.5 4.2 %copy-start = (bf16[1,144,4096]{2,1,0:T(8,128)(2,1)S(1)}, bf16[1,144,4096]{2,1,0:T(8,128)(2,1)}, u32[]{:S(2)}) copy-start(bf16[1,144,4096]{2,1,0:T(8,128)(2,1)} %param.11) | copy-start | bytes 3538948
  12.5 46.8 %collective-permute-start.3 = (bf16[128,4096]{1,0:T(8,128)(2,1)}, bf16[128,4096]{1,0:T(8,128)(2,1)}, u32[]{:S(2)}, u32[]{:S(2)}) collective-permute-start(bf16[128,4096]{1,0:T(8,128)(2,1)} %get-tuple-element.15), channel_id=1, source_target_pairs={{0,1},{1,0},{2,3},{3,2},{4,5},{5,4},{6,7},{7,6},{8,9},{9,8},{10,11... | collective-permute-start | bytes 3145736 | tf_op jit(solution)/shard_map/ppermute | solution.py:14
  16.2 0.6 copy-start.14
  21.9 14.9 %copy-start.12 = (bf16[4096,128]{1,0:T(8,128)(2,1)S(1)}, bf16[4096,128]{1,0:T(8,128)(2,1)}, u32[]{:S(2)}) copy-start(bf16[4096,128]{1,0:T(8,128)(2,1)} %get-tuple-element.12) | copy-start | bytes 3145732
  21.9 14.9 %copy-start.15 = (f32[1,144]{1,0:T(1,128)S(1)}, f32[1,144]{1,0:T(1,128)}, u32[]{:S(2)}) copy-start(f32[1,144]{1,0:T(1,128)} %copy-done.14) | copy-start | bytes 1732
  36.8 2.5 copy-start.8
  36.8 2.5 copy-start.20
  36.8 2.5 copy-start.23
  36.8 2.5 copy-start.25
  39.4 19.9 %copy-start.2 = (bf16[1,144,4096]{2,1,0:T(8,128)(2,1)S(1)}, bf16[1,144,4096]{2,1,0:T(8,128)(2,1)}, u32[]{:S(2)}) copy-start(bf16[1,144,4096]{2,1,0:T(8,128)(2,1)} %param.12) | copy-start | bytes 3538948
  39.4 19.9 %copy-start.10 = (bf16[128,4096]{1,0:T(8,128)(2,1)S(1)}, bf16[128,4096]{1,0:T(8,128)(2,1)}, u32[]{:S(2)}) copy-start(bf16[128,4096]{1,0:T(8,128)(2,1)} %get-tuple-element.14) | copy-start | bytes 3145732
  42.0 22.5 %collective-permute-start.2 = (f32[2,144,256]{2,1,0:T(8,128)S(1)}, f32[2,144,256]{2,1,0:T(8,128)S(1)}, u32[]{:S(2)}, u32[]{:S(2)}) collective-permute-start(f32[2,144,256]{2,1,0:T(8,128)S(1)} %pad_maximum_fusion), channel_id=1, source_target_pairs={{0,1},{1,0},{2,3},{3,2},{4,5},{5,4},{6,7},{7,6},{8,9},{9,8},{10,11... | collective-permute-start | bytes 884744 | tf_op jit(solution)/shard_map/ppermute | solution.py:14
  62.4 7.0 %collective-permute-start.5 = (f32[144,256]{1,0:T(8,128)}, f32[144,256]{1,0:T(8,128)}, u32[]{:S(2)}, u32[]{:S(2)}) collective-permute-start(f32[144,256]{1,0:T(8,128)} %fusion.36), channel_id=1, source_target_pairs={{0,1},{1,0},{2,3},{3,2},{4,5},{5,4},{6,7},{7,6},{8,9},{9,8},{10,11... | collective-permute-start | bytes 442376 | tf_op jit(solution)/shard_map/ppermute | solution.py:14
  64.6 0.7 copy-start.6
  176.5 8.7 %copy-start.16 = (f32[1,144]{1,0:T(1,128)S(1)}, f32[1,144]{1,0:T(1,128)}, u32[]{:S(2)}) copy-start(f32[1,144]{1,0:T(1,128)} %copy-done.14) | copy-start | bytes 1732
  176.5 8.7 %copy-start.13 = (bf16[144,256]{1,0:T(8,128)(2,1)S(1)}, bf16[144,256]{1,0:T(8,128)(2,1)}, u32[]{:S(2)}) copy-start(bf16[144,256]{1,0:T(8,128)(2,1)} %fusion.44) | copy-start | bytes 221188
  176.5 53.8 %all-to-all-start.1 = ((f32[8,2,256,128]{3,2,1,0:T(8,128)}), f32[8,2,256,128]{3,2,1,0:T(8,128)S(1)}, u32[]{:S(2)}, u32[]{:S(2)}) async-start(f32[8,2,256,128]{3,2,1,0:T(8,128)} %bitcast.97), calls=%async_computation.1 | async-start | bytes 4194304 | tf_op jit(solution)/shard_map/all_to_all | solution.py:127
  185.2 5.9 %copy-start.7 = (f32[2,144,256]{2,1,0:T(8,128)S(1)}, f32[2,144,256]{2,1,0:T(8,128)}, u32[]{:S(2)}) copy-start(f32[2,144,256]{2,1,0:T(8,128)} %copy-done.6) | copy-start | bytes 884740
  185.2 5.9 %copy-start.9 = (bf16[1,144,4096]{2,1,0:T(8,128)(2,1)S(1)}, bf16[1,144,4096]{2,1,0:T(8,128)(2,1)}, u32[]{:S(2)}) copy-start(bf16[1,144,4096]{2,1,0:T(8,128)(2,1)} %param.8) | copy-start | bytes 3538948
  185.2 5.9 %copy-start.11 = (bf16[128,4096]{1,0:T(8,128)(2,1)S(1)}, bf16[128,4096]{1,0:T(8,128)(2,1)}, u32[]{:S(2)}) copy-start(bf16[128,4096]{1,0:T(8,128)(2,1)} %get-tuple-element.14) | copy-start | bytes 3145732
  185.2 5.9 %copy-start.21 = (bf16[4096]{0:T(1024)(128)(2,1)S(1)}, bf16[4096]{0:T(1024)(128)(2,1)}, u32[]{:S(2)}) copy-start(bf16[4096]{0:T(1024)(128)(2,1)} %param.10) | copy-start | bytes 24580
  185.2 5.8 %copy-start.24 = (pred[144]{0:T(512)(128)(4,1)S(1)}, pred[144]{0:T(512)(128)(4,1)}, u32[]{:S(2)}) copy-start(pred[144]{0:T(512)(128)(4,1)} %copy-done.22) | copy-start | bytes 436
  188.9 7.7 %copy-start.3 = (bf16[1,144,4096]{2,1,0:T(8,128)(2,1)S(1)}, bf16[1,144,4096]{2,1,0:T(8,128)(2,1)}, u32[]{:S(2)}) copy-start(bf16[1,144,4096]{2,1,0:T(8,128)(2,1)} %param.12) | copy-start | bytes 3538948
  188.9 7.7 %collective-permute-start.6 = (f32[144]{0:T(256)S(1)}, f32[144]{0:T(256)S(1)}, u32[]{:S(2)}, u32[]{:S(2)}) collective-permute-start(f32[144]{0:T(256)S(1)} %get-tuple-element.20), channel_id=1, source_target_pairs={{0,1},{1,0},{2,3},{3,2},{4,5},{5,4},{6,7},{7,6},{8,9},{9,8},{10,11... | collective-permute-start | bytes 1736 | tf_op jit(solution)/shard_map/ppermute | solution.py:14
  194.6 42.4 %collective-permute-start.4 = (bf16[144,4096]{1,0:T(8,128)(2,1)}, bf16[144,4096]{1,0:T(8,128)(2,1)}, u32[]{:S(2)}, u32[]{:S(2)}) collective-permute-start(bf16[144,4096]{1,0:T(8,128)(2,1)} %fusion), channel_id=1, source_target_pairs={{0,2},{2,4},{4,6},{1,3},{3,5},{5,7},{8,10},{10,12},{12,14},{9,11},... | collective-permute-start | bytes 3538952 | tf_op jit(solution)/shard_map/ppermute | solution.py:10
  198.6 38.5 %collective-permute-start.7 = (bf16[144,4096]{1,0:T(8,128)(2,1)}, bf16[144,4096]{1,0:T(8,128)(2,1)S(1)}, u32[]{:S(2)}, u32[]{:S(2)}) collective-permute-start(bf16[144,4096]{1,0:T(8,128)(2,1)} %fusion.10), channel_id=1, source_target_pairs={{2,0},{4,2},{6,4},{3,1},{5,3},{7,5},{10,8},{12,10},{14,12},{11,9},... | collective-permute-start | bytes 3538952 | tf_op jit(solution)/shard_map/ppermute | solution.py:10
  230.4 16.5 %collective-permute-start.8 = (f32[2,256,128]{2,1,0:T(8,128)S(1)}, f32[2,256,128]{2,1,0:T(8,128)S(1)}, u32[]{:S(2)}, u32[]{:S(2)}) collective-permute-start(f32[2,256,128]{2,1,0:T(8,128)S(1)} %reduce_sum.49), channel_id=1, source_target_pairs={{1,128},{9,136},{17,144},{25,152},{33,160},{41,168},{49,176},{57,1... | collective-permute-start | bytes 786440 | tf_op jit(solution)/shard_map/ppermute | solution.py:137

commit v7 on v6

--- a/solution.py
+++ b/solution.py
@@ -18,12 +18,6 @@
     return shard + swapped(shard, axis)
 
 
-def contract_rows(left, right):
-    return lax.dot_general(
-        left, right, (((0,), (0,)), ((), ())), preferred_element_type=jnp.float32
-    )
-
-
 def contract_cols(left, right):
     return lax.dot_general(
         left, right, (((1,), (1,)), ((), ())), preferred_element_type=jnp.float32
@@ -38,7 +32,7 @@
     )
 
 
-def on_device(arriving, keep_mask, mask_vector, stashed, cotangent, gain, down_adapter, up_adapter):
+def step(arriving, keep_mask, mask_vector, stashed, cotangent, gain, down_adapter, up_adapter):
     half = lax.axis_index("mp")
     first = half == 0
     is_first = lax.axis_index("section") == 0
@@ -57,17 +51,17 @@
     down_theirs = lax.dynamic_slice_in_dim(down_local, (1 - half) * width, width, axis=0)
     up_mine = lax.dynamic_slice_in_dim(up_local, half * width, width, axis=1)
     up_theirs = lax.dynamic_slice_in_dim(up_local, (1 - half) * width, width, axis=1)
-    down_half = in_unit_order(down_mine, swapped(down_theirs, "mp"), first, 1)
-    up_half = in_unit_order(up_mine, swapped(up_theirs, "mp"), first, 0)
+    down_received = swapped(down_theirs, "mp")
+    up_received = swapped(up_theirs, "mp")
+    down_half = in_unit_order(down_mine, down_received, first, 1)
+    up_half = in_unit_order(up_mine, up_received, first, 0)
 
     input_values = inputs.astype(jnp.float32)
     saved_values = saved.astype(jnp.float32)
-    squares = pair_sum(
-        jnp.stack(
-            [jnp.sum(input_values * input_values, axis=1), jnp.sum(saved_values * saved_values, axis=1)]
-        ),
-        "mp",
+    squares = jnp.stack(
+        [jnp.sum(input_values * input_values, axis=1), jnp.sum(saved_values * saved_values, axis=1)]
     )
+    squares = pair_sum(squares, "mp")
     scale = lax.rsqrt(squares[0] / full_width + 1e-05)[:, None]
     saved_scale = lax.rsqrt(squares[1] / full_width + 1e-05)[:, None]
     normed = (input_values * scale * gain_row).astype(jnp.bfloat16)
@@ -153,7 +147,7 @@
         P("section", "mp", None),
     )
     return jax.shard_map(
-        on_device,
+        step,
         mesh=mesh,
         in_specs=placed,
         out_specs=(

time: 252 us -> 252 us (level)
  no operation moved by 1% of the time
where the time goes in v7:
time: 252 us
  blocking collectives  94.6 us (38%)
  waiting for transfers between devices  68.8 us (27%)
  starting transfers between devices  32.4 us (13%)
  other arithmetic  20.8 us (8%)
  matrix products  17.8 us (7%)
  local copies, waits for them, and re-layouts  16.3 us (6%)
    all_to_all x1, blocking collectives, step(): lax.all_to_all(slots, 'dp', 0, 0, tiled=True, axis_index_groups=y_groups)  94.6 us
    ppermute x6, waiting for transfers between devices, swapped(): return lax.ppermute(shard, axis, [(0, 1), (1, 0)])  31 us
    all_to_all x1, waiting for transfers between devices, step(): lax.all_to_all(over_y.reshape(nz, 2, block, units), 'dp', 0, 0, tiled=Tru...  28 us
    ppermute x6, starting transfers between devices, swapped(): return lax.ppermute(shard, axis, [(0, 1), (1, 0)])  11.5 us
    ppermute x1, waiting for transfers between devices, step(): moved = lax.ppermute(summed, ('dp', 'mp'), pairs)  9.8 us
    all_to_all x1, starting transfers between devices, step(): lax.all_to_all(over_y.reshape(nz, 2, block, units), 'dp', 0, 0, tiled=Tru...  8.7 us
    dot_general x2, matrix products, contract_cols(): lax.dot_general(left, right, (((1,), (1,)), ((), ())), preferred_element_...  6.75 us
    ppermute x1, starting transfers between devices, step(): moved = lax.ppermute(summed, ('dp', 'mp'), pairs)  6.67 us
  transfers between devices with their start and end apart: 10, of which 5 were waited for; matrix products, arithmetic and copies ran while one was open for 12% of the time, Pallas kernels for 0%

profile of v7, /device:TPU:38, one launch (start us, length us, event | category | flops | bytes accessed | tf_op | source)
XLA Modules:
  0.0 251.7 jit_solution(4959537084474058335)
XLA Ops:
  0.6 1.7 fusion.5
  2.4 0.7 compare_or_fusion
  3.1 1.8 fusion.14
  4.8 0.6 copy-done.18
  5.4 0.6 pad_maximum_fusion.1
  6.0 1.4 collective-permute-start
  7.4 1.6 dynamic-slice_bitcast_fusion.3
  9.0 2.1 collective-permute-start.1
  11.1 1.4 dynamic-slice_bitcast_fusion.1
  12.5 1.4 collective-permute-start.3
  14.0 0.9 stack.42
  14.9 0.0 collective-permute-done
  14.9 0.7 fusion.53
  15.6 0.6 fusion.49
  16.2 0.6 copy-done.14
  16.8 0.4 fusion.13
  17.1 1.7 stack.41
  18.9 3.0 %maximum_bitcast_fusion = bf16[4,4,2,144,256]{4,0,1,3,2:T(4,128)(2,1)S(1)} fusion(bf16[1,144,4,4,256]{4,3,2,1,0:T(4,128)(2,1)S(1)} %stack.42, bf16[1,144,4,4,256]{4,3,2,1,0:T(4,128)(2,1)} %stack.41), kind=kLoop, calls=%fused_computation.23 | loop fusion | flops 1179648 | bytes 4718592 | tf_op jit(solution)/shard_map/transpose | solution.py:108
  21.9 0.8 copy.15
  22.7 14.1 %collective-permute-done.1 = bf16[4096,128]{1,0:T(8,128)(2,1)} collective-permute-done((bf16[4096,128]{1,0:T(8,128)(2,1)}, bf16[4096,128]{1,0:T(8,128)(2,1)}, u32[]{:S(2)}, u32[]{:S(2)}) %collective-permute-start.1) | collective-permute-done | bytes 1048608 | tf_op jit(solution)/shard_map/ppermute | solution.py:14
  36.8 0.0 copy-start.25
  36.9 2.5 fusion.30
  39.4 0.0 copy-start.2
  39.4 0.0 copy-start.10
  39.4 2.6 %fusion.33 = f32[1,144,256]{2,1,0:T(8,128)S(1)} fusion(f32[4096]{0:T(1024)S(1)} %bitcast.101, f32[144]{0:T(256)S(1)} %bitcast.111, bf16[1,144,4096]{2,1,0:T(8,128)(2,1)S(1)} %copy-done.8, pred[144]{0:T(512)(128)(4,1)S(1)} %copy-done.23, bf16[4096]{0:T(1024)(128)(2,1)S(1)} %copy-done.20, bf16[4096,128]{1,0:T(8,128)(2,1)} %collective-permute-done.1, ...), kind=kOutput, calls=%fused_computation.39 | convolution fusion | flops 314376192 | bytes 3449553 | tf_op jit(solution)/shard_map/dot_general | solution.py:73
  42.0 2.2 collective-permute-start.2
  44.3 15.0 %collective-permute-done.3 = bf16[128,4096]{1,0:T(8,128)(2,1)} collective-permute-done((bf16[128,4096]{1,0:T(8,128)(2,1)}, bf16[128,4096]{1,0:T(8,128)(2,1)}, u32[]{:S(2)}, u32[]{:S(2)}) %collective-permute-start.3) | collective-permute-done | bytes 1048608 | tf_op jit(solution)/shard_map/ppermute | solution.py:14
  59.3 3.1 %fusion.36 = f32[144,256]{1,0:T(8,128)} fusion(bf16[1,144,4096]{2,1,0:T(8,128)(2,1)S(1)} %copy-done.2, bf16[128,4096]{1,0:T(8,128)(2,1)} %collective-permute-done.3, bf16[128,4096]{1,0:T(8,128)(2,1)S(1)} %copy-done.10, pred[]{:T(512)S(6)} %eq.18), kind=kOutput, calls=%fused_computation.40 | convolution fusion | flops 311427072 | bytes 3424257 | tf_op jit(solution)/shard_map/dot_general | solution.py:22
  62.4 2.1 collective-permute-start.5
  64.6 0.0 collective-permute-done.2
  64.6 0.0 copy-start.6
  64.6 0.7 copy-done.6
  65.3 0.7 multiply_convert_fusion
  66.0 1.5 stack.45
  67.5 1.9 collective-permute-done.5
  69.4 1.7 fusion.44
  71.2 1.5 stack.44
  72.7 1.1 maximum_bitcast_fusion.1
  73.9 2.4 fusion.17
  76.3 94.6 %all_to_all.10 = f32[4,2,4,2,256,128]{5,4,3,2,1,0:T(8,128)} all-to-all(f32[4,2,4,2,256,128]{5,4,3,2,1,0:T(8,128)S(1)} %fusion.17), channel_id=1, replica_groups={{0,8,16,24},{32,40,48,56},{64,72,80,88},{96,104,112,120},{128,136,144,1..., dimensions={0} | all-to-all | bytes 16777216 | tf_op jit(solution)/shard_map/all_to_all | solution.py:118
  170.9 5.6 %reduce_sum.48 = f32[2,4,2,256,128]{4,3,2,1,0:T(8,128)} reduce(f32[4,2,4,2,256,128]{5,4,3,2,1,0:T(8,128)} %all_to_all.10, f32[]{:T(128)} %constant.45.clone.1), dimensions={0}, to_apply=%region_3.4 | reduce | flops 1572864 | bytes 10485764 | tf_op jit(solution)/shard_map/reduce_sum | solution.py:120
  176.5 8.7 %all-to-all-start.1 = ((f32[8,2,256,128]{3,2,1,0:T(8,128)}), f32[8,2,256,128]{3,2,1,0:T(8,128)S(1)}, u32[]{:S(2)}, u32[]{:S(2)}) async-start(f32[8,2,256,128]{3,2,1,0:T(8,128)} %bitcast.97), calls=%async_computation.1 | async-start | bytes 4194304 | tf_op jit(solution)/shard_map/all_to_all | solution.py:121
  185.2 0.0 copy-start.7
  185.2 0.0 copy-start.9
  185.2 0.0 copy-start.11
  185.2 0.0 copy-start.21
  185.3 3.6 %fusion.11 = (f32[144]{0:T(256)S(1)}, f32[144,4096]{1,0:T(8,128)S(1)}) fusion(bf16[1,144,4096]{2,1,0:T(8,128)(2,1)S(1)} %copy-done, f32[4096]{0:T(1024)S(1)} %bitcast.102, bf16[144,256]{1,0:T(8,128)(2,1)S(1)} %copy-done.13, bf16[4096,128]{1,0:T(8,128)(2,1)} %collective-permute-done.1, bf16[4096,128]{1,0:T(8,128)(2,1)} %get-tuple-element.12, pred[]{:T(512)S(6)} %eq.18), kind=kOutput, calls=%fused_computation.17 | convolution fusion | flops 313786240 | bytes 5726785 | tf_op jit(solution)/shard_map/dot_general | solution.py:22
  188.9 0.0 copy-start.3
  188.9 2.2 collective-permute-start.6
  191.1 3.5 %fusion = bf16[144,4096]{1,0:T(8,128)(2,1)} fusion(bf16[128,4096]{1,0:T(8,128)(2,1)} %collective-permute-done.3, bf16[128,4096]{1,0:T(8,128)(2,1)S(1)} %copy-done.11, pred[]{:T(512)S(6)} %eq.18, f32[2,144,256]{2,1,0:T(8,128)S(1)} %copy-done.7, bf16[4096]{0:T(1024)(128)(2,1)S(1)} %copy-done.21, bf16[1,144,4096]{2,1,0:T(8,128)(2,1)S(1)} %copy-done.9, ...), kind=kOutput, calls=%fused_computation.2 | convolution fusion | flops 313970688 | bytes 4612609 | tf_op jit(solution)/shard_map/dot_general | solution.py:82
  194.6 1.9 collective-permute-start.4
  196.6 0.0 collective-permute-done.6
  196.6 2.0 fusion.10
  198.6 3.6 %collective-permute-start.7 = (bf16[144,4096]{1,0:T(8,128)(2,1)}, bf16[144,4096]{1,0:T(8,128)(2,1)S(1)}, u32[]{:S(2)}, u32[]{:S(2)}) collective-permute-start(bf16[144,4096]{1,0:T(8,128)(2,1)} %fusion.10), channel_id=1, source_target_pairs={{2,0},{4,2},{6,4},{3,1},{5,3},{7,5},{10,8},{12,10},{14,12},{11,9},... | collective-permute-start | bytes 3538952 | tf_op jit(solution)/shard_map/ppermute | solution.py:10
  202.2 28.0 %all-to-all-done.1 = f32[8,2,256,128]{3,2,1,0:T(8,128)S(1)} async-done(((f32[8,2,256,128]{3,2,1,0:T(8,128)}), f32[8,2,256,128]{3,2,1,0:T(8,128)S(1)}, u32[]{:S(2)}, u32[]{:S(2)}) %all-to-all-start.1) | async-done | bytes 2097184 | tf_op jit(solution)/shard_map/all_to_all | solution.py:121
  230.3 0.1 reduce_sum.49
  230.4 6.7 %collective-permute-start.8 = (f32[2,256,128]{2,1,0:T(8,128)S(1)}, f32[2,256,128]{2,1,0:T(8,128)S(1)}, u32[]{:S(2)}, u32[]{:S(2)}) collective-permute-start(f32[2,256,128]{2,1,0:T(8,128)S(1)} %reduce_sum.49), channel_id=1, source_target_pairs={{1,128},{9,136},{17,144},{25,152},{33,160},{41,168},{49,176},{57,1... | collective-permute-start | bytes 786440 | tf_op jit(solution)/shard_map/ppermute | solution.py:131
  237.1 0.0 collective-permute-done.4
  237.1 0.0 collective-permute-done.7
  237.1 9.8 %collective-permute-done.8 = f32[2,256,128]{2,1,0:T(8,128)S(1)} collective-permute-done((f32[2,256,128]{2,1,0:T(8,128)S(1)}, f32[2,256,128]{2,1,0:T(8,128)S(1)}, u32[]{:S(2)}, u32[]{:S(2)}) %collective-permute-start.8) | collective-permute-done | bytes 262176 | tf_op jit(solution)/shard_map/ppermute | solution.py:131
  246.9 0.7 slice_bitcast_fusion.1
  247.6 0.8 copy.17
  248.4 2.4 copy.20
  250.7 1.0 copy.21
  (47 shorter events, 0.2 us)
Async XLA Ops:
  0.6 6.8 %copy-start.4 = (bf16[1,8192,128]{2,1,0:T(8,128)(2,1)S(1)}, bf16[1,8192,128]{2,1,0:T(8,128)(2,1)}, u32[]{:S(2)}) copy-start(bf16[1,8192,128]{2,1,0:T(8,128)(2,1)} %param.14) | copy-start | bytes 6291460
  2.4 3.6 %copy-start.19 = (f32[144]{0:T(256)}, f32[144]{0:T(256)S(1)}, u32[]{:S(2)}) copy-start(f32[144]{0:T(256)S(1)} %fusion.5) | copy-start | bytes 1732
  3.1 2.9 %copy-start.22 = (pred[144]{0:T(512)(128)(4,1)}, pred[144]{0:T(512)(128)(4,1)S(1)}, u32[]{:S(2)}) copy-start(pred[144]{0:T(512)(128)(4,1)S(1)} %compare_or_fusion) | copy-start | bytes 436
  4.8 0.6 copy-start.18
  6.0 8.9 %collective-permute-start = (f32[2,144]{1,0:T(2,128)}, f32[2,144]{1,0:T(2,128)}, u32[]{:S(2)}, u32[]{:S(2)}) collective-permute-start(f32[2,144]{1,0:T(2,128)} %pad_maximum_fusion.1), channel_id=1, source_target_pairs={{0,1},{1,0},{2,3},{3,2},{4,5},{5,4},{6,7},{7,6},{8,9},{9,8},{10,11... | collective-permute-start | bytes 3464 | tf_op jit(solution)/shard_map/ppermute | solution.py:14
  7.4 3.7 %copy-start.5 = (bf16[1,128,8192]{2,1,0:T(8,128)(2,1)S(1)}, bf16[1,128,8192]{2,1,0:T(8,128)(2,1)}, u32[]{:S(2)}) copy-start(bf16[1,128,8192]{2,1,0:T(8,128)(2,1)} %param.15) | copy-start | bytes 6291460
  9.0 5.0 %copy-start.17 = (bf16[1,4096]{1,0:T(2,128)(2,1)S(1)}, bf16[1,4096]{1,0:T(2,128)(2,1)}, u32[]{:S(2)}) copy-start(bf16[1,4096]{1,0:T(2,128)(2,1)} %param.13) | copy-start | bytes 24580
  9.0 5.0 %copy-start.1 = (bf16[1,144,4096]{2,1,0:T(8,128)(2,1)S(1)}, bf16[1,144,4096]{2,1,0:T(8,128)(2,1)}, u32[]{:S(2)}) copy-start(bf16[1,144,4096]{2,1,0:T(8,128)(2,1)} %param.12) | copy-start | bytes 3538948
  9.0 27.8 %collective-permute-start.1 = (bf16[4096,128]{1,0:T(8,128)(2,1)}, bf16[4096,128]{1,0:T(8,128)(2,1)}, u32[]{:S(2)}, u32[]{:S(2)}) collective-permute-start(bf16[4096,128]{1,0:T(8,128)(2,1)} %get-tuple-element.13), channel_id=1, source_target_pairs={{0,1},{1,0},{2,3},{3,2},{4,5},{5,4},{6,7},{7,6},{8,9},{9,8},{10,11... | collective-permute-start | bytes 3145736 | tf_op jit(solution)/shard_map/ppermute | solution.py:14
  12.5 4.2 %copy-start = (bf16[1,144,4096]{2,1,0:T(8,128)(2,1)S(1)}, bf16[1,144,4096]{2,1,0:T(8,128)(2,1)}, u32[]{:S(2)}) copy-start(bf16[1,144,4096]{2,1,0:T(8,128)(2,1)} %param.11) | copy-start | bytes 3538948
  12.5 46.8 %collective-permute-start.3 = (bf16[128,4096]{1,0:T(8,128)(2,1)}, bf16[128,4096]{1,0:T(8,128)(2,1)}, u32[]{:S(2)}, u32[]{:S(2)}) collective-permute-start(bf16[128,4096]{1,0:T(8,128)(2,1)} %get-tuple-element.15), channel_id=1, source_target_pairs={{0,1},{1,0},{2,3},{3,2},{4,5},{5,4},{6,7},{7,6},{8,9},{9,8},{10,11... | collective-permute-start | bytes 3145736 | tf_op jit(solution)/shard_map/ppermute | solution.py:14
  16.2 0.6 copy-start.14
  21.9 14.9 %copy-start.12 = (bf16[4096,128]{1,0:T(8,128)(2,1)S(1)}, bf16[4096,128]{1,0:T(8,128)(2,1)}, u32[]{:S(2)}) copy-start(bf16[4096,128]{1,0:T(8,128)(2,1)} %get-tuple-element.12) | copy-start | bytes 3145732
  21.9 14.9 %copy-start.15 = (f32[1,144]{1,0:T(1,128)S(1)}, f32[1,144]{1,0:T(1,128)}, u32[]{:S(2)}) copy-start(f32[1,144]{1,0:T(1,128)} %copy-done.14) | copy-start | bytes 1732
  36.8 2.5 copy-start.8
  36.8 2.5 copy-start.20
  36.8 2.5 copy-start.23
  36.8 2.5 copy-start.25
  39.4 19.9 %copy-start.2 = (bf16[1,144,4096]{2,1,0:T(8,128)(2,1)S(1)}, bf16[1,144,4096]{2,1,0:T(8,128)(2,1)}, u32[]{:S(2)}) copy-start(bf16[1,144,4096]{2,1,0:T(8,128)(2,1)} %param.12) | copy-start | bytes 3538948
  39.4 19.9 %copy-start.10 = (bf16[128,4096]{1,0:T(8,128)(2,1)S(1)}, bf16[128,4096]{1,0:T(8,128)(2,1)}, u32[]{:S(2)}) copy-start(bf16[128,4096]{1,0:T(8,128)(2,1)} %get-tuple-element.14) | copy-start | bytes 3145732
  42.0 22.5 %collective-permute-start.2 = (f32[2,144,256]{2,1,0:T(8,128)S(1)}, f32[2,144,256]{2,1,0:T(8,128)S(1)}, u32[]{:S(2)}, u32[]{:S(2)}) collective-permute-start(f32[2,144,256]{2,1,0:T(8,128)S(1)} %pad_maximum_fusion), channel_id=1, source_target_pairs={{0,1},{1,0},{2,3},{3,2},{4,5},{5,4},{6,7},{7,6},{8,9},{9,8},{10,11... | collective-permute-start | bytes 884744 | tf_op jit(solution)/shard_map/ppermute | solution.py:14
  62.4 7.0 %collective-permute-start.5 = (f32[144,256]{1,0:T(8,128)}, f32[144,256]{1,0:T(8,128)}, u32[]{:S(2)}, u32[]{:S(2)}) collective-permute-start(f32[144,256]{1,0:T(8,128)} %fusion.36), channel_id=1, source_target_pairs={{0,1},{1,0},{2,3},{3,2},{4,5},{5,4},{6,7},{7,6},{8,9},{9,8},{10,11... | collective-permute-start | bytes 442376 | tf_op jit(solution)/shard_map/ppermute | solution.py:14
  64.6 0.7 copy-start.6
  176.5 8.7 %copy-start.16 = (f32[1,144]{1,0:T(1,128)S(1)}, f32[1,144]{1,0:T(1,128)}, u32[]{:S(2)}) copy-start(f32[1,144]{1,0:T(1,128)} %copy-done.14) | copy-start | bytes 1732
  176.5 8.7 %copy-start.13 = (bf16[144,256]{1,0:T(8,128)(2,1)S(1)}, bf16[144,256]{1,0:T(8,128)(2,1)}, u32[]{:S(2)}) copy-start(bf16[144,256]{1,0:T(8,128)(2,1)} %fusion.44) | copy-start | bytes 221188
  176.5 53.8 %all-to-all-start.1 = ((f32[8,2,256,128]{3,2,1,0:T(8,128)}), f32[8,2,256,128]{3,2,1,0:T(8,128)S(1)}, u32[]{:S(2)}, u32[]{:S(2)}) async-start(f32[8,2,256,128]{3,2,1,0:T(8,128)} %bitcast.97), calls=%async_computation.1 | async-start | bytes 4194304 | tf_op jit(solution)/shard_map/all_to_all | solution.py:121
  185.2 5.9 %copy-start.7 = (f32[2,144,256]{2,1,0:T(8,128)S(1)}, f32[2,144,256]{2,1,0:T(8,128)}, u32[]{:S(2)}) copy-start(f32[2,144,256]{2,1,0:T(8,128)} %copy-done.6) | copy-start | bytes 884740
  185.2 5.9 %copy-start.9 = (bf16[1,144,4096]{2,1,0:T(8,128)(2,1)S(1)}, bf16[1,144,4096]{2,1,0:T(8,128)(2,1)}, u32[]{:S(2)}) copy-start(bf16[1,144,4096]{2,1,0:T(8,128)(2,1)} %param.8) | copy-start | bytes 3538948
  185.2 5.9 %copy-start.11 = (bf16[128,4096]{1,0:T(8,128)(2,1)S(1)}, bf16[128,4096]{1,0:T(8,128)(2,1)}, u32[]{:S(2)}) copy-start(bf16[128,4096]{1,0:T(8,128)(2,1)} %get-tuple-element.14) | copy-start | bytes 3145732
  185.2 5.9 %copy-start.21 = (bf16[4096]{0:T(1024)(128)(2,1)S(1)}, bf16[4096]{0:T(1024)(128)(2,1)}, u32[]{:S(2)}) copy-start(bf16[4096]{0:T(1024)(128)(2,1)} %param.10) | copy-start | bytes 24580
  185.2 5.8 %copy-start.24 = (pred[144]{0:T(512)(128)(4,1)S(1)}, pred[144]{0:T(512)(128)(4,1)}, u32[]{:S(2)}) copy-start(pred[144]{0:T(512)(128)(4,1)} %copy-done.22) | copy-start | bytes 436
  188.9 7.7 %copy-start.3 = (bf16[1,144,4096]{2,1,0:T(8,128)(2,1)S(1)}, bf16[1,144,4096]{2,1,0:T(8,128)(2,1)}, u32[]{:S(2)}) copy-start(bf16[1,144,4096]{2,1,0:T(8,128)(2,1)} %param.12) | copy-start | bytes 3538948
  188.9 7.7 %collective-permute-start.6 = (f32[144]{0:T(256)S(1)}, f32[144]{0:T(256)S(1)}, u32[]{:S(2)}, u32[]{:S(2)}) collective-permute-start(f32[144]{0:T(256)S(1)} %get-tuple-element.20), channel_id=1, source_target_pairs={{0,1},{1,0},{2,3},{3,2},{4,5},{5,4},{6,7},{7,6},{8,9},{9,8},{10,11... | collective-permute-start | bytes 1736 | tf_op jit(solution)/shard_map/ppermute | solution.py:14
  194.6 42.4 %collective-permute-start.4 = (bf16[144,4096]{1,0:T(8,128)(2,1)}, bf16[144,4096]{1,0:T(8,128)(2,1)}, u32[]{:S(2)}, u32[]{:S(2)}) collective-permute-start(bf16[144,4096]{1,0:T(8,128)(2,1)} %fusion), channel_id=1, source_target_pairs={{0,2},{2,4},{4,6},{1,3},{3,5},{5,7},{8,10},{10,12},{12,14},{9,11},... | collective-permute-start | bytes 3538952 | tf_op jit(solution)/shard_map/ppermute | solution.py:10
  198.6 38.5 %collective-permute-start.7 = (bf16[144,4096]{1,0:T(8,128)(2,1)}, bf16[144,4096]{1,0:T(8,128)(2,1)S(1)}, u32[]{:S(2)}, u32[]{:S(2)}) collective-permute-start(bf16[144,4096]{1,0:T(8,128)(2,1)} %fusion.10), channel_id=1, source_target_pairs={{2,0},{4,2},{6,4},{3,1},{5,3},{7,5},{10,8},{12,10},{14,12},{11,9},... | collective-permute-start | bytes 3538952 | tf_op jit(solution)/shard_map/ppermute | solution.py:10
  230.4 16.5 %collective-permute-start.8 = (f32[2,256,128]{2,1,0:T(8,128)S(1)}, f32[2,256,128]{2,1,0:T(8,128)S(1)}, u32[]{:S(2)}, u32[]{:S(2)}) collective-permute-start(f32[2,256,128]{2,1,0:T(8,128)S(1)} %reduce_sum.49), channel_id=1, source_target_pairs={{1,128},{9,136},{17,144},{25,152},{33,160},{41,168},{49,176},{57,1... | collective-permute-start | bytes 786440 | tf_op jit(solution)/shard_map/ppermute | solution.py:131

commit v8 on v7

--- a/solution.py
+++ b/solution.py
@@ -51,17 +51,18 @@
     down_theirs = lax.dynamic_slice_in_dim(down_local, (1 - half) * width, width, axis=0)
     up_mine = lax.dynamic_slice_in_dim(up_local, half * width, width, axis=1)
     up_theirs = lax.dynamic_slice_in_dim(up_local, (1 - half) * width, width, axis=1)
-    down_received = swapped(down_theirs, "mp")
+    down_half = in_unit_order(down_mine, swapped(down_theirs, "mp"), first, 1)
     up_received = swapped(up_theirs, "mp")
-    down_half = in_unit_order(down_mine, down_received, first, 1)
     up_half = in_unit_order(up_mine, up_received, first, 0)
 
     input_values = inputs.astype(jnp.float32)
     saved_values = saved.astype(jnp.float32)
-    squares = jnp.stack(
-        [jnp.sum(input_values * input_values, axis=1), jnp.sum(saved_values * saved_values, axis=1)]
+    squares = pair_sum(
+        jnp.stack(
+            [jnp.sum(input_values * input_values, axis=1), jnp.sum(saved_values * saved_values, axis=1)]
+        ),
+        "mp",
     )
-    squares = pair_sum(squares, "mp")
     scale = lax.rsqrt(squares[0] / full_width + 1e-05)[:, None]
     saved_scale = lax.rsqrt(squares[1] / full_width + 1e-05)[:, None]
     normed = (input_values * scale * gain_row).astype(jnp.bfloat16)
@@ -104,20 +105,22 @@
     ny = 4
     nz = replicas // ny
     tokens = saved.shape[0]
-    rows = jnp.stack([saved_normed, upstream])
-    rows = rows.reshape(2, tokens, nz // 2, ny, block).transpose(3, 2, 0, 1, 4)
-    rows = jnp.broadcast_to(rows[:, None], (ny, 2, nz // 2, 2, tokens, block))
-    cols = jnp.stack([pre_grad, saved_hidden])
-    cols = cols.reshape(2, tokens, 2, units).transpose(2, 0, 1, 3)
-    cols = jnp.broadcast_to(cols[None, :, None], (ny, 2, nz // 2, 2, tokens, units))
-    slots = lax.dot_general(
-        rows, cols, (((4,), (4,)), ((0, 1, 2, 3), (0, 1, 2, 3))), preferred_element_type=jnp.float32
-    )
     y_groups = [[z * ny + y for y in range(ny)] for z in range(nz)]
     z_groups = [[z * ny + y for z in range(nz)] for y in range(ny)]
-    over_y = lax.all_to_all(
-        slots, "dp", 0, 0, tiled=True, axis_index_groups=y_groups
-    ).sum(axis=0)
+
+    def summed_over_y(rows, cols):
+        rows = rows.reshape(tokens, nz // 2, ny, block).transpose(2, 1, 0, 3)
+        rows = jnp.broadcast_to(rows[:, None], (ny, 2, nz // 2, tokens, block))
+        cols = cols.reshape(tokens, 2, units).transpose(1, 0, 2)
+        cols = jnp.broadcast_to(cols[None, :, None], (ny, 2, nz // 2, tokens, units))
+        slots = lax.dot_general(
+            rows, cols, (((3,), (3,)), ((0, 1, 2), (0, 1, 2))), preferred_element_type=jnp.float32
+        )
+        return lax.all_to_all(slots, "dp", 0, 0, tiled=True, axis_index_groups=y_groups).sum(axis=0)
+
+    up_over_y = summed_over_y(upstream, saved_hidden)
+    down_over_y = summed_over_y(saved_normed, pre_grad)
+    over_y = jnp.stack([down_over_y, up_over_y], axis=2)
     summed = lax.all_to_all(
         over_y.reshape(nz, 2, block, units), "dp", 0, 0, tiled=True, axis_index_groups=z_groups
     ).sum(axis=0)

time: 252 us -> 237 us (0.940)
  blocking collectives: 94.6 us -> 0 us
  waiting for transfers between devices: 68.8 us -> 147 us
  other arithmetic: 20.8 us -> 12.7 us
  starting transfers between devices: 32.4 us -> 37.8 us
  matrix products: 17.8 us -> 22.4 us
    all_to_all x1 -> x0, blocking collectives: 94.6 us -> none  [step(): lax.all_to_all(slots, 'dp', 0, 0, tiled=True, axis_index_groups=y_groups)]
    all_to_all x0 -> x2, waiting for transfers between devices: none -> 50.7 us  [summed_over_y(): lax.all_to_all(slots, 'dp', 0, 0, tiled=True, axis_index_groups=y_groups)]
    ppermute x6, waiting for transfers between devices: 31 us -> 53.8 us  [swapped(): return lax.ppermute(shard, axis, [(0, 1), (1, 0)])]
    all_to_all x0 -> x2, starting transfers between devices: none -> 10.1 us  [summed_over_y(): lax.all_to_all(slots, 'dp', 0, 0, tiled=True, axis_index_groups=y_groups)]
    another operation x4 -> x2, local copies, waits for them, and re-layouts: 5.71 us -> 1.23 us  [the longest x1 0.91 us: summed_over_y(): rows = rows.reshape(tokens, nz // 2, ny, block).transpose(2, 1, 0, 3)]
    dot_general x1 -> x2, matrix products: 2.4 us -> 6.13 us  [summed_over_y(): lax.dot_general(rows, cols, (((3,), (3,)), ((0, 1, 2), (0, 1, 2))), prefe...]
    transpose x2, other arithmetic: 4.17 us -> 0.65 us  [the longest x1 0.6 us: summed_over_y(): rows = rows.reshape(tokens, nz // 2, ny, block).transpose(2, 1, 0, 3)]
    ppermute x1, starting transfers between devices: 6.67 us -> 4.11 us  [step(): moved = lax.ppermute(summed, ('dp', 'mp'), pairs)]
  transfers between devices with their start and end apart: 10 -> 12, of which waited for: 5 -> 8; matrix products, arithmetic and copies ran while one was open for 12% -> 11% of each run, Pallas kernels for 0% -> 0%
where the time goes in v8:
time: 237 us; the launch traced here: 236 us
  waiting for transfers between devices  147 us (62%)
  starting transfers between devices  37.8 us (16%)
  matrix products  22.4 us (9%)
  local copies, waits for them, and re-layouts  14.7 us (6%)
  other arithmetic  12.7 us (5%)
    ppermute x6, waiting for transfers between devices, swapped(): return lax.ppermute(shard, axis, [(0, 1), (1, 0)])  53.8 us
    all_to_all x2, waiting for transfers between devices, summed_over_y(): lax.all_to_all(slots, 'dp', 0, 0, tiled=True, axis_index_groups=y_groups)  50.7 us
    all_to_all x1, waiting for transfers between devices, step(): lax.all_to_all(over_y.reshape(nz, 2, block, units), 'dp', 0, 0, tiled=Tru...  30.2 us
    ppermute x1, waiting for transfers between devices, step(): moved = lax.ppermute(summed, ('dp', 'mp'), pairs)  12.3 us
    all_to_all x2, starting transfers between devices, summed_over_y(): lax.all_to_all(slots, 'dp', 0, 0, tiled=True, axis_index_groups=y_groups)  10.1 us
    ppermute x6, starting transfers between devices, swapped(): return lax.ppermute(shard, axis, [(0, 1), (1, 0)])  9.42 us
    all_to_all x1, starting transfers between devices, step(): lax.all_to_all(over_y.reshape(nz, 2, block, units), 'dp', 0, 0, tiled=Tru...  8.7 us
    dot_general x2, matrix products, contract_cols(): lax.dot_general(left, right, (((1,), (1,)), ((), ())), preferred_element_...  6.97 us
  transfers between devices with their start and end apart: 12, of which 8 were waited for; matrix products, arithmetic and copies ran while one was open for 11% of the time, Pallas kernels for 0%

profile of v8, /device:TPU:38, one launch (start us, length us, event | category | flops | bytes accessed | tf_op | source)
XLA Modules:
  0.0 235.8 jit_solution(13353329541693361885)
XLA Ops:
  0.7 0.0 copy-start.7
  0.7 0.0 copy-start.21
  0.7 2.8 %dynamic-slice_bitcast_fusion.3 = (bf16[4096,128]{1,0:T(8,128)(2,1)S(1)}, bf16[4096,128]{1,0:T(8,128)(2,1)}) fusion(bf16[1,8192,128]{2,1,0:T(8,128)(2,1)} %param.14, s32[]{:T(128)S(6)} %select_n.43, s32[]{:T(128)S(6)} %select_n.44), kind=kLoop, calls=%fused_computation.43 | loop fusion | bytes 4194312 | tf_op jit(solution)/shard_map/dynamic_slice | solution.py:50
  3.5 1.4 collective-permute-start.1
  4.9 0.3 fusion.4
  5.3 0.5 fusion.1
  5.8 2.2 collective-permute-start
  8.0 0.0 copy-start.16
  8.0 22.2 %collective-permute-done = f32[2,144]{1,0:T(2,128)S(1)} collective-permute-done((f32[2,144]{1,0:T(2,128)S(1)}, f32[2,144]{1,0:T(2,128)S(1)}, u32[]{:S(2)}, u32[]{:S(2)}) %collective-permute-start) | collective-permute-done | bytes 1184 | tf_op jit(solution)/shard_map/ppermute | solution.py:14
  30.3 0.0 copy-start.22
  30.3 2.4 %fusion.28 = f32[1,144,256]{2,1,0:T(8,128)S(1)} fusion(bf16[1,144,4096]{2,1,0:T(8,128)(2,1)S(1)} %copy-done, f32[144]{0:T(256)S(1)} %bitcast.105, f32[4096]{0:T(1024)S(1)} %bitcast.102, bf16[4096,128]{1,0:T(8,128)(2,1)} %collective-permute-done.1, bf16[4096,128]{1,0:T(8,128)(2,1)S(1)} %get-tuple-element.24, pred[]{:T(512)S(6)} %eq.18), kind=kOutput, calls=%fused_computation.38 | convolution fusion | flops 313786368 | bytes 3441217 | tf_op jit(solution)/shard_map/dot_general | solution.py:75
  32.8 0.0 copy-start.11
  32.8 0.0 copy-start.1
  32.8 3.2 %fusion.25 = f32[1,144,256]{2,1,0:T(8,128)S(1)} fusion(f32[4096]{0:T(1024)S(1)} %bitcast.103, f32[144]{0:T(256)S(1)} %bitcast.113, bf16[1,144,4096]{2,1,0:T(8,128)(2,1)S(1)} %copy-done.7, pred[144]{0:T(512)(128)(4,1)} %copy-done.24, bf16[4096]{0:T(1024)(128)(2,1)S(1)} %copy-done.22, bf16[4096,128]{1,0:T(8,128)(2,1)} %collective-permute-done.1, ...), kind=kOutput, calls=%fused_computation.37 | convolution fusion | flops 314376192 | bytes 3449553 | tf_op jit(solution)/shard_map/dot_general | solution.py:74
  36.1 0.8 pad_maximum_fusion.1
  36.8 1.4 collective-permute-start.2
  38.2 0.9 reshape_squeeze.3
  39.2 0.0 copy-start.12
  39.2 0.4 copy.38
  39.6 7.0 %collective-permute-done.2 = f32[2,144,256]{2,1,0:T(8,128)} collective-permute-done((f32[2,144,256]{2,1,0:T(8,128)}, f32[2,144,256]{2,1,0:T(8,128)}, u32[]{:S(2)}, u32[]{:S(2)}) %collective-permute-start.2) | collective-permute-done | bytes 294944 | tf_op jit(solution)/shard_map/ppermute | solution.py:14
  46.6 1.0 fusion.52
  47.6 0.7 copy-done.4
  48.3 0.1 squeeze.27
  48.4 0.1 fusion.43
  48.5 2.8 %convolution_bitcast_fusion = f32[4,2,4,256,128]{3,4,2,1,0:T(8,128)} fusion(bf16[4,4,144,256]{3,2,1,0:T(8,128)(2,1)S(1)} %copy.38, bf16[2,144,128]{2,1,0:T(8,128)(2,1)S(1)} %fusion.43), kind=kOutput, calls=%fused_computation.20 | convolution fusion | flops 301989888 | bytes 5447680 | tf_op jit(solution)/shard_map/dot_general | solution.py:116
  51.3 5.0 %all-to-all-start.1 = ((f32[4,2,4,256,128]{3,4,2,1,0:T(8,128)}), f32[4,2,4,256,128]{3,4,2,1,0:T(8,128)}, u32[]{:S(2)}, u32[]{:S(2)}) async-start(f32[4,2,4,256,128]{3,4,2,1,0:T(8,128)} %convolution_bitcast_fusion), calls=%async_computation.1 | async-start | bytes 8388608 | tf_op jit(solution)/shard_map/all_to_all | solution.py:119
  56.4 1.5 dynamic-slice_bitcast_fusion.1
  57.8 1.4 collective-permute-start.3
  59.2 1.9 reshape.79
  61.2 0.6 convert_reduce_fusion
  61.8 0.7 mul.155
  62.5 20.3 %collective-permute-done.3 = bf16[128,4096]{1,0:T(8,128)(2,1)} collective-permute-done((bf16[128,4096]{1,0:T(8,128)(2,1)}, bf16[128,4096]{1,0:T(8,128)(2,1)}, u32[]{:S(2)}, u32[]{:S(2)}) %collective-permute-start.3) | collective-permute-done | bytes 1048608 | tf_op jit(solution)/shard_map/ppermute | solution.py:14
  82.8 3.5 %fusion.31 = f32[144,256]{1,0:T(8,128)S(1)} fusion(bf16[1,144,4096]{2,1,0:T(8,128)(2,1)} %param.12, bf16[128,4096]{1,0:T(8,128)(2,1)} %collective-permute-done.3, bf16[128,4096]{1,0:T(8,128)(2,1)} %get-tuple-element.26, pred[]{:T(512)S(6)} %eq.18), kind=kOutput, calls=%fused_computation.39 | convolution fusion | flops 311427072 | bytes 3424257 | tf_op jit(solution)/shard_map/dot_general | solution.py:22
  86.4 1.5 collective-permute-start.5
  87.9 0.6 fusion.11
  88.5 0.4 copy.34
  88.9 4.2 %collective-permute-done.5 = f32[144,256]{1,0:T(8,128)S(1)} collective-permute-done((f32[144,256]{1,0:T(8,128)S(1)}, f32[144,256]{1,0:T(8,128)S(1)}, u32[]{:S(2)}, u32[]{:S(2)}) %collective-permute-start.5) | collective-permute-done | bytes 147488 | tf_op jit(solution)/shard_map/ppermute | solution.py:14
  93.1 0.1 fusion.41
  93.3 3.3 %fusion.19 = f32[4,2,4,256,128]{4,3,2,1,0:T(8,128)} fusion(bf16[4,4,144,256]{3,2,1,0:T(8,128)(2,1)S(1)} %copy.34, bf16[2,144,128]{2,1,0:T(8,128)(2,1)S(1)} %copy.35), kind=kOutput, calls=%fused_computation.31 | convolution fusion | flops 301989888 | bytes 5447680 | tf_op jit(solution)/shard_map/dot_general | solution.py:116
  96.6 7.2 %all-to-all-done.1 = f32[4,2,4,256,128]{3,4,2,1,0:T(8,128)} async-done(((f32[4,2,4,256,128]{3,4,2,1,0:T(8,128)}), f32[4,2,4,256,128]{3,4,2,1,0:T(8,128)}, u32[]{:S(2)}, u32[]{:S(2)}) %all-to-all-start.1) | async-done | bytes 4194336 | tf_op jit(solution)/shard_map/all_to_all | solution.py:119
  103.8 5.1 %all-to-all-start = ((f32[4,2,4,256,128]{4,3,2,1,0:T(8,128)}), f32[4,2,4,256,128]{4,3,2,1,0:T(8,128)}, u32[]{:S(2)}, u32[]{:S(2)}) async-start(f32[4,2,4,256,128]{4,3,2,1,0:T(8,128)} %fusion.19), calls=%async_computation | async-start | bytes 8388608 | tf_op jit(solution)/shard_map/all_to_all | solution.py:119
  108.9 2.6 %reduce_sum.58 = f32[2,4,256,128]{2,3,1,0:T(8,128)S(1)} reduce(f32[4,2,4,256,128]{3,4,2,1,0:T(8,128)} %all-to-all-done.1, f32[]{:T(128)} %constant.45.clone.1), dimensions={0}, to_apply=%region_4.5 | reduce | flops 786432 | bytes 5242884 | tf_op jit(solution)/shard_map/reduce_sum | solution.py:119
  111.5 0.3 copy.39
  111.8 43.5 %all-to-all-done = f32[4,2,4,256,128]{4,3,2,1,0:T(8,128)} async-done(((f32[4,2,4,256,128]{4,3,2,1,0:T(8,128)}), f32[4,2,4,256,128]{4,3,2,1,0:T(8,128)}, u32[]{:S(2)}, u32[]{:S(2)}) %all-to-all-start) | async-done | bytes 4194336 | tf_op jit(solution)/shard_map/all_to_all | solution.py:119
  155.3 2.5 %reduce_sum.57 = f32[2,4,256,128]{3,2,1,0:T(8,128)S(1)} reduce(f32[4,2,4,256,128]{4,3,2,1,0:T(8,128)} %all-to-all-done, f32[]{:T(128)} %constant.45.clone.1), dimensions={0}, to_apply=%region_3.4 | reduce | flops 786432 | bytes 5242884 | tf_op jit(solution)/shard_map/reduce_sum | solution.py:119
  157.8 1.5 pad_maximum_fusion
  159.3 8.7 %all-to-all-start.2 = ((f32[8,2,256,128]{3,2,1,0:T(8,128)}), f32[8,2,256,128]{3,2,1,0:T(8,128)S(1)}, u32[]{:S(2)}, u32[]{:S(2)}) async-start(f32[8,2,256,128]{3,2,1,0:T(8,128)} %pad_maximum_fusion), calls=%async_computation.2 | async-start | bytes 4194304 | tf_op jit(solution)/shard_map/all_to_all | solution.py:124
  168.0 0.0 copy-start.8
  168.0 0.0 copy-start.23
  168.1 3.4 %fusion.10 = (f32[144]{0:T(256)S(1)}, f32[144,4096]{1,0:T(8,128)S(1)}) fusion(bf16[1,144,4096]{2,1,0:T(8,128)(2,1)S(1)} %copy-done, f32[4096]{0:T(1024)S(1)} %bitcast.104, bf16[144,256]{1,0:T(8,128)(2,1)S(1)} %fusion.41, bf16[4096,128]{1,0:T(8,128)(2,1)} %collective-permute-done.1, bf16[4096,128]{1,0:T(8,128)(2,1)} %copy-done.9, pred[]{:T(512)S(6)} %eq.18), kind=kOutput, calls=%fused_computation.18 | convolution fusion | flops 313786240 | bytes 5726785 | tf_op jit(solution)/shard_map/dot_general | solution.py:22
  171.5 0.0 copy-start.2
  171.5 1.5 collective-permute-start.6
  173.0 3.6 %fusion = bf16[144,4096]{1,0:T(8,128)(2,1)} fusion(bf16[128,4096]{1,0:T(8,128)(2,1)} %collective-permute-done.3, bf16[128,4096]{1,0:T(8,128)(2,1)S(1)} %copy-done.10, pred[]{:T(512)S(6)} %eq.18, f32[2,144,256]{2,1,0:T(8,128)S(1)} %copy-done.6, bf16[4096]{0:T(1024)(128)(2,1)S(1)} %copy-done.23, bf16[1,144,4096]{2,1,0:T(8,128)(2,1)S(1)} %copy-done.8, ...), kind=kOutput, calls=%fused_computation.2 | convolution fusion | flops 313970688 | bytes 4612609 | tf_op jit(solution)/shard_map/dot_general | solution.py:83
  176.7 1.9 collective-permute-start.4
  178.6 2.0 fusion.9
  180.6 3.6 %collective-permute-start.7 = (bf16[144,4096]{1,0:T(8,128)(2,1)}, bf16[144,4096]{1,0:T(8,128)(2,1)S(1)}, u32[]{:S(2)}, u32[]{:S(2)}) collective-permute-start(bf16[144,4096]{1,0:T(8,128)(2,1)} %fusion.9), channel_id=1, source_target_pairs={{2,0},{4,2},{6,4},{3,1},{5,3},{7,5},{10,8},{12,10},{14,12},{11,9},... | collective-permute-start | bytes 3538952 | tf_op jit(solution)/shard_map/ppermute | solution.py:10
  184.3 30.2 %all-to-all-done.2 = f32[8,2,256,128]{3,2,1,0:T(8,128)S(1)} async-done(((f32[8,2,256,128]{3,2,1,0:T(8,128)}), f32[8,2,256,128]{3,2,1,0:T(8,128)S(1)}, u32[]{:S(2)}, u32[]{:S(2)}) %all-to-all-start.2) | async-done | bytes 2097184 | tf_op jit(solution)/shard_map/all_to_all | solution.py:124
  214.4 0.1 reduce_sum.59
  214.5 4.1 %collective-permute-start.8 = (f32[2,256,128]{2,1,0:T(8,128)S(1)}, f32[2,256,128]{2,1,0:T(8,128)S(1)}, u32[]{:S(2)}, u32[]{:S(2)}) collective-permute-start(f32[2,256,128]{2,1,0:T(8,128)S(1)} %reduce_sum.59), channel_id=1, source_target_pairs={{1,128},{9,136},{17,144},{25,152},{33,160},{41,168},{49,176},{57,1... | collective-permute-start | bytes 786440 | tf_op jit(solution)/shard_map/ppermute | solution.py:134
  218.7 12.3 %collective-permute-done.8 = f32[2,256,128]{2,1,0:T(8,128)S(1)} collective-permute-done((f32[2,256,128]{2,1,0:T(8,128)S(1)}, f32[2,256,128]{2,1,0:T(8,128)S(1)}, u32[]{:S(2)}, u32[]{:S(2)}) %collective-permute-start.8) | collective-permute-done | bytes 262176 | tf_op jit(solution)/shard_map/ppermute | solution.py:134
  231.0 0.7 slice_bitcast_fusion.1
  231.7 0.8 copy.40
  232.4 2.4 %copy.46 = bf16[1,144,4096]{2,1,0:T(8,128)(2,1)} copy(bf16[1,144,4096]{2,1,0:T(8,128)(2,1)} %bitcast.14) | data formatting | bytes 2359296
  234.8 1.0 copy.47
  (58 shorter events, 0.2 us)
Async XLA Ops:
  0.6 4.3 %copy-start = (bf16[1,144,4096]{2,1,0:T(8,128)(2,1)S(1)}, bf16[1,144,4096]{2,1,0:T(8,128)(2,1)}, u32[]{:S(2)}) copy-start(bf16[1,144,4096]{2,1,0:T(8,128)(2,1)} %param.11) | copy-start | bytes 3538948
  0.6 4.6 %copy-start.26 = (s32[144]{0:T(256)S(1)}, s32[144]{0:T(256)}, u32[]{:S(2)}) copy-start(s32[144]{0:T(256)} %param.9) | copy-start | bytes 1732
  0.7 4.6 %copy-start.7 = (bf16[1,144,4096]{2,1,0:T(8,128)(2,1)S(1)}, bf16[1,144,4096]{2,1,0:T(8,128)(2,1)}, u32[]{:S(2)}) copy-start(bf16[1,144,4096]{2,1,0:T(8,128)(2,1)} %param.8) | copy-start | bytes 3538948
  0.7 4.6 %copy-start.21 = (bf16[4096]{0:T(1024)(128)(2,1)S(1)}, bf16[4096]{0:T(1024)(128)(2,1)}, u32[]{:S(2)}) copy-start(bf16[4096]{0:T(1024)(128)(2,1)} %param.10) | copy-start | bytes 24580
  3.5 29.2 %copy-start.9 = (bf16[4096,128]{1,0:T(8,128)(2,1)}, bf16[4096,128]{1,0:T(8,128)(2,1)S(1)}, u32[]{:S(2)}) copy-start(bf16[4096,128]{1,0:T(8,128)(2,1)S(1)} %get-tuple-element.24) | copy-start | bytes 3145732
  3.5 4.5 %copy-start.15 = (bf16[1,4096]{1,0:T(2,128)(2,1)S(1)}, bf16[1,4096]{1,0:T(2,128)(2,1)}, u32[]{:S(2)}) copy-start(bf16[1,4096]{1,0:T(2,128)(2,1)} %param.13) | copy-start | bytes 24580
  3.5 26.8 %collective-permute-start.1 = (bf16[4096,128]{1,0:T(8,128)(2,1)}, bf16[4096,128]{1,0:T(8,128)(2,1)}, u32[]{:S(2)}, u32[]{:S(2)}) collective-permute-start(bf16[4096,128]{1,0:T(8,128)(2,1)} %get-tuple-element.25), channel_id=1, source_target_pairs={{0,1},{1,0},{2,3},{3,2},{4,5},{5,4},{6,7},{7,6},{8,9},{9,8},{10,11... | collective-permute-start | bytes 3145736 | tf_op jit(solution)/shard_map/ppermute | solution.py:14
  5.3 27.5 %copy-start.24 = (pred[144]{0:T(512)(128)(4,1)}, pred[144]{0:T(512)(128)(4,1)S(1)}, u32[]{:S(2)}) copy-start(pred[144]{0:T(512)(128)(4,1)S(1)} %compare_or_fusion) | copy-start | bytes 436
  5.8 24.5 %collective-permute-start = (f32[2,144]{1,0:T(2,128)S(1)}, f32[2,144]{1,0:T(2,128)S(1)}, u32[]{:S(2)}, u32[]{:S(2)}) collective-permute-start(f32[2,144]{1,0:T(2,128)S(1)} %pad_maximum_fusion.2), channel_id=1, source_target_pairs={{0,1},{1,0},{2,3},{3,2},{4,5},{5,4},{6,7},{7,6},{8,9},{9,8},{10,11... | collective-permute-start | bytes 3464 | tf_op jit(solution)/shard_map/ppermute | solution.py:14
  8.0 24.8 %copy-start.16 = (f32[1,4096]{1,0:T(1,128)}, f32[1,4096]{1,0:T(1,128)S(1)}, u32[]{:S(2)}) copy-start(f32[1,4096]{1,0:T(1,128)S(1)} %convert_element_type.50) | copy-start | bytes 49156
  30.3 2.5 %copy-start.18 = (f32[1,144]{1,0:T(1,128)}, f32[1,144]{1,0:T(1,128)S(1)}, u32[]{:S(2)}) copy-start(f32[1,144]{1,0:T(1,128)S(1)} %get-tuple-element.31) | copy-start | bytes 1732
  30.3 2.5 %copy-start.22 = (bf16[4096]{0:T(1024)(128)(2,1)S(1)}, bf16[4096]{0:T(1024)(128)(2,1)}, u32[]{:S(2)}) copy-start(bf16[4096]{0:T(1024)(128)(2,1)} %param.10) | copy-start | bytes 24580
  32.8 3.3 %copy-start.11 = (f32[1,144,256]{2,1,0:T(8,128)}, f32[1,144,256]{2,1,0:T(8,128)S(1)}, u32[]{:S(2)}) copy-start(f32[1,144,256]{2,1,0:T(8,128)S(1)} %fusion.28) | copy-start | bytes 442372
  32.8 5.4 %copy-start.1 = (bf16[1,144,4096]{2,1,0:T(8,128)(2,1)S(1)}, bf16[1,144,4096]{2,1,0:T(8,128)(2,1)}, u32[]{:S(2)}) copy-start(bf16[1,144,4096]{2,1,0:T(8,128)(2,1)} %param.12) | copy-start | bytes 3538948
  36.1 0.8 copy-start.13
  36.8 9.7 %collective-permute-start.2 = (f32[2,144,256]{2,1,0:T(8,128)}, f32[2,144,256]{2,1,0:T(8,128)}, u32[]{:S(2)}, u32[]{:S(2)}) collective-permute-start(f32[2,144,256]{2,1,0:T(8,128)} %pad_maximum_fusion.1), channel_id=1, source_target_pairs={{0,1},{1,0},{2,3},{3,2},{4,5},{5,4},{6,7},{7,6},{8,9},{9,8},{10,11... | collective-permute-start | bytes 884744 | tf_op jit(solution)/shard_map/ppermute | solution.py:14
  39.2 7.4 %copy-start.12 = (f32[1,144,256]{2,1,0:T(8,128)S(1)}, f32[1,144,256]{2,1,0:T(8,128)}, u32[]{:S(2)}) copy-start(f32[1,144,256]{2,1,0:T(8,128)} %copy-done.11) | copy-start | bytes 442372
  39.2 7.4 %copy-start.14 = (f32[1,144,256]{2,1,0:T(8,128)S(1)}, f32[1,144,256]{2,1,0:T(8,128)}, u32[]{:S(2)}) copy-start(f32[1,144,256]{2,1,0:T(8,128)} %copy-done.13) | copy-start | bytes 442372
  47.6 0.7 copy-start.4
  51.3 5.0 %copy-start.3 = (bf16[1,128,8192]{2,1,0:T(8,128)(2,1)S(1)}, bf16[1,128,8192]{2,1,0:T(8,128)(2,1)}, u32[]{:S(2)}) copy-start(bf16[1,128,8192]{2,1,0:T(8,128)(2,1)} %param.15) | copy-start | bytes 6291460
  51.3 52.5 %all-to-all-start.1 = ((f32[4,2,4,256,128]{3,4,2,1,0:T(8,128)}), f32[4,2,4,256,128]{3,4,2,1,0:T(8,128)}, u32[]{:S(2)}, u32[]{:S(2)}) async-start(f32[4,2,4,256,128]{3,4,2,1,0:T(8,128)} %convolution_bitcast_fusion), calls=%async_computation.1 | async-start | bytes 8388608 | tf_op jit(solution)/shard_map/all_to_all | solution.py:119
  57.8 25.0 %collective-permute-start.3 = (bf16[128,4096]{1,0:T(8,128)(2,1)}, bf16[128,4096]{1,0:T(8,128)(2,1)}, u32[]{:S(2)}, u32[]{:S(2)}) collective-permute-start(bf16[128,4096]{1,0:T(8,128)(2,1)} %get-tuple-element.27), channel_id=1, source_target_pairs={{0,1},{1,0},{2,3},{3,2},{4,5},{5,4},{6,7},{7,6},{8,9},{9,8},{10,11... | collective-permute-start | bytes 3145736 | tf_op jit(solution)/shard_map/ppermute | solution.py:14
  82.8 5.0 %copy-start.19 = (f32[1,144]{1,0:T(1,128)S(1)}, f32[1,144]{1,0:T(1,128)}, u32[]{:S(2)}) copy-start(f32[1,144]{1,0:T(1,128)} %copy-done.18) | copy-start | bytes 1732
  86.4 6.7 %copy-start.5 = (f32[2,144,256]{2,1,0:T(8,128)S(1)}, f32[2,144,256]{2,1,0:T(8,128)}, u32[]{:S(2)}) copy-start(f32[2,144,256]{2,1,0:T(8,128)} %copy-done.4) | copy-start | bytes 884740
  86.4 6.7 %collective-permute-start.5 = (f32[144,256]{1,0:T(8,128)S(1)}, f32[144,256]{1,0:T(8,128)S(1)}, u32[]{:S(2)}, u32[]{:S(2)}) collective-permute-start(f32[144,256]{1,0:T(8,128)S(1)} %fusion.31), channel_id=1, source_target_pairs={{0,1},{1,0},{2,3},{3,2},{4,5},{5,4},{6,7},{7,6},{8,9},{9,8},{10,11... | collective-permute-start | bytes 442376 | tf_op jit(solution)/shard_map/ppermute | solution.py:14
  103.8 51.5 %all-to-all-start = ((f32[4,2,4,256,128]{4,3,2,1,0:T(8,128)}), f32[4,2,4,256,128]{4,3,2,1,0:T(8,128)}, u32[]{:S(2)}, u32[]{:S(2)}) async-start(f32[4,2,4,256,128]{4,3,2,1,0:T(8,128)} %fusion.19), calls=%async_computation | async-start | bytes 8388608 | tf_op jit(solution)/shard_map/all_to_all | solution.py:119
  159.3 8.7 %copy-start.20 = (f32[1,144]{1,0:T(1,128)S(1)}, f32[1,144]{1,0:T(1,128)}, u32[]{:S(2)}) copy-start(f32[1,144]{1,0:T(1,128)} %copy-done.18) | copy-start | bytes 1732
  159.3 8.7 %copy-start.17 = (f32[1,4096]{1,0:T(1,128)S(1)}, f32[1,4096]{1,0:T(1,128)}, u32[]{:S(2)}) copy-start(f32[1,4096]{1,0:T(1,128)} %copy-done.16) | copy-start | bytes 49156
  159.3 55.1 %all-to-all-start.2 = ((f32[8,2,256,128]{3,2,1,0:T(8,128)}), f32[8,2,256,128]{3,2,1,0:T(8,128)S(1)}, u32[]{:S(2)}, u32[]{:S(2)}) async-start(f32[8,2,256,128]{3,2,1,0:T(8,128)} %pad_maximum_fusion), calls=%async_computation.2 | async-start | bytes 4194304 | tf_op jit(solution)/shard_map/all_to_all | solution.py:124
  168.0 5.0 %copy-start.6 = (f32[2,144,256]{2,1,0:T(8,128)S(1)}, f32[2,144,256]{2,1,0:T(8,128)}, u32[]{:S(2)}) copy-start(f32[2,144,256]{2,1,0:T(8,128)} %copy-done.4) | copy-start | bytes 884740
  168.0 5.0 %copy-start.8 = (bf16[1,144,4096]{2,1,0:T(8,128)(2,1)S(1)}, bf16[1,144,4096]{2,1,0:T(8,128)(2,1)}, u32[]{:S(2)}) copy-start(bf16[1,144,4096]{2,1,0:T(8,128)(2,1)} %param.8) | copy-start | bytes 3538948
  168.0 5.0 %copy-start.10 = (bf16[128,4096]{1,0:T(8,128)(2,1)S(1)}, bf16[128,4096]{1,0:T(8,128)(2,1)}, u32[]{:S(2)}) copy-start(bf16[128,4096]{1,0:T(8,128)(2,1)} %get-tuple-element.26) | copy-start | bytes 3145732
  168.0 5.0 %copy-start.23 = (bf16[4096]{0:T(1024)(128)(2,1)S(1)}, bf16[4096]{0:T(1024)(128)(2,1)}, u32[]{:S(2)}) copy-start(bf16[4096]{0:T(1024)(128)(2,1)} %param.10) | copy-start | bytes 24580
  168.0 5.0 %copy-start.25 = (pred[144]{0:T(512)(128)(4,1)S(1)}, pred[144]{0:T(512)(128)(4,1)}, u32[]{:S(2)}) copy-start(pred[144]{0:T(512)(128)(4,1)} %copy-done.24) | copy-start | bytes 436
  171.5 7.1 %copy-start.2 = (bf16[1,144,4096]{2,1,0:T(8,128)(2,1)S(1)}, bf16[1,144,4096]{2,1,0:T(8,128)(2,1)}, u32[]{:S(2)}) copy-start(bf16[1,144,4096]{2,1,0:T(8,128)(2,1)} %param.12) | copy-start | bytes 3538948
  171.5 7.1 %collective-permute-start.6 = (f32[144]{0:T(256)S(1)}, f32[144]{0:T(256)S(1)}, u32[]{:S(2)}, u32[]{:S(2)}) collective-permute-start(f32[144]{0:T(256)S(1)} %get-tuple-element.32), channel_id=1, source_target_pairs={{0,1},{1,0},{2,3},{3,2},{4,5},{5,4},{6,7},{7,6},{8,9},{9,8},{10,11... | collective-permute-start | bytes 1736 | tf_op jit(solution)/shard_map/ppermute | solution.py:14
  176.7 42.0 %collective-permute-start.4 = (bf16[144,4096]{1,0:T(8,128)(2,1)}, bf16[144,4096]{1,0:T(8,128)(2,1)}, u32[]{:S(2)}, u32[]{:S(2)}) collective-permute-start(bf16[144,4096]{1,0:T(8,128)(2,1)} %fusion), channel_id=1, source_target_pairs={{0,2},{2,4},{4,6},{1,3},{3,5},{5,7},{8,10},{10,12},{12,14},{9,11},... | collective-permute-start | bytes 3538952 | tf_op jit(solution)/shard_map/ppermute | solution.py:10
  180.6 38.1 %collective-permute-start.7 = (bf16[144,4096]{1,0:T(8,128)(2,1)}, bf16[144,4096]{1,0:T(8,128)(2,1)S(1)}, u32[]{:S(2)}, u32[]{:S(2)}) collective-permute-start(bf16[144,4096]{1,0:T(8,128)(2,1)} %fusion.9), channel_id=1, source_target_pairs={{2,0},{4,2},{6,4},{3,1},{5,3},{7,5},{10,8},{12,10},{14,12},{11,9},... | collective-permute-start | bytes 3538952 | tf_op jit(solution)/shard_map/ppermute | solution.py:10
  214.5 16.4 %collective-permute-start.8 = (f32[2,256,128]{2,1,0:T(8,128)S(1)}, f32[2,256,128]{2,1,0:T(8,128)S(1)}, u32[]{:S(2)}, u32[]{:S(2)}) collective-permute-start(f32[2,256,128]{2,1,0:T(8,128)S(1)} %reduce_sum.59), channel_id=1, source_target_pairs={{1,128},{9,136},{17,144},{25,152},{33,160},{41,168},{49,176},{57,1... | collective-permute-start | bytes 786440 | tf_op jit(solution)/shard_map/ppermute | solution.py:134
